TPU v7x, 128 devices: a whole 4x4x4 slice. The times are simulated.
128 devices in a mesh: tm: 32 (over x, z, core), chan: 4 (over y).
Axes of the slice: x: 4, y: 4, z: 4, core: 2. Of those that a mesh axis runs over, the one named last changes fastest.
Arguments:
- inputs: bfloat16 [64, 256, 512], P('tm'), may hold values from -6 to 6
- decay: float32 [64, 512], P('tm', 'chan'), may hold values from 0 to 1, as said below
- kernel_b: bfloat16 [9, 512, 256], P(None, 'chan'), may hold values from -0.125 to 0.125
- kernel_c: bfloat16 [9, 256, 512], P(None, 'chan'), may hold values from -0.09375 to 0.09375
- cotangent: bfloat16 [64, 256, 512], P('tm', 'chan'), may hold values from -0.03125 to 0.03125
Outputs:
- grad_b: float32 [9, 512, 256], P(None, 'chan')
- grad_c: float32 [9, 256, 512], P(None, 'chan')
- decay_grad: float32 [64, 512], P('tm', 'chan')
Inputs may be any that keep to these rules, and one draw needn't show every extreme that they name: decay lies strictly between 0 and 1.
All inputs are finite; a program needn't handle non-finite values.
Results may differ from a plain program's by a relative error of at most 0.003.
Values may be sent and summed in bfloat16 or wider, within the bound.
No kernel may reach another device: no remote copies, remote signals or barrier semaphores. Data moves between devices by JAX's collectives and lax.ppermute only.
A program may use at most 128 MiB of HBM per device.

v0:
```python
import jax
import jax.numpy as jnp
from jax import lax
from jax.sharding import PartitionSpec as P

W = 64


offsets = ((-1, -1), (-1, 0), (-1, 1), (0, -1), (0, 0), (0, 1), (1, -1), (1, 0), (1, 1))


def passed_along(value, axis, steps):
    count = lax.axis_size(axis)
    first, last = (max(0, -steps), min(count, count - steps))
    return lax.ppermute(value, axis, [(source, source + steps) for source in range(first, last)])


def shift_cells(source, row_shift, col_shift, grid_width):
    cell_count = source.shape[-1]
    margin = grid_width + 1
    padded = jnp.pad(source, [(0, 0)] * (source.ndim - 1) + [(margin, margin)])
    first_cell = margin + row_shift * grid_width + col_shift
    shifted = lax.slice_in_dim(padded, first_cell, first_cell + cell_count, axis=source.ndim - 1)
    column = jnp.arange(cell_count) % grid_width
    inside = (column + col_shift >= 0) & (column + col_shift < grid_width)
    return jnp.where(inside, shifted, jnp.zeros((), source.dtype))


def stencil_stack(source, grid_width, decay_factor):
    parts = [
        shift_cells(source, decay_factor * pair[0], decay_factor * pair[1], grid_width)
        for pair in offsets
    ]
    return jnp.stack(parts, axis=source.ndim - 2)


def body(inputs, decay, kernel_b, kernel_c, cotangent):
    local_rows = kernel_b.shape[1]
    cell_count = inputs.shape[-1]
    blank_state = jnp.zeros((local_rows, cell_count), jnp.float32)
    input_stack = stencil_stack(inputs, W, 1)
    drives = jnp.einsum("kpc,fkcs->fps", kernel_b, input_stack, preferred_element_type=jnp.float32)

    def advance(current, frame_pair):
        frame_rate, drive = frame_pair
        current = frame_rate[:, None] * current + drive
        return (current, current)

    local_end, local_states = lax.scan(advance, blank_state, (decay, drives))
    decay_total = jnp.prod(decay, axis=0)

    def relay_state(turn_index, carried):
        outgoing = decay_total[:, None] * carried + local_end
        return passed_along(outgoing, "tm", 1)

    entering = lax.fori_loop(0, lax.axis_size("tm") - 1, relay_state, blank_state)
    cumulative = jnp.cumprod(decay, axis=0)
    states = local_states + cumulative[:, :, None] * entering[None]
    previous = jnp.concatenate([entering[None], states[:-1]], axis=0)
    states_bf = states.astype(jnp.bfloat16)
    cot_stack = stencil_stack(cotangent, W, -1)
    injected = lax.psum_scatter(
        jnp.einsum("kup,fkus->pfs", kernel_c, cot_stack, preferred_element_type=jnp.float32),
        "chan",
        scatter_dimension=0,
        tiled=True,
    )
    injected = jnp.moveaxis(injected, 1, 0)

    def retreat(carried, frame_pair):
        frame_rate, source = frame_pair
        adjoint = source + carried
        return (frame_rate[:, None] * adjoint, adjoint)

    message, local_adjoint = lax.scan(retreat, blank_state, (decay, injected), reverse=True)

    def relay_adjoint(turn_index, carried):
        outgoing = decay_total[:, None] * carried + message
        return passed_along(outgoing, "tm", -1)

    arriving = lax.fori_loop(0, lax.axis_size("tm") - 1, relay_adjoint, blank_state)
    suffix = jnp.flip(jnp.cumprod(jnp.flip(decay, 0), 0), 0)
    later_decay = jnp.concatenate([suffix[1:], jnp.ones_like(decay[:1])], axis=0)
    adjoint = local_adjoint + later_decay[:, :, None] * arriving[None]
    decay_grad = jnp.sum(adjoint * previous, axis=2)
    adjoint_bf = adjoint.astype(jnp.bfloat16)
    grad_b_part = jnp.einsum(
        "fps,fkcs->kpc", adjoint_bf, input_stack, preferred_element_type=jnp.float32
    )
    shifted = stencil_stack(lax.all_gather(states_bf, "chan", axis=1, tiled=True), W, 1)
    grad_c_part = jnp.einsum(
        "fus,fkps->kup", cotangent, shifted, preferred_element_type=jnp.float32
    )
    grad_b, grad_c = lax.psum((grad_b_part, grad_c_part), "tm")
    return (grad_b, grad_c, decay_grad)


def solution(mesh):
    in_specs = (
        P("tm", None, None),
        P("tm", "chan"),
        P(None, "chan", None),
        P(None, "chan", None),
        P("tm", "chan", None),
    )
    out_specs = (P(None, "chan", None), P(None, "chan", None), P("tm", "chan"))
    return jax.shard_map(body, mesh=mesh, in_specs=in_specs, out_specs=out_specs, check_vma=False)
```

profile of v0, /device:TPU:1, one launch (start us, length us, event | category | flops | bytes accessed | tf_op | source)
XLA Modules:
  0.0 817.5 jit_solution(8985757919530302460)
XLA Ops:
  20.7 275.2 %while.51 = (s32[]{:T(128)}, f32[128,512]{1,0:T(8,128)S(1)}, f32[128]{0:T(128)S(1)}, f32[128,512]{1,0:T(8,128)S(1)}, s32[]{:T(128)}) while((s32[]{:T(128)}, f32[128,512]{1,0:T(8,128)S(1)}, f32[128]{0:T(128)S(1)}, f32[128,512]{1,0:T(8,128)S(1)}, s32[]{:T(128)}) %tuple.101), condition=%wide.region_12.13_spmd, body=%wide.region_11.12_spmd.sunk | while | flops 131074 | bytes 1835621 | solution.py:56
  138.1 6.0 collective-permute-start.1
  147.5 6.5 collective-permute-start.1
  157.4 6.5 collective-permute-start.1
  167.3 6.5 collective-permute-start.1
  177.2 6.5 collective-permute-start.1
  187.1 6.5 collective-permute-start.1
  197.0 6.5 collective-permute-start.1
  206.9 6.5 collective-permute-start.1
  216.8 6.5 collective-permute-start.1
  226.7 6.5 collective-permute-start.1
  236.6 6.5 collective-permute-start.1
  246.5 6.5 collective-permute-start.1
  256.4 6.5 collective-permute-start.1
  266.3 6.5 collective-permute-start.1
  276.2 6.5 collective-permute-start.1
  286.1 6.5 collective-permute-start.1
  300.5 49.7 %all-gather.2.cloned.1.call-done = bf16[2,512,512]{2,1,0:T(8,128)(2,1)} async-done(((bf16[2,128,512]{2,1,0:T(8,128)(2,1)}), bf16[2,512,512]{2,1,0:T(8,128)(2,1)}) %all-gather.2.cloned.1.call-update) | async-done | bytes 1048592 | tf_op jit(solution)/shard_map/all_gather | solution.py:90
  361.1 23.6 %reduce-scatter.2.cloned.1.call-done = f32[128,2,512]{0,2,1:T(8,128)} async-done(((f32[512,2,512]{0,2,1:T(8,128)}), f32[128,2,512]{0,2,1:T(8,128)}) %reduce-scatter.2.cloned.1.call-update) | async-done | bytes 524304 | tf_op jit(solution)/shard_map/reduce_scatter | solution.py:62
  387.4 279.4 %while.50 = (s32[]{:T(128)}, f32[128,512]{1,0:T(8,128)S(1)}, f32[128]{0:T(128)S(1)}, f32[128,512]{1,0:T(8,128)S(1)}, s32[]{:T(128)}) while((s32[]{:T(128)}, f32[128,512]{1,0:T(8,128)S(1)}, f32[128]{0:T(128)S(1)}, f32[128,512]{1,0:T(8,128)S(1)}, s32[]{:T(128)}) %tuple.113), condition=%wide.region_6.7_spmd, body=%wide.region_5.6_spmd.sunk | while | flops 131074 | bytes 1835621 | solution.py:81
  397.4 5.8 collective-permute-done
  405.2 5.8 collective-permute-done
  413.0 5.8 collective-permute-done
  420.8 5.8 collective-permute-done
  428.5 5.8 collective-permute-done
  436.3 5.8 collective-permute-done
  444.1 5.8 collective-permute-done
  451.9 5.8 collective-permute-done
  483.0 5.8 collective-permute-done
  490.8 7.7 collective-permute-done
  500.6 7.9 collective-permute-done
  510.5 7.9 collective-permute-done
  520.4 7.9 collective-permute-done
  530.3 7.9 collective-permute-done
  540.2 7.9 collective-permute-done
  550.0 7.9 collective-permute-done
  559.9 7.9 collective-permute-done
  569.8 7.9 collective-permute-done
  579.7 7.9 collective-permute-done
  589.6 7.9 collective-permute-done
  599.5 7.9 collective-permute-done
  609.4 7.9 collective-permute-done
  619.3 7.9 collective-permute-done
  629.2 7.9 collective-permute-done
  639.1 7.9 collective-permute-done
  649.0 7.9 collective-permute-done
  658.9 7.9 collective-permute-done
  672.4 133.6 %all-reduce.6.cloned.1.call-done = (f32[9,128,256]{1,2,0:T(8,128)}, f32[9,64,512]{2,1,0:T(8,128)}) async-done(((f32[9,128,256]{1,2,0:T(8,128)}, f32[9,64,512]{2,1,0:T(8,128)}), (f32[9,128,256]{1,2,0:T(8,128)}, f32[9,64,512]{2,1,0:T(8,128)})) %all-reduce.6.cloned.1.call-update) | async-done | bytes 2359312 | tf_op jit(solution)/shard_map/psum | solution.py:94
  (235 shorter events, 301.6 us)
Async XLA Ops:
  7.2 343.0 %all-gather.2.cloned.1.call-start = ((), (), s32[]{:S(2)}) async-start(), calls=%async_computation.2 | async-start | bytes 1310720 | tf_op jit(solution)/shard_map/all_gather | solution.py:90
  20.8 8.2 %collective-permute-start.1 = (f32[128,512]{1,0:T(8,128)S(1)}, f32[128,512]{1,0:T(8,128)S(1)}, u32[]{:S(2)}, u32[]{:S(2)}) collective-permute-start(f32[128,512]{1,0:T(8,128)S(1)} %multiply_add_fusion.8), channel_id=1, source_target_pairs={{0,4},{4,8},{8,12},{12,16},{16,20},{20,24},{24,28},{28,32},{32,36}... | collective-permute-start | bytes 786440 | tf_op jit(solution)/shard_map/while/body/eval_jaxpr/ppermute | solution.py:15
  29.1 7.7 collective-permute-start.1
  36.9 7.7 collective-permute-start.1
  44.7 7.7 collective-permute-start.1
  60.2 7.7 collective-permute-start.1
  68.0 7.7 collective-permute-start.1
  75.8 7.7 collective-permute-start.1
  83.6 7.7 collective-permute-start.1
  91.4 7.7 collective-permute-start.1
  99.2 7.7 collective-permute-start.1
  138.1 9.3 %collective-permute-start.1 = (f32[128,512]{1,0:T(8,128)S(1)}, f32[128,512]{1,0:T(8,128)S(1)}, u32[]{:S(2)}, u32[]{:S(2)}) collective-permute-start(f32[128,512]{1,0:T(8,128)S(1)} %multiply_add_fusion.8), channel_id=1, source_target_pairs={{0,4},{4,8},{8,12},{12,16},{16,20},{20,24},{24,28},{28,32},{32,36}... | collective-permute-start | bytes 786440 | tf_op jit(solution)/shard_map/while/body/eval_jaxpr/ppermute | solution.py:15
  147.5 9.8 %collective-permute-start.1 = (f32[128,512]{1,0:T(8,128)S(1)}, f32[128,512]{1,0:T(8,128)S(1)}, u32[]{:S(2)}, u32[]{:S(2)}) collective-permute-start(f32[128,512]{1,0:T(8,128)S(1)} %multiply_add_fusion.8), channel_id=1, source_target_pairs={{0,4},{4,8},{8,12},{12,16},{16,20},{20,24},{24,28},{28,32},{32,36}... | collective-permute-start | bytes 786440 | tf_op jit(solution)/shard_map/while/body/eval_jaxpr/ppermute | solution.py:15
  157.4 9.8 %collective-permute-start.1 = (f32[128,512]{1,0:T(8,128)S(1)}, f32[128,512]{1,0:T(8,128)S(1)}, u32[]{:S(2)}, u32[]{:S(2)}) collective-permute-start(f32[128,512]{1,0:T(8,128)S(1)} %multiply_add_fusion.8), channel_id=1, source_target_pairs={{0,4},{4,8},{8,12},{12,16},{16,20},{20,24},{24,28},{28,32},{32,36}... | collective-permute-start | bytes 786440 | tf_op jit(solution)/shard_map/while/body/eval_jaxpr/ppermute | solution.py:15
  167.3 9.8 %collective-permute-start.1 = (f32[128,512]{1,0:T(8,128)S(1)}, f32[128,512]{1,0:T(8,128)S(1)}, u32[]{:S(2)}, u32[]{:S(2)}) collective-permute-start(f32[128,512]{1,0:T(8,128)S(1)} %multiply_add_fusion.8), channel_id=1, source_target_pairs={{0,4},{4,8},{8,12},{12,16},{16,20},{20,24},{24,28},{28,32},{32,36}... | collective-permute-start | bytes 786440 | tf_op jit(solution)/shard_map/while/body/eval_jaxpr/ppermute | solution.py:15
  177.2 9.8 %collective-permute-start.1 = (f32[128,512]{1,0:T(8,128)S(1)}, f32[128,512]{1,0:T(8,128)S(1)}, u32[]{:S(2)}, u32[]{:S(2)}) collective-permute-start(f32[128,512]{1,0:T(8,128)S(1)} %multiply_add_fusion.8), channel_id=1, source_target_pairs={{0,4},{4,8},{8,12},{12,16},{16,20},{20,24},{24,28},{28,32},{32,36}... | collective-permute-start | bytes 786440 | tf_op jit(solution)/shard_map/while/body/eval_jaxpr/ppermute | solution.py:15
  187.1 9.8 %collective-permute-start.1 = (f32[128,512]{1,0:T(8,128)S(1)}, f32[128,512]{1,0:T(8,128)S(1)}, u32[]{:S(2)}, u32[]{:S(2)}) collective-permute-start(f32[128,512]{1,0:T(8,128)S(1)} %multiply_add_fusion.8), channel_id=1, source_target_pairs={{0,4},{4,8},{8,12},{12,16},{16,20},{20,24},{24,28},{28,32},{32,36}... | collective-permute-start | bytes 786440 | tf_op jit(solution)/shard_map/while/body/eval_jaxpr/ppermute | solution.py:15
  197.0 9.8 %collective-permute-start.1 = (f32[128,512]{1,0:T(8,128)S(1)}, f32[128,512]{1,0:T(8,128)S(1)}, u32[]{:S(2)}, u32[]{:S(2)}) collective-permute-start(f32[128,512]{1,0:T(8,128)S(1)} %multiply_add_fusion.8), channel_id=1, source_target_pairs={{0,4},{4,8},{8,12},{12,16},{16,20},{20,24},{24,28},{28,32},{32,36}... | collective-permute-start | bytes 786440 | tf_op jit(solution)/shard_map/while/body/eval_jaxpr/ppermute | solution.py:15
  206.9 9.8 %collective-permute-start.1 = (f32[128,512]{1,0:T(8,128)S(1)}, f32[128,512]{1,0:T(8,128)S(1)}, u32[]{:S(2)}, u32[]{:S(2)}) collective-permute-start(f32[128,512]{1,0:T(8,128)S(1)} %multiply_add_fusion.8), channel_id=1, source_target_pairs={{0,4},{4,8},{8,12},{12,16},{16,20},{20,24},{24,28},{28,32},{32,36}... | collective-permute-start | bytes 786440 | tf_op jit(solution)/shard_map/while/body/eval_jaxpr/ppermute | solution.py:15
  216.8 9.8 %collective-permute-start.1 = (f32[128,512]{1,0:T(8,128)S(1)}, f32[128,512]{1,0:T(8,128)S(1)}, u32[]{:S(2)}, u32[]{:S(2)}) collective-permute-start(f32[128,512]{1,0:T(8,128)S(1)} %multiply_add_fusion.8), channel_id=1, source_target_pairs={{0,4},{4,8},{8,12},{12,16},{16,20},{20,24},{24,28},{28,32},{32,36}... | collective-permute-start | bytes 786440 | tf_op jit(solution)/shard_map/while/body/eval_jaxpr/ppermute | solution.py:15
  226.7 9.8 %collective-permute-start.1 = (f32[128,512]{1,0:T(8,128)S(1)}, f32[128,512]{1,0:T(8,128)S(1)}, u32[]{:S(2)}, u32[]{:S(2)}) collective-permute-start(f32[128,512]{1,0:T(8,128)S(1)} %multiply_add_fusion.8), channel_id=1, source_target_pairs={{0,4},{4,8},{8,12},{12,16},{16,20},{20,24},{24,28},{28,32},{32,36}... | collective-permute-start | bytes 786440 | tf_op jit(solution)/shard_map/while/body/eval_jaxpr/ppermute | solution.py:15
  236.6 9.8 %collective-permute-start.1 = (f32[128,512]{1,0:T(8,128)S(1)}, f32[128,512]{1,0:T(8,128)S(1)}, u32[]{:S(2)}, u32[]{:S(2)}) collective-permute-start(f32[128,512]{1,0:T(8,128)S(1)} %multiply_add_fusion.8), channel_id=1, source_target_pairs={{0,4},{4,8},{8,12},{12,16},{16,20},{20,24},{24,28},{28,32},{32,36}... | collective-permute-start | bytes 786440 | tf_op jit(solution)/shard_map/while/body/eval_jaxpr/ppermute | solution.py:15
  246.5 9.8 %collective-permute-start.1 = (f32[128,512]{1,0:T(8,128)S(1)}, f32[128,512]{1,0:T(8,128)S(1)}, u32[]{:S(2)}, u32[]{:S(2)}) collective-permute-start(f32[128,512]{1,0:T(8,128)S(1)} %multiply_add_fusion.8), channel_id=1, source_target_pairs={{0,4},{4,8},{8,12},{12,16},{16,20},{20,24},{24,28},{28,32},{32,36}... | collective-permute-start | bytes 786440 | tf_op jit(solution)/shard_map/while/body/eval_jaxpr/ppermute | solution.py:15
  256.4 9.8 %collective-permute-start.1 = (f32[128,512]{1,0:T(8,128)S(1)}, f32[128,512]{1,0:T(8,128)S(1)}, u32[]{:S(2)}, u32[]{:S(2)}) collective-permute-start(f32[128,512]{1,0:T(8,128)S(1)} %multiply_add_fusion.8), channel_id=1, source_target_pairs={{0,4},{4,8},{8,12},{12,16},{16,20},{20,24},{24,28},{28,32},{32,36}... | collective-permute-start | bytes 786440 | tf_op jit(solution)/shard_map/while/body/eval_jaxpr/ppermute | solution.py:15
  266.3 9.8 %collective-permute-start.1 = (f32[128,512]{1,0:T(8,128)S(1)}, f32[128,512]{1,0:T(8,128)S(1)}, u32[]{:S(2)}, u32[]{:S(2)}) collective-permute-start(f32[128,512]{1,0:T(8,128)S(1)} %multiply_add_fusion.8), channel_id=1, source_target_pairs={{0,4},{4,8},{8,12},{12,16},{16,20},{20,24},{24,28},{28,32},{32,36}... | collective-permute-start | bytes 786440 | tf_op jit(solution)/shard_map/while/body/eval_jaxpr/ppermute | solution.py:15
  276.2 9.8 %collective-permute-start.1 = (f32[128,512]{1,0:T(8,128)S(1)}, f32[128,512]{1,0:T(8,128)S(1)}, u32[]{:S(2)}, u32[]{:S(2)}) collective-permute-start(f32[128,512]{1,0:T(8,128)S(1)} %multiply_add_fusion.8), channel_id=1, source_target_pairs={{0,4},{4,8},{8,12},{12,16},{16,20},{20,24},{24,28},{28,32},{32,36}... | collective-permute-start | bytes 786440 | tf_op jit(solution)/shard_map/while/body/eval_jaxpr/ppermute | solution.py:15
  286.1 9.8 %collective-permute-start.1 = (f32[128,512]{1,0:T(8,128)S(1)}, f32[128,512]{1,0:T(8,128)S(1)}, u32[]{:S(2)}, u32[]{:S(2)}) collective-permute-start(f32[128,512]{1,0:T(8,128)S(1)} %multiply_add_fusion.8), channel_id=1, source_target_pairs={{0,4},{4,8},{8,12},{12,16},{16,20},{20,24},{24,28},{28,32},{32,36}... | collective-permute-start | bytes 786440 | tf_op jit(solution)/shard_map/while/body/eval_jaxpr/ppermute | solution.py:15
  296.7 88.0 %reduce-scatter.2.cloned.1.call-start = ((), (), s32[]{:S(2)}) async-start(), calls=%async_computation.1 | async-start | bytes 2621440 | tf_op jit(solution)/shard_map/reduce_scatter | solution.py:62
  300.2 505.8 %all-reduce.6.cloned.1.call-start = ((), (), s32[]{:S(2)}) async-start(), calls=%async_computation.3 | async-start | bytes 4718592 | tf_op jit(solution)/shard_map/psum | solution.py:94
  387.5 7.9 collective-permute-start
  488.9 9.6 %collective-permute-start = (f32[128,512]{1,0:T(8,128)S(1)}, f32[128,512]{1,0:T(8,128)S(1)}, u32[]{:S(2)}, u32[]{:S(2)}) collective-permute-start(f32[128,512]{1,0:T(8,128)S(1)} %multiply_add_fusion.7), channel_id=1, source_target_pairs={{4,0},{8,4},{12,8},{16,12},{20,16},{24,20},{28,24},{32,28},{36,32}... | collective-permute-start | bytes 786440 | tf_op jit(solution)/shard_map/while/body/eval_jaxpr/ppermute | solution.py:15
  498.6 9.8 %collective-permute-start = (f32[128,512]{1,0:T(8,128)S(1)}, f32[128,512]{1,0:T(8,128)S(1)}, u32[]{:S(2)}, u32[]{:S(2)}) collective-permute-start(f32[128,512]{1,0:T(8,128)S(1)} %multiply_add_fusion.7), channel_id=1, source_target_pairs={{4,0},{8,4},{12,8},{16,12},{20,16},{24,20},{28,24},{32,28},{36,32}... | collective-permute-start | bytes 786440 | tf_op jit(solution)/shard_map/while/body/eval_jaxpr/ppermute | solution.py:15
  508.5 9.8 %collective-permute-start = (f32[128,512]{1,0:T(8,128)S(1)}, f32[128,512]{1,0:T(8,128)S(1)}, u32[]{:S(2)}, u32[]{:S(2)}) collective-permute-start(f32[128,512]{1,0:T(8,128)S(1)} %multiply_add_fusion.7), channel_id=1, source_target_pairs={{4,0},{8,4},{12,8},{16,12},{20,16},{24,20},{28,24},{32,28},{36,32}... | collective-permute-start | bytes 786440 | tf_op jit(solution)/shard_map/while/body/eval_jaxpr/ppermute | solution.py:15
  518.4 9.8 %collective-permute-start = (f32[128,512]{1,0:T(8,128)S(1)}, f32[128,512]{1,0:T(8,128)S(1)}, u32[]{:S(2)}, u32[]{:S(2)}) collective-permute-start(f32[128,512]{1,0:T(8,128)S(1)} %multiply_add_fusion.7), channel_id=1, source_target_pairs={{4,0},{8,4},{12,8},{16,12},{20,16},{24,20},{28,24},{32,28},{36,32}... | collective-permute-start | bytes 786440 | tf_op jit(solution)/shard_map/while/body/eval_jaxpr/ppermute | solution.py:15
  528.3 9.8 %collective-permute-start = (f32[128,512]{1,0:T(8,128)S(1)}, f32[128,512]{1,0:T(8,128)S(1)}, u32[]{:S(2)}, u32[]{:S(2)}) collective-permute-start(f32[128,512]{1,0:T(8,128)S(1)} %multiply_add_fusion.7), channel_id=1, source_target_pairs={{4,0},{8,4},{12,8},{16,12},{20,16},{24,20},{28,24},{32,28},{36,32}... | collective-permute-start | bytes 786440 | tf_op jit(solution)/shard_map/while/body/eval_jaxpr/ppermute | solution.py:15
  538.2 9.8 %collective-permute-start = (f32[128,512]{1,0:T(8,128)S(1)}, f32[128,512]{1,0:T(8,128)S(1)}, u32[]{:S(2)}, u32[]{:S(2)}) collective-permute-start(f32[128,512]{1,0:T(8,128)S(1)} %multiply_add_fusion.7), channel_id=1, source_target_pairs={{4,0},{8,4},{12,8},{16,12},{20,16},{24,20},{28,24},{32,28},{36,32}... | collective-permute-start | bytes 786440 | tf_op jit(solution)/shard_map/while/body/eval_jaxpr/ppermute | solution.py:15
  548.1 9.8 %collective-permute-start = (f32[128,512]{1,0:T(8,128)S(1)}, f32[128,512]{1,0:T(8,128)S(1)}, u32[]{:S(2)}, u32[]{:S(2)}) collective-permute-start(f32[128,512]{1,0:T(8,128)S(1)} %multiply_add_fusion.7), channel_id=1, source_target_pairs={{4,0},{8,4},{12,8},{16,12},{20,16},{24,20},{28,24},{32,28},{36,32}... | collective-permute-start | bytes 786440 | tf_op jit(solution)/shard_map/while/body/eval_jaxpr/ppermute | solution.py:15
  558.0 9.8 %collective-permute-start = (f32[128,512]{1,0:T(8,128)S(1)}, f32[128,512]{1,0:T(8,128)S(1)}, u32[]{:S(2)}, u32[]{:S(2)}) collective-permute-start(f32[128,512]{1,0:T(8,128)S(1)} %multiply_add_fusion.7), channel_id=1, source_target_pairs={{4,0},{8,4},{12,8},{16,12},{20,16},{24,20},{28,24},{32,28},{36,32}... | collective-permute-start | bytes 786440 | tf_op jit(solution)/shard_map/while/body/eval_jaxpr/ppermute | solution.py:15
  567.9 9.8 %collective-permute-start = (f32[128,512]{1,0:T(8,128)S(1)}, f32[128,512]{1,0:T(8,128)S(1)}, u32[]{:S(2)}, u32[]{:S(2)}) collective-permute-start(f32[128,512]{1,0:T(8,128)S(1)} %multiply_add_fusion.7), channel_id=1, source_target_pairs={{4,0},{8,4},{12,8},{16,12},{20,16},{24,20},{28,24},{32,28},{36,32}... | collective-permute-start | bytes 786440 | tf_op jit(solution)/shard_map/while/body/eval_jaxpr/ppermute | solution.py:15
  577.8 9.8 %collective-permute-start = (f32[128,512]{1,0:T(8,128)S(1)}, f32[128,512]{1,0:T(8,128)S(1)}, u32[]{:S(2)}, u32[]{:S(2)}) collective-permute-start(f32[128,512]{1,0:T(8,128)S(1)} %multiply_add_fusion.7), channel_id=1, source_target_pairs={{4,0},{8,4},{12,8},{16,12},{20,16},{24,20},{28,24},{32,28},{36,32}... | collective-permute-start | bytes 786440 | tf_op jit(solution)/shard_map/while/body/eval_jaxpr/ppermute | solution.py:15
  587.7 9.8 %collective-permute-start = (f32[128,512]{1,0:T(8,128)S(1)}, f32[128,512]{1,0:T(8,128)S(1)}, u32[]{:S(2)}, u32[]{:S(2)}) collective-permute-start(f32[128,512]{1,0:T(8,128)S(1)} %multiply_add_fusion.7), channel_id=1, source_target_pairs={{4,0},{8,4},{12,8},{16,12},{20,16},{24,20},{28,24},{32,28},{36,32}... | collective-permute-start | bytes 786440 | tf_op jit(solution)/shard_map/while/body/eval_jaxpr/ppermute | solution.py:15
  597.6 9.8 %collective-permute-start = (f32[128,512]{1,0:T(8,128)S(1)}, f32[128,512]{1,0:T(8,128)S(1)}, u32[]{:S(2)}, u32[]{:S(2)}) collective-permute-start(f32[128,512]{1,0:T(8,128)S(1)} %multiply_add_fusion.7), channel_id=1, source_target_pairs={{4,0},{8,4},{12,8},{16,12},{20,16},{24,20},{28,24},{32,28},{36,32}... | collective-permute-start | bytes 786440 | tf_op jit(solution)/shard_map/while/body/eval_jaxpr/ppermute | solution.py:15
  607.5 9.8 %collective-permute-start = (f32[128,512]{1,0:T(8,128)S(1)}, f32[128,512]{1,0:T(8,128)S(1)}, u32[]{:S(2)}, u32[]{:S(2)}) collective-permute-start(f32[128,512]{1,0:T(8,128)S(1)} %multiply_add_fusion.7), channel_id=1, source_target_pairs={{4,0},{8,4},{12,8},{16,12},{20,16},{24,20},{28,24},{32,28},{36,32}... | collective-permute-start | bytes 786440 | tf_op jit(solution)/shard_map/while/body/eval_jaxpr/ppermute | solution.py:15
  617.4 9.8 %collective-permute-start = (f32[128,512]{1,0:T(8,128)S(1)}, f32[128,512]{1,0:T(8,128)S(1)}, u32[]{:S(2)}, u32[]{:S(2)}) collective-permute-start(f32[128,512]{1,0:T(8,128)S(1)} %multiply_add_fusion.7), channel_id=1, source_target_pairs={{4,0},{8,4},{12,8},{16,12},{20,16},{24,20},{28,24},{32,28},{36,32}... | collective-permute-start | bytes 786440 | tf_op jit(solution)/shard_map/while/body/eval_jaxpr/ppermute | solution.py:15
  627.3 9.8 %collective-permute-start = (f32[128,512]{1,0:T(8,128)S(1)}, f32[128,512]{1,0:T(8,128)S(1)}, u32[]{:S(2)}, u32[]{:S(2)}) collective-permute-start(f32[128,512]{1,0:T(8,128)S(1)} %multiply_add_fusion.7), channel_id=1, source_target_pairs={{4,0},{8,4},{12,8},{16,12},{20,16},{24,20},{28,24},{32,28},{36,32}... | collective-permute-start | bytes 786440 | tf_op jit(solution)/shard_map/while/body/eval_jaxpr/ppermute | solution.py:15
  637.2 9.8 %collective-permute-start = (f32[128,512]{1,0:T(8,128)S(1)}, f32[128,512]{1,0:T(8,128)S(1)}, u32[]{:S(2)}, u32[]{:S(2)}) collective-permute-start(f32[128,512]{1,0:T(8,128)S(1)} %multiply_add_fusion.7), channel_id=1, source_target_pairs={{4,0},{8,4},{12,8},{16,12},{20,16},{24,20},{28,24},{32,28},{36,32}... | collective-permute-start | bytes 786440 | tf_op jit(solution)/shard_map/while/body/eval_jaxpr/ppermute | solution.py:15
  647.1 9.8 %collective-permute-start = (f32[128,512]{1,0:T(8,128)S(1)}, f32[128,512]{1,0:T(8,128)S(1)}, u32[]{:S(2)}, u32[]{:S(2)}) collective-permute-start(f32[128,512]{1,0:T(8,128)S(1)} %multiply_add_fusion.7), channel_id=1, source_target_pairs={{4,0},{8,4},{12,8},{16,12},{20,16},{24,20},{28,24},{32,28},{36,32}... | collective-permute-start | bytes 786440 | tf_op jit(solution)/shard_map/while/body/eval_jaxpr/ppermute | solution.py:15
  657.0 9.8 %collective-permute-start = (f32[128,512]{1,0:T(8,128)S(1)}, f32[128,512]{1,0:T(8,128)S(1)}, u32[]{:S(2)}, u32[]{:S(2)}) collective-permute-start(f32[128,512]{1,0:T(8,128)S(1)} %multiply_add_fusion.7), channel_id=1, source_target_pairs={{4,0},{8,4},{12,8},{16,12},{20,16},{24,20},{28,24},{32,28},{36,32}... | collective-permute-start | bytes 786440 | tf_op jit(solution)/shard_map/while/body/eval_jaxpr/ppermute | solution.py:15
  (25 other events, 725.1 us)
Sparse Core Ops, SparseCore 0:
  296.9 53.3 all-gather.1
  352.6 32.0 reduce-scatter.1
  671.7 134.1 all-reduce.5
where the time goes:
time: 820 us; the launch traced here: 818 us
  waiting for transfers between devices  525 us (64%)
  starting transfers between devices  230 us (28%)
  other arithmetic  24.4 us (3%)
  between operations  14.1 us (2%)
  matrix products  12.6 us (2%)
  local copies, waits for them, and re-layouts  9.91 us (1%)
    ppermute x62, waiting for transfers between devices, passed_along(): lax.ppermute(value, axis, [(source, source + steps) for source in range(f...  318 us
    ppermute x62, starting transfers between devices, passed_along(): lax.ppermute(value, axis, [(source, source + steps) for source in range(f...  230 us
    psum x1, waiting for transfers between devices, body(): grad_b, grad_c = lax.psum((grad_b_part, grad_c_part), 'tm')  134 us
    all_gather x1, waiting for transfers between devices, body(): lax.all_gather(states_bf, 'chan', axis=1, tiled=True)  49.7 us
    reduce_scatter x1, waiting for transfers between devices, body(): lax.psum_scatter(jnp.einsum('kup,fkus->pfs', kernel_c, cot_stack, preferr...  23.6 us
  transfers between devices with their start and end apart: 65, of which 65 were waited for; matrix products, arithmetic and copies ran while one was open for 2% of the time, Pallas kernels for 0%

commit v1 on v0

--- a/solution.py
+++ b/solution.py
@@ -13,6 +13,21 @@
     count = lax.axis_size(axis)
     first, last = (max(0, -steps), min(count, count - steps))
     return lax.ppermute(value, axis, [(source, source + steps) for source in range(first, last)])
+
+
+def exclusive_scan(factor, value, axis, direction):
+    rows = value.shape[0]
+    packed = jnp.concatenate([value, jnp.pad(factor, (0, value.shape[1] - rows))[None]], axis=0)
+    packed = passed_along(packed, axis, direction)
+    distance = 1
+    while distance < lax.axis_size(axis):
+        arrived = passed_along(packed, axis, direction * distance)
+        scale = packed[rows, :rows]
+        combined_value = scale[:, None] * arrived[:rows] + packed[:rows]
+        combined_factor = packed[rows] * arrived[rows]
+        packed = jnp.concatenate([combined_value, combined_factor[None]], axis=0)
+        distance *= 2
+    return packed[:rows]
 
 
 def shift_cells(source, row_shift, col_shift, grid_width):
@@ -48,12 +63,7 @@
 
     local_end, local_states = lax.scan(advance, blank_state, (decay, drives))
     decay_total = jnp.prod(decay, axis=0)
-
-    def relay_state(turn_index, carried):
-        outgoing = decay_total[:, None] * carried + local_end
-        return passed_along(outgoing, "tm", 1)
-
-    entering = lax.fori_loop(0, lax.axis_size("tm") - 1, relay_state, blank_state)
+    entering = exclusive_scan(decay_total, local_end, "tm", 1)
     cumulative = jnp.cumprod(decay, axis=0)
     states = local_states + cumulative[:, :, None] * entering[None]
     previous = jnp.concatenate([entering[None], states[:-1]], axis=0)
@@ -74,11 +84,7 @@
 
     message, local_adjoint = lax.scan(retreat, blank_state, (decay, injected), reverse=True)
 
-    def relay_adjoint(turn_index, carried):
-        outgoing = decay_total[:, None] * carried + message
-        return passed_along(outgoing, "tm", -1)
-
-    arriving = lax.fori_loop(0, lax.axis_size("tm") - 1, relay_adjoint, blank_state)
+    arriving = exclusive_scan(decay_total, message, "tm", -1)
     suffix = jnp.flip(jnp.cumprod(jnp.flip(decay, 0), 0), 0)
     later_decay = jnp.concatenate([suffix[1:], jnp.ones_like(decay[:1])], axis=0)
     adjoint = local_adjoint + later_decay[:, :, None] * arriving[None]

time: 820 us -> 275 us (0.34)
  waiting for transfers between devices: 525 us -> 169 us
  starting transfers between devices: 230 us -> 45.6 us
    ppermute x62 -> x12, waiting for transfers between devices: 318 us -> 29.3 us  [passed_along(): lax.ppermute(value, axis, [(source, source + steps) for source in range(f...]
    ppermute x62 -> x12, starting transfers between devices: 230 us -> 45.5 us  [passed_along(): lax.ppermute(value, axis, [(source, source + steps) for source in range(f...]
    all_gather x1, waiting for transfers between devices: 49.7 us -> 3.49 us  [body(): lax.all_gather(states_bf, 'chan', axis=1, tiled=True)]
    psum x1, waiting for transfers between devices: 134 us -> 109 us  [body(): grad_b, grad_c = lax.psum((grad_b_part, grad_c_part), 'tm')]
  transfers between devices with their start and end apart: 65 -> 15, of which waited for: 65 -> 13; matrix products, arithmetic and copies ran while one was open for 2% -> 5% of each run, Pallas kernels for 0% -> 0%
where the time goes in v1:
time: 275 us
  waiting for transfers between devices  169 us (61%)
  starting transfers between devices  45.6 us (17%)
  other arithmetic  23.4 us (9%)
  between operations  14.4 us (5%)
  matrix products  12.6 us (5%)
  local copies, waits for them, and re-layouts  9.9 us (4%)
    psum x1, waiting for transfers between devices, body(): grad_b, grad_c = lax.psum((grad_b_part, grad_c_part), 'tm')  109 us
    ppermute x12, starting transfers between devices, passed_along(): lax.ppermute(value, axis, [(source, source + steps) for source in range(f...  45.5 us
    ppermute x12, waiting for transfers between devices, passed_along(): lax.ppermute(value, axis, [(source, source + steps) for source in range(f...  29.3 us
    reduce_scatter x1, waiting for transfers between devices, body(): lax.psum_scatter(jnp.einsum('kup,fkus->pfs', kernel_c, cot_stack, preferr...  26.3 us
    unnamed x26, other arithmetic  16.5 us
    unnamed x18, local copies, waits for them, and re-layouts  7.18 us
  transfers between devices with their start and end apart: 15, of which 13 were waited for; matrix products, arithmetic and copies ran while one was open for 5% of the time, Pallas kernels for 0%

profile of v1, /device:TPU:1, one launch (start us, length us, event | category | flops | bytes accessed | tf_op | source)
XLA Modules:
  0.0 274.6 jit_solution(10285928507059048756)
XLA Ops:
  7.3 1.1 fusion.68
  8.3 1.0 fusion.71
  9.4 1.0 fusion.74
  10.4 1.0 fusion.77
  11.4 0.9 bitcast_dynamic-update-slice_fusion.4
  12.3 1.0 fusion.80
  13.3 1.0 fusion.83
  14.4 1.0 fusion.86
  15.4 1.0 fusion.89
  16.4 2.4 convolution_bitcast_fusion
  21.3 2.1 copy-done.4
  23.4 1.4 convolution_bitcast_fusion.3
  25.5 26.3 %reduce-scatter.2.cloned.1.call-done = f32[128,2,512]{0,2,1:T(8,128)} async-done(((f32[512,2,512]{0,2,1:T(8,128)}), f32[128,2,512]{0,2,1:T(8,128)}) %reduce-scatter.2.cloned.1.call-update) | async-done | bytes 524304 | tf_op jit(solution)/shard_map/reduce_scatter | solution.py:72
  51.9 2.6 while.30
  51.9 1.0 constant_dynamic-slice_fusion.6
  53.2 1.0 constant_dynamic-slice_fusion.6
  54.5 3.8 %collective-permute-start.6 = (f32[129,512]{1,0:T(8,128)S(1)}, f32[129,512]{1,0:T(8,128)S(1)}, u32[]{:S(2)}, u32[]{:S(2)}) collective-permute-start(f32[129,512]{1,0:T(8,128)S(1)} %get-tuple-element.214), channel_id=1, source_target_pairs={{0,4},{4,8},{8,12},{12,16},{16,20},{20,24},{24,28},{28,32},{32,36}... | collective-permute-start | bytes 792584 | tf_op jit(solution)/shard_map/ppermute | solution.py:15
  58.3 1.9 collective-permute-start
  60.4 1.4 collective-permute-done.6
  61.8 4.4 %collective-permute-start.7 = (f32[129,512]{1,0:T(8,128)S(1)}, f32[129,512]{1,0:T(8,128)S(1)}, u32[]{:S(2)}, u32[]{:S(2)}) collective-permute-start(f32[129,512]{1,0:T(8,128)S(1)} %collective-permute-done.6), channel_id=1, source_target_pairs={{0,4},{4,8},{8,12},{12,16},{16,20},{20,24},{24,28},{28,32},{32,36}... | collective-permute-start | bytes 792584 | tf_op jit(solution)/shard_map/ppermute | solution.py:15
  66.2 1.9 collective-permute-start.1
  68.2 1.5 collective-permute-done.7
  69.8 3.2 %collective-permute-start.8 = (f32[129,512]{1,0:T(8,128)S(1)}, f32[129,512]{1,0:T(8,128)S(1)}, u32[]{:S(2)}, u32[]{:S(2)}) collective-permute-start(f32[129,512]{1,0:T(8,128)S(1)} %pad_maximum_fusion.6), channel_id=1, source_target_pairs={{0,8},{4,12},{8,16},{12,20},{16,24},{20,28},{24,32},{28,36},{32,40... | collective-permute-start | bytes 792584 | tf_op jit(solution)/shard_map/ppermute | solution.py:15
  73.0 1.1 collective-permute-done.1
  74.2 1.3 collective-permute-start.2
  75.5 2.1 collective-permute-done.8
  77.8 8.0 %collective-permute-start.9 = (f32[129,512]{1,0:T(8,128)S(1)}, f32[129,512]{1,0:T(8,128)S(1)}, u32[]{:S(2)}, u32[]{:S(2)}) collective-permute-start(f32[129,512]{1,0:T(8,128)S(1)} %pad_maximum_fusion.7), channel_id=1, source_target_pairs={{0,16},{4,20},{8,24},{12,28},{16,32},{20,36},{24,40},{28,44},{32,4... | collective-permute-start | bytes 792584 | tf_op jit(solution)/shard_map/ppermute | solution.py:15
  86.0 1.3 collective-permute-start.3
  87.3 4.0 %collective-permute-done.9 = f32[129,512]{1,0:T(8,128)S(1)} collective-permute-done((f32[129,512]{1,0:T(8,128)S(1)}, f32[129,512]{1,0:T(8,128)S(1)}, u32[]{:S(2)}, u32[]{:S(2)}) %collective-permute-start.9) | collective-permute-done | bytes 264224 | tf_op jit(solution)/shard_map/ppermute | solution.py:15
  91.4 4.3 %collective-permute-start.10 = (f32[129,512]{1,0:T(8,128)S(1)}, f32[129,512]{1,0:T(8,128)S(1)}, u32[]{:S(2)}, u32[]{:S(2)}) collective-permute-start(f32[129,512]{1,0:T(8,128)S(1)} %pad_maximum_fusion.8), channel_id=1, source_target_pairs={{0,32},{4,36},{8,40},{12,44},{16,48},{20,52},{24,56},{28,60},{32,6... | collective-permute-start | bytes 792584 | tf_op jit(solution)/shard_map/ppermute | solution.py:15
  95.8 1.8 collective-permute-done.3
  97.7 1.5 collective-permute-done.10
  99.4 12.6 %collective-permute-start.11 = (f32[129,512]{1,0:T(8,128)S(1)}, f32[129,512]{1,0:T(8,128)S(1)}, u32[]{:S(2)}, u32[]{:S(2)}) collective-permute-start(f32[129,512]{1,0:T(8,128)S(1)} %pad_maximum_fusion.9), channel_id=1, source_target_pairs={{0,64},{4,68},{8,72},{12,76},{16,80},{20,84},{24,88},{28,92},{32,9... | collective-permute-start | bytes 792584 | tf_op jit(solution)/shard_map/ppermute | solution.py:15
  112.0 1.3 collective-permute-start.4
  113.3 2.4 collective-permute-done.11
  115.8 0.8 fusion.99
  116.7 6.1 %collective-permute-done.4 = f32[129,512]{1,0:T(8,128)} collective-permute-done((f32[129,512]{1,0:T(8,128)S(1)}, f32[129,512]{1,0:T(8,128)}, u32[]{:S(2)}, u32[]{:S(2)}) %collective-permute-start.4) | collective-permute-done | bytes 264224 | tf_op jit(solution)/shard_map/ppermute | solution.py:15
  123.5 1.0 fusion.61
  124.6 1.5 collective-permute-start.5
  126.2 7.2 %collective-permute-done.5 = f32[129,512]{1,0:T(8,128)S(1)} collective-permute-done((f32[129,512]{1,0:T(8,128)S(1)}, f32[129,512]{1,0:T(8,128)S(1)}, u32[]{:S(2)}, u32[]{:S(2)}) %collective-permute-start.5) | collective-permute-done | bytes 264224 | tf_op jit(solution)/shard_map/ppermute | solution.py:15
  133.5 4.9 %convolution_bitcast_fusion.2 = f32[9,128,256]{1,2,0:T(8,128)} fusion(bf16[2,9,256,512]{3,2,0,1:T(8,128)(2,1)} %copy-done.4, f32[2,128,512]{2,1,0:T(8,128)S(1)} %get-tuple-element.135, f32[128,512]{1,0:T(8,128)S(1)} %fusion.60, f32[2,128]{1,0:T(2,128)S(1)} %broadcast_select_fusion), kind=kOutput, calls=%fused_computation.22 | convolution fusion | flops 604372992 | bytes 6685696 | tf_op jit(solution)/shard_map/fps,fkcs->kpc/dot_general | solution.py:93
  138.4 3.5 %all-gather.2.cloned.1.call-done = bf16[2,512,512]{2,1,0:T(8,128)(2,1)} async-done(((bf16[2,128,512]{2,1,0:T(8,128)(2,1)}), bf16[2,512,512]{2,1,0:T(8,128)(2,1)}) %all-gather.2.cloned.1.call-update) | async-done | bytes 1048592 | tf_op jit(solution)/shard_map/all_gather | solution.py:96
  141.8 1.7 fusion.4
  143.6 1.8 fusion.7
  148.8 4.0 %convolution_bitcast_fusion.1 = f32[9,64,512]{2,1,0:T(8,128)} fusion(bf16[2,9,512,512]{3,2,0,1:T(8,128)(2,1)S(1)} %fusion.25, bf16[2,64,512]{2,1,0:T(8,128)(2,1)S(1)} %copy-done.3), kind=kOutput, calls=%fused_computation.21 | convolution fusion | flops 603979776 | bytes 10747904 | tf_op jit(solution)/shard_map/fus,fkps->kup/dot_general | solution.py:97
  153.6 109.4 %all-reduce.7.cloned.1.call-done = (f32[9,128,256]{1,2,0:T(8,128)}, f32[9,64,512]{2,1,0:T(8,128)}) async-done(((f32[9,128,256]{1,2,0:T(8,128)}, f32[9,64,512]{2,1,0:T(8,128)}), (f32[9,128,256]{1,2,0:T(8,128)}, f32[9,64,512]{2,1,0:T(8,128)})) %all-reduce.7.cloned.1.call-update) | async-done | bytes 2359312 | tf_op jit(solution)/shard_map/psum | solution.py:100
  263.0 2.7 copy.19
  265.7 2.4 copy.78
  (107 shorter events, 10.6 us)
Async XLA Ops:
  7.2 9.2 %copy-start = (bf16[9,64,512]{2,1,0:T(8,128)(2,1)S(1)}, bf16[9,64,512]{2,1,0:T(8,128)(2,1)}, u32[]{:S(2)}) copy-start(bf16[9,64,512]{2,1,0:T(8,128)(2,1)} %param.12) | copy-start | bytes 1769476
  7.2 44.6 %reduce-scatter.2.cloned.1.call-start = ((), (), s32[]{:S(2)}) async-start(), calls=%async_computation.1 | async-start | bytes 2621440 | tf_op jit(solution)/shard_map/reduce_scatter | solution.py:72
  16.4 2.5 copy-start.5
  16.4 2.5 copy-start.2
  18.8 123.0 %all-gather.2.cloned.1.call-start = ((), (), s32[]{:S(2)}) async-start(), calls=%async_computation.2 | async-start | bytes 1310720 | tf_op jit(solution)/shard_map/all_gather | solution.py:96
  18.9 4.5 %copy-start.7 = (bf16[9,128,256]{2,1,0:T(8,128)(2,1)S(1)}, bf16[9,128,256]{2,1,0:T(8,128)(2,1)}, u32[]{:S(2)}) copy-start(bf16[9,128,256]{2,1,0:T(8,128)(2,1)} %param.11) | copy-start | bytes 1769476
  21.3 2.1 copy-start.4
  54.5 7.3 %collective-permute-start.6 = (f32[129,512]{1,0:T(8,128)S(1)}, f32[129,512]{1,0:T(8,128)S(1)}, u32[]{:S(2)}, u32[]{:S(2)}) collective-permute-start(f32[129,512]{1,0:T(8,128)S(1)} %get-tuple-element.214), channel_id=1, source_target_pairs={{0,4},{4,8},{8,12},{12,16},{16,20},{20,24},{24,28},{28,32},{32,36}... | collective-permute-start | bytes 792584 | tf_op jit(solution)/shard_map/ppermute | solution.py:15
  58.3 7.9 %collective-permute-start = (f32[129,512]{1,0:T(8,128)S(1)}, f32[129,512]{1,0:T(8,128)S(1)}, u32[]{:S(2)}, u32[]{:S(2)}) collective-permute-start(f32[129,512]{1,0:T(8,128)S(1)} %get-tuple-element.215), channel_id=1, source_target_pairs={{4,0},{8,4},{12,8},{16,12},{20,16},{24,20},{28,24},{32,28},{36,32}... | collective-permute-start | bytes 792584 | tf_op jit(solution)/shard_map/ppermute | solution.py:15
  61.8 7.9 %collective-permute-start.7 = (f32[129,512]{1,0:T(8,128)S(1)}, f32[129,512]{1,0:T(8,128)S(1)}, u32[]{:S(2)}, u32[]{:S(2)}) collective-permute-start(f32[129,512]{1,0:T(8,128)S(1)} %collective-permute-done.6), channel_id=1, source_target_pairs={{0,4},{4,8},{8,12},{12,16},{16,20},{20,24},{24,28},{28,32},{32,36}... | collective-permute-start | bytes 792584 | tf_op jit(solution)/shard_map/ppermute | solution.py:15
  66.2 7.9 %collective-permute-start.1 = (f32[129,512]{1,0:T(8,128)S(1)}, f32[129,512]{1,0:T(8,128)S(1)}, u32[]{:S(2)}, u32[]{:S(2)}) collective-permute-start(f32[129,512]{1,0:T(8,128)S(1)} %collective-permute-done), channel_id=1, source_target_pairs={{4,0},{8,4},{12,8},{16,12},{20,16},{24,20},{28,24},{32,28},{36,32}... | collective-permute-start | bytes 792584 | tf_op jit(solution)/shard_map/ppermute | solution.py:15
  69.8 7.9 %collective-permute-start.8 = (f32[129,512]{1,0:T(8,128)S(1)}, f32[129,512]{1,0:T(8,128)S(1)}, u32[]{:S(2)}, u32[]{:S(2)}) collective-permute-start(f32[129,512]{1,0:T(8,128)S(1)} %pad_maximum_fusion.6), channel_id=1, source_target_pairs={{0,8},{4,12},{8,16},{12,20},{16,24},{20,28},{24,32},{28,36},{32,40... | collective-permute-start | bytes 792584 | tf_op jit(solution)/shard_map/ppermute | solution.py:15
  74.2 11.6 %collective-permute-start.2 = (f32[129,512]{1,0:T(8,128)S(1)}, f32[129,512]{1,0:T(8,128)S(1)}, u32[]{:S(2)}, u32[]{:S(2)}) collective-permute-start(f32[129,512]{1,0:T(8,128)S(1)} %pad_maximum_fusion.2), channel_id=1, source_target_pairs={{8,0},{12,4},{16,8},{20,12},{24,16},{28,20},{32,24},{36,28},{40,32... | collective-permute-start | bytes 792584 | tf_op jit(solution)/shard_map/ppermute | solution.py:15
  77.8 48.3 %copy-start.6 = (pred[2]{0:T(512)(128)(4,1)S(1)}, pred[2]{0:T(512)(128)(4,1)}, u32[]{:S(2)}) copy-start(pred[2]{0:T(512)(128)(4,1)} %constant.163.clone.1) | copy-start | bytes 10
  77.8 13.5 %collective-permute-start.9 = (f32[129,512]{1,0:T(8,128)S(1)}, f32[129,512]{1,0:T(8,128)S(1)}, u32[]{:S(2)}, u32[]{:S(2)}) collective-permute-start(f32[129,512]{1,0:T(8,128)S(1)} %pad_maximum_fusion.7), channel_id=1, source_target_pairs={{0,16},{4,20},{8,24},{12,28},{16,32},{20,36},{24,40},{28,44},{32,4... | collective-permute-start | bytes 792584 | tf_op jit(solution)/shard_map/ppermute | solution.py:15
  86.0 11.6 %collective-permute-start.3 = (f32[129,512]{1,0:T(8,128)S(1)}, f32[129,512]{1,0:T(8,128)S(1)}, u32[]{:S(2)}, u32[]{:S(2)}) collective-permute-start(f32[129,512]{1,0:T(8,128)S(1)} %pad_maximum_fusion.3), channel_id=1, source_target_pairs={{16,0},{20,4},{24,8},{28,12},{32,16},{36,20},{40,24},{44,28},{48,3... | collective-permute-start | bytes 792584 | tf_op jit(solution)/shard_map/ppermute | solution.py:15
  91.4 7.8 %collective-permute-start.10 = (f32[129,512]{1,0:T(8,128)S(1)}, f32[129,512]{1,0:T(8,128)S(1)}, u32[]{:S(2)}, u32[]{:S(2)}) collective-permute-start(f32[129,512]{1,0:T(8,128)S(1)} %pad_maximum_fusion.8), channel_id=1, source_target_pairs={{0,32},{4,36},{8,40},{12,44},{16,48},{20,52},{24,56},{28,60},{32,6... | collective-permute-start | bytes 792584 | tf_op jit(solution)/shard_map/ppermute | solution.py:15
  99.4 16.3 %collective-permute-start.11 = (f32[129,512]{1,0:T(8,128)S(1)}, f32[129,512]{1,0:T(8,128)S(1)}, u32[]{:S(2)}, u32[]{:S(2)}) collective-permute-start(f32[129,512]{1,0:T(8,128)S(1)} %pad_maximum_fusion.9), channel_id=1, source_target_pairs={{0,64},{4,68},{8,72},{12,76},{16,80},{20,84},{24,88},{28,92},{32,9... | collective-permute-start | bytes 792584 | tf_op jit(solution)/shard_map/ppermute | solution.py:15
  112.0 10.8 %collective-permute-start.4 = (f32[129,512]{1,0:T(8,128)S(1)}, f32[129,512]{1,0:T(8,128)}, u32[]{:S(2)}, u32[]{:S(2)}) collective-permute-start(f32[129,512]{1,0:T(8,128)S(1)} %pad_maximum_fusion.4), channel_id=1, source_target_pairs={{32,0},{36,4},{40,8},{44,12},{48,16},{52,20},{56,24},{60,28},{64,3... | collective-permute-start | bytes 792584 | tf_op jit(solution)/shard_map/ppermute | solution.py:15
  116.6 146.4 %all-reduce.7.cloned.1.call-start = ((), (), s32[]{:S(2)}) async-start(), calls=%async_computation.3 | async-start | bytes 4718592 | tf_op jit(solution)/shard_map/psum | solution.py:100
  124.6 8.8 %collective-permute-start.5 = (f32[129,512]{1,0:T(8,128)S(1)}, f32[129,512]{1,0:T(8,128)S(1)}, u32[]{:S(2)}, u32[]{:S(2)}) collective-permute-start(f32[129,512]{1,0:T(8,128)S(1)} %pad_maximum_fusion.5), channel_id=1, source_target_pairs={{64,0},{68,4},{72,8},{76,12},{80,16},{84,20},{88,24},{92,28},{96,3... | collective-permute-start | bytes 792584 | tf_op jit(solution)/shard_map/ppermute | solution.py:15
  141.8 3.5 %copy-start.1 = (bf16[2,512,512]{2,1,0:T(8,128)(2,1)S(1)}, bf16[2,512,512]{2,1,0:T(8,128)(2,1)}, u32[]{:S(2)}) copy-start(bf16[2,512,512]{2,1,0:T(8,128)(2,1)} %all-gather.2.cloned.1.call-done) | copy-start | bytes 3145732
  146.6 2.2 copy-start.3
Sparse Core Ops, SparseCore 0:
  18.9 32.8 reduce-scatter.1
  116.8 25.0 all-gather.1
  152.9 110.0 all-reduce.6

commit v2 on v0

--- a/solution.py
+++ b/solution.py
@@ -13,6 +13,42 @@
     count = lax.axis_size(axis)
     first, last = (max(0, -steps), min(count, count - steps))
     return lax.ppermute(value, axis, [(source, source + steps) for source in range(first, last)])
+
+
+def scan_chunks(factor, value, reverse):
+    count = value.shape[0]
+    distance = 1
+    while distance < count:
+        if reverse:
+            pads = ((0, distance), (0, 0), (0, 0))
+            earlier_value = jnp.pad(value[distance:], pads)
+            earlier_factor = jnp.pad(factor[distance:], pads)
+        else:
+            pads = ((distance, 0), (0, 0), (0, 0))
+            earlier_value = jnp.pad(value[:-distance], pads)
+            earlier_factor = jnp.pad(factor[:-distance], pads)
+        value = value + factor * earlier_value
+        factor = factor * earlier_factor
+        distance *= 2
+    return value
+
+
+def block_scans(factor, forward_value, backward_value, axis):
+    count = lax.axis_size(axis)
+    rows, cells = forward_value.shape
+    chunk = rows // count
+    factor_row = jnp.pad(factor.reshape(count, chunk), ((0, 0), (0, cells - chunk)))[:, None, :]
+    packed = jnp.concatenate(
+        [forward_value.reshape(count, chunk, cells), backward_value.reshape(count, chunk, cells), factor_row], axis=1
+    )
+    gathered = lax.all_to_all(packed, axis, 0, 0, tiled=True)
+    block_factor = gathered[:, 2 * chunk, :chunk][:, :, None]
+    forward_total = scan_chunks(block_factor, gathered[:, :chunk], False)
+    backward_total = scan_chunks(block_factor, gathered[:, chunk : 2 * chunk], True)
+    entering = jnp.pad(forward_total[:-1], ((1, 0), (0, 0), (0, 0)))
+    arriving = jnp.pad(backward_total[1:], ((0, 1), (0, 0), (0, 0)))
+    returned = lax.all_to_all(jnp.concatenate([entering, arriving], axis=1), axis, 0, 0, tiled=True)
+    return returned[:, :chunk].reshape(rows, cells), returned[:, chunk:].reshape(rows, cells)
 
 
 def shift_cells(source, row_shift, col_shift, grid_width):
@@ -48,16 +84,6 @@
 
     local_end, local_states = lax.scan(advance, blank_state, (decay, drives))
     decay_total = jnp.prod(decay, axis=0)
-
-    def relay_state(turn_index, carried):
-        outgoing = decay_total[:, None] * carried + local_end
-        return passed_along(outgoing, "tm", 1)
-
-    entering = lax.fori_loop(0, lax.axis_size("tm") - 1, relay_state, blank_state)
-    cumulative = jnp.cumprod(decay, axis=0)
-    states = local_states + cumulative[:, :, None] * entering[None]
-    previous = jnp.concatenate([entering[None], states[:-1]], axis=0)
-    states_bf = states.astype(jnp.bfloat16)
     cot_stack = stencil_stack(cotangent, W, -1)
     injected = lax.psum_scatter(
         jnp.einsum("kup,fkus->pfs", kernel_c, cot_stack, preferred_element_type=jnp.float32),
@@ -74,11 +100,11 @@
 
     message, local_adjoint = lax.scan(retreat, blank_state, (decay, injected), reverse=True)
 
-    def relay_adjoint(turn_index, carried):
-        outgoing = decay_total[:, None] * carried + message
-        return passed_along(outgoing, "tm", -1)
-
-    arriving = lax.fori_loop(0, lax.axis_size("tm") - 1, relay_adjoint, blank_state)
+    entering, arriving = block_scans(decay_total, local_end, message, "tm")
+    cumulative = jnp.cumprod(decay, axis=0)
+    states = local_states + cumulative[:, :, None] * entering[None]
+    previous = jnp.concatenate([entering[None], states[:-1]], axis=0)
+    states_bf = states.astype(jnp.bfloat16)
     suffix = jnp.flip(jnp.cumprod(jnp.flip(decay, 0), 0), 0)
     later_decay = jnp.concatenate([suffix[1:], jnp.ones_like(decay[:1])], axis=0)
     adjoint = local_adjoint + later_decay[:, :, None] * arriving[None]

time: 820 us -> 251 us (0.31)
  waiting for transfers between devices: 525 us -> 160 us
  starting transfers between devices: 230 us -> 4.23 us
  blocking collectives: 0 us -> 24.4 us
    ppermute x62 -> x0, waiting for transfers between devices: 318 us -> none  [passed_along(): lax.ppermute(value, axis, [(source, source + steps) for source in range(f...]
    ppermute x62 -> x0, starting transfers between devices: 230 us -> none  [passed_along(): lax.ppermute(value, axis, [(source, source + steps) for source in range(f...]
    all_gather x1, waiting for transfers between devices: 49.7 us -> 12.6 us  [body(): lax.all_gather(states_bf, 'chan', axis=1, tiled=True)]
    all_to_all x0 -> x1, blocking collectives: none -> 24.4 us  [block_scans(): gathered = lax.all_to_all(packed, axis, 0, 0, tiled=True)]
    psum x1, waiting for transfers between devices: 134 us -> 109 us  [body(): grad_b, grad_c = lax.psum((grad_b_part, grad_c_part), 'tm')]
    all_to_all x0 -> x1, waiting for transfers between devices: none -> 11.5 us  [block_scans(): lax.all_to_all(jnp.concatenate([entering, arriving], axis=1), axis, 0, 0,...]
  transfers between devices with their start and end apart: 65 -> 4, of which waited for: 65 -> 4; matrix products, arithmetic and copies ran while one was open for 2% -> 4% of each run, Pallas kernels for 0% -> 0%
where the time goes in v2:
time: 251 us; the launch traced here: 250 us
  waiting for transfers between devices  160 us (64%)
  blocking collectives  24.4 us (10%)
  other arithmetic  22.3 us (9%)
  between operations  14.3 us (6%)
  matrix products  12.5 us (5%)
  local copies, waits for them, and re-layouts  12.2 us (5%)
  starting transfers between devices  4.23 us (2%)
    psum x1, waiting for transfers between devices, body(): grad_b, grad_c = lax.psum((grad_b_part, grad_c_part), 'tm')  109 us
    reduce_scatter x1, waiting for transfers between devices, body(): lax.psum_scatter(jnp.einsum('kup,fkus->pfs', kernel_c, cot_stack, preferr...  26.7 us
    all_to_all x1, blocking collectives, block_scans(): gathered = lax.all_to_all(packed, axis, 0, 0, tiled=True)  24.4 us
    unnamed x26, other arithmetic  15.8 us
    all_gather x1, waiting for transfers between devices, body(): lax.all_gather(states_bf, 'chan', axis=1, tiled=True)  12.6 us
    all_to_all x1, waiting for transfers between devices, block_scans(): lax.all_to_all(jnp.concatenate([entering, arriving], axis=1), axis, 0, 0,...  11.5 us
    unnamed x21, local copies, waits for them, and re-layouts  7.58 us
  transfers between devices with their start and end apart: 4, of which 4 were waited for; matrix products, arithmetic and copies ran while one was open for 4% of the time, Pallas kernels for 0%

profile of v2, /device:TPU:1, one launch (start us, length us, event | category | flops | bytes accessed | tf_op | source)
XLA Modules:
  0.0 250.4 jit_solution(12761832331705758522)
XLA Ops:
  7.3 1.1 fusion.60
  8.3 1.0 fusion.63
  9.4 1.0 fusion.66
  10.4 1.0 fusion.69
  11.4 0.9 bitcast_dynamic-update-slice_fusion.4
  12.3 1.0 fusion.72
  13.3 1.0 fusion.75
  14.4 1.0 fusion.78
  15.4 1.0 fusion.81
  16.4 2.4 convolution_bitcast_fusion
  19.1 0.2 copy.34
  19.3 0.2 fusion.30
  19.8 0.2 fusion.39
  20.0 0.2 bitcast_dynamic-update-slice_fusion.3
  20.2 0.2 fusion.42
  20.4 0.2 fusion.45
  20.9 2.1 copy-done.2
  23.0 1.4 convolution_bitcast_fusion.3
  24.4 0.6 while.31
  25.2 26.7 %reduce-scatter.2.cloned.1.call-done = f32[128,2,512]{0,2,1:T(8,128)} async-done(((f32[512,2,512]{0,2,1:T(8,128)}), f32[128,2,512]{0,2,1:T(8,128)}) %reduce-scatter.2.cloned.1.call-update) | async-done | bytes 524304 | tf_op jit(solution)/shard_map/reduce_scatter | solution.py:88
  51.9 2.6 %while.30 = (s32[]{:T(128)}, f32[128,512]{1,0:T(8,128)S(1)}, f32[2,128,512]{2,1,0:T(8,128)S(1)}, f32[2,128]{1,0:T(2,128)S(1)}, f32[2,128,512]{1,2,0:T(8,128)}, /*index=5*/s32[]{:T(128)}, s32[]{:T(128)}) while((s32[]{:T(128)}, f32[128,512]{1,0:T(8,128)S(1)}, f32[2,128,512]{2,1,0:T(8,128)S(1)}, f32[2,128]{1,0:T(2,128)S(1)}, ...), condition=%wide.region_2.3_spmd.clone, body=%wide.region_1.2_spmd.clone.sunk | while | flops 327684 | bytes 2623096 | solution.py:101
  51.9 1.0 constant_dynamic-slice_fusion.6
  53.2 1.0 constant_dynamic-slice_fusion.6
  54.6 0.2 pad_maximum_fusion
  54.8 24.4 %all_to_all.10 = f32[32,9,512]{2,1,0:T(8,128)S(1)} all-to-all(f32[32,9,512]{2,1,0:T(8,128)S(1)} %pad_maximum_fusion), channel_id=1, replica_groups=mesh['tm'=32,'chan'=4] {'tm'}, dimensions={0} | all-to-all | bytes 1179648 | tf_op jit(solution)/shard_map/all_to_all | solution.py:44
  80.9 0.2 slice_add_fusion.1
  81.2 0.2 multiply_add_fusion.4
  82.3 0.9 select_maximum_fusion
  83.2 3.9 %all-to-all-start.1 = ((f32[32,8,512]{2,1,0:T(8,128)}), f32[32,8,512]{2,1,0:T(8,128)S(1)}, u32[]{:S(2)}, u32[]{:S(2)}) async-start(f32[32,8,512]{2,1,0:T(8,128)} %select_maximum_fusion), calls=%async_computation.2 | async-start | bytes 1048576 | tf_op jit(solution)/shard_map/all_to_all | solution.py:50
  87.3 11.5 %all-to-all-done.1 = f32[32,8,512]{2,1,0:T(8,128)S(1)} async-done(((f32[32,8,512]{2,1,0:T(8,128)}), f32[32,8,512]{2,1,0:T(8,128)S(1)}, u32[]{:S(2)}, u32[]{:S(2)}) %all-to-all-start.1) | async-done | bytes 524320 | tf_op jit(solution)/shard_map/all_to_all | solution.py:50
  99.0 0.8 fusion.91
  99.8 0.2 all-reduce.27.cloned.1.call-start
  100.3 4.8 %convolution_bitcast_fusion.2 = f32[9,128,256]{1,2,0:T(8,128)} fusion(bf16[2,9,256,512]{2,3,1,0:T(8,128)(2,1)} %copy-done.2, f32[2,128,512]{2,1,0:T(8,128)S(1)} %get-tuple-element.135, f32[128,512]{1,0:T(8,128)S(1)} %mul.231, f32[2,128]{1,0:T(2,128)S(1)} %broadcast_select_fusion), kind=kOutput, calls=%fused_computation.22 | convolution fusion | flops 604372992 | bytes 6685696 | tf_op jit(solution)/shard_map/fps,fkcs->kpc/dot_general | solution.py:113
  105.1 12.6 %all-gather.2.cloned.1.call-done = bf16[2,512,512]{2,1,0:T(8,128)(2,1)} async-done(((bf16[2,128,512]{2,1,0:T(8,128)(2,1)}), bf16[2,512,512]{2,1,0:T(8,128)(2,1)}) %all-gather.2.cloned.1.call-update) | async-done | bytes 1048592 | tf_op jit(solution)/shard_map/all_gather | solution.py:116
  117.7 1.7 fusion.4
  119.4 1.8 fusion.7
  121.2 0.5 fusion.10
  121.7 0.5 fusion.13
  122.2 0.2 bitcast_dynamic-update-slice_fusion.2
  122.5 0.5 fusion.16
  123.0 0.5 fusion.19
  123.5 0.5 fusion.22
  124.1 0.5 fusion.25
  124.6 4.0 %convolution_bitcast_fusion.1 = f32[9,64,512]{2,1,0:T(8,128)} fusion(bf16[2,9,512,512]{3,2,0,1:T(8,128)(2,1)S(1)} %fusion.25, bf16[2,64,512]{2,1,0:T(8,128)(2,1)S(1)} %copy-done.3), kind=kOutput, calls=%fused_computation.21 | convolution fusion | flops 603979776 | bytes 10747904 | tf_op jit(solution)/shard_map/fus,fkps->kup/dot_general | solution.py:117
  128.7 0.8 fusion.52
  129.5 109.4 %all-reduce.27.cloned.1.call-done = (f32[9,128,256]{1,2,0:T(8,128)}, f32[9,64,512]{2,1,0:T(8,128)}) async-done(((f32[9,128,256]{1,2,0:T(8,128)}, f32[9,64,512]{2,1,0:T(8,128)}), (f32[9,128,256]{1,2,0:T(8,128)}, f32[9,64,512]{2,1,0:T(8,128)})) %all-reduce.27.cloned.1.call-update) | async-done | bytes 2359312 | tf_op jit(solution)/shard_map/psum | solution.py:120
  238.9 2.7 %copy.69 = f32[9,128,256]{2,1,0:T(8,128)} copy(f32[9,128,256]{1,2,0:T(8,128)} %get-tuple-element.221) | data formatting | bytes 2359296
  241.5 2.4 copy.130
  (100 shorter events, 5.5 us)
Async XLA Ops:
  7.2 9.2 %copy-start = (bf16[9,64,512]{2,1,0:T(8,128)(2,1)S(1)}, bf16[9,64,512]{2,1,0:T(8,128)(2,1)}, u32[]{:S(2)}) copy-start(bf16[9,64,512]{2,1,0:T(8,128)(2,1)} %param.12) | copy-start | bytes 1769476
  7.2 44.7 %reduce-scatter.2.cloned.1.call-start = ((), (), s32[]{:S(2)}) async-start(), calls=%async_computation.3 | async-start | bytes 2621440 | tf_op jit(solution)/shard_map/reduce_scatter | solution.py:88
  16.4 2.5 copy-start.6
  16.4 2.7 %copy-start.5 = (bf16[2,256,512]{2,1,0:T(8,128)(2,1)S(1)}, bf16[2,256,512]{2,1,0:T(8,128)(2,1)}, u32[]{:S(2)}) copy-start(bf16[2,256,512]{2,1,0:T(8,128)(2,1)} %param.9) | copy-start | bytes 1572868
  19.3 3.7 %copy-start.4 = (bf16[9,128,256]{2,1,0:T(8,128)(2,1)S(1)}, bf16[9,128,256]{2,1,0:T(8,128)(2,1)}, u32[]{:S(2)}) copy-start(bf16[9,128,256]{2,1,0:T(8,128)(2,1)} %param.11) | copy-start | bytes 1769476
  20.9 2.1 copy-start.2
  81.7 18.4 %copy-start.7 = (pred[2]{0:T(512)(128)(4,1)S(1)}, pred[2]{0:T(512)(128)(4,1)}, u32[]{:S(2)}) copy-start(pred[2]{0:T(512)(128)(4,1)} %constant.163.clone.1) | copy-start | bytes 10
  83.2 15.5 %all-to-all-start.1 = ((f32[32,8,512]{2,1,0:T(8,128)}), f32[32,8,512]{2,1,0:T(8,128)S(1)}, u32[]{:S(2)}, u32[]{:S(2)}) async-start(f32[32,8,512]{2,1,0:T(8,128)} %select_maximum_fusion), calls=%async_computation.2 | async-start | bytes 1048576 | tf_op jit(solution)/shard_map/all_to_all | solution.py:50
  87.2 30.5 %all-gather.2.cloned.1.call-start = ((), (), s32[]{:S(2)}) async-start(), calls=%async_computation.4 | async-start | bytes 1310720 | tf_op jit(solution)/shard_map/all_gather | solution.py:116
  99.8 139.1 %all-reduce.27.cloned.1.call-start = ((), (), s32[]{:S(2)}) async-start(), calls=%async_computation.5 | async-start | bytes 4718592 | tf_op jit(solution)/shard_map/psum | solution.py:120
  117.7 3.5 %copy-start.1 = (bf16[2,512,512]{2,1,0:T(8,128)(2,1)S(1)}, bf16[2,512,512]{2,1,0:T(8,128)(2,1)}, u32[]{:S(2)}) copy-start(bf16[2,512,512]{2,1,0:T(8,128)(2,1)} %all-gather.2.cloned.1.call-done) | copy-start | bytes 3145732
  122.4 2.2 copy-start.3
Sparse Core Ops, SparseCore 0:
  19.0 32.8 reduce-scatter.1
  99.9 17.6 all-gather.1
  128.7 110.1 all-reduce.26

commit v3 on v2

--- a/solution.py
+++ b/solution.py
@@ -1,7 +1,7 @@
 import jax
 import jax.numpy as jnp
 from jax import lax
-from jax.sharding import PartitionSpec as P
+from jax.sharding import Mesh, PartitionSpec as P
 
 W = 64
 
@@ -70,6 +70,25 @@
     return jnp.stack(parts, axis=source.ndim - 2)
 
 
+FRAME_AXES = ("chip", "core")
+
+
+def pair_then_chip_sum(first, second):
+    core = lax.axis_index("core")
+    swap = [(0, 1), (1, 0)]
+    first_flat, second_flat = first.reshape(-1), second.reshape(-1)
+    kept = jnp.where(core == 0, first_flat, second_flat)
+    sent = jnp.where(core == 0, second_flat, first_flat)
+    pair_sum = (kept + lax.ppermute(sent, "core", swap)).reshape(lax.axis_size("chip"), -1)
+    pieces = lax.all_to_all(pair_sum, "chip", 0, 0, tiled=True)
+    reduced = jnp.sum(pieces, axis=0, keepdims=True)
+    total = lax.all_to_all(jnp.broadcast_to(reduced, pieces.shape), "chip", 0, 0, tiled=True).reshape(-1)
+    partner = lax.ppermute(total, "core", swap)
+    first_total = jnp.where(core == 0, total, partner)
+    second_total = jnp.where(core == 0, partner, total)
+    return first_total.reshape(first.shape), second_total.reshape(second.shape)
+
+
 def body(inputs, decay, kernel_b, kernel_c, cotangent):
     local_rows = kernel_b.shape[1]
     cell_count = inputs.shape[-1]
@@ -100,7 +119,7 @@
 
     message, local_adjoint = lax.scan(retreat, blank_state, (decay, injected), reverse=True)
 
-    entering, arriving = block_scans(decay_total, local_end, message, "tm")
+    entering, arriving = block_scans(decay_total, local_end, message, FRAME_AXES)
     cumulative = jnp.cumprod(decay, axis=0)
     states = local_states + cumulative[:, :, None] * entering[None]
     previous = jnp.concatenate([entering[None], states[:-1]], axis=0)
@@ -117,17 +136,19 @@
     grad_c_part = jnp.einsum(
         "fus,fkps->kup", cotangent, shifted, preferred_element_type=jnp.float32
     )
-    grad_b, grad_c = lax.psum((grad_b_part, grad_c_part), "tm")
+    grad_b, grad_c = pair_then_chip_sum(grad_b_part, grad_c_part)
     return (grad_b, grad_c, decay_grad)
 
 
 def solution(mesh):
+    chan = mesh.shape["chan"]
+    frame_mesh = Mesh(mesh.devices.reshape(-1, 2, chan), (*FRAME_AXES, "chan"))
     in_specs = (
-        P("tm", None, None),
-        P("tm", "chan"),
+        P(FRAME_AXES, None, None),
+        P(FRAME_AXES, "chan"),
         P(None, "chan", None),
         P(None, "chan", None),
-        P("tm", "chan", None),
+        P(FRAME_AXES, "chan", None),
     )
-    out_specs = (P(None, "chan", None), P(None, "chan", None), P("tm", "chan"))
-    return jax.shard_map(body, mesh=mesh, in_specs=in_specs, out_specs=out_specs, check_vma=False)
+    out_specs = (P(None, "chan", None), P(None, "chan", None), P(FRAME_AXES, "chan"))
+    return jax.shard_map(body, mesh=frame_mesh, in_specs=in_specs, out_specs=out_specs, check_vma=False)

time: 251 us -> 194 us (0.77)
  waiting for transfers between devices: 160 us -> 54.1 us
  blocking collectives: 24.4 us -> 68.3 us
  starting transfers between devices: 4.23 us -> 9.97 us
    psum x1 -> x0, waiting for transfers between devices: 109 us -> none  [body(): grad_b, grad_c = lax.psum((grad_b_part, grad_c_part), 'tm')]
    all_to_all x0 -> x2, blocking collectives: none -> 43.9 us  [the longest x1 24.1 us: pair_then_chip_sum(): pieces = lax.all_to_all(pair_sum, 'chip', 0, 0, tiled=True)]
    ppermute x0 -> x2, starting transfers between devices: none -> 5.79 us  [the longest x1 2.96 us: pair_then_chip_sum(): partner = lax.ppermute(total, 'core', swap)]
    unnamed x21 -> x29, local copies, waits for them, and re-layouts: 7.58 us -> 3.47 us
    reshape x0 -> x2, local copies, waits for them, and re-layouts: none -> 3.75 us  [the longest x1 2.41 us: pair_then_chip_sum(): second_total.reshape(second.shape)]
    ppermute x0 -> x2, waiting for transfers between devices: none -> 3.22 us  [the longest x1 2.47 us: pair_then_chip_sum(): lax.ppermute(sent, 'core', swap)]
    unnamed x26, other arithmetic: 15.8 us -> 12.7 us
    select_n x0 -> x2, other arithmetic: none -> 2.59 us  [the longest x1 2.44 us: pair_then_chip_sum(): second_total = jnp.where(core == 0, partner, total)]
  transfers between devices with their start and end apart: 4 -> 5, of which waited for: 4 -> 5; matrix products, arithmetic and copies ran while one was open for 4% -> 6% of each run, Pallas kernels for 0% -> 0%
where the time goes in v3:
time: 194 us
  blocking collectives  68.3 us (35%)
  waiting for transfers between devices  54.1 us (28%)
  other arithmetic  22.1 us (11%)
  between operations  14.7 us (8%)
  local copies, waits for them, and re-layouts  13.8 us (7%)
  matrix products  10.5 us (5%)
  starting transfers between devices  9.97 us (5%)
    reduce_scatter x1, waiting for transfers between devices, body(): lax.psum_scatter(jnp.einsum('kup,fkus->pfs', kernel_c, cot_stack, preferr...  26.7 us
    all_to_all x1, blocking collectives, block_scans(): gathered = lax.all_to_all(packed, axis, 0, 0, tiled=True)  24.5 us
    all_to_all x1, blocking collectives, pair_then_chip_sum(): pieces = lax.all_to_all(pair_sum, 'chip', 0, 0, tiled=True)  24.1 us
    all_to_all x1, blocking collectives, pair_then_chip_sum(): lax.all_to_all(jnp.broadcast_to(reduced, pieces.shape), 'chip', 0, 0, til...  19.8 us
    all_gather x1, waiting for transfers between devices, body(): lax.all_gather(states_bf, 'chan', axis=1, tiled=True)  12.8 us
    unnamed x26, other arithmetic  12.7 us
    all_to_all x1, waiting for transfers between devices, block_scans(): lax.all_to_all(jnp.concatenate([entering, arriving], axis=1), axis, 0, 0,...  11.3 us
    all_to_all x1, starting transfers between devices, block_scans(): lax.all_to_all(jnp.concatenate([entering, arriving], axis=1), axis, 0, 0,...  3.92 us
  transfers between devices with their start and end apart: 5, of which 5 were waited for; matrix products, arithmetic and copies ran while one was open for 6% of the time, Pallas kernels for 0%

profile of v3, /device:TPU:1, one launch (start us, length us, event | category | flops | bytes accessed | tf_op | source)
XLA Modules:
  0.0 193.7 jit_solution(4221707975487912603)
XLA Ops:
  7.3 1.1 fusion.60
  8.3 1.0 fusion.63
  9.4 1.0 fusion.66
  10.4 1.0 fusion.69
  11.4 0.9 bitcast_dynamic-update-slice_fusion.4
  12.3 1.0 fusion.72
  13.7 2.4 %convolution_bitcast_fusion = f32[512,2,512]{0,2,1:T(8,128)} fusion(bf16[2,9,64,512]{3,2,1,0:T(8,128)(2,1)S(1)} %fusion.81, bf16[9,64,512]{2,1,0:T(8,128)(2,1)S(1)} %copy-done), kind=kOutput, calls=%fused_computation.20 | convolution fusion | flops 603979776 | bytes 3866624 | tf_op jit(solution)/shard_map/kup,fkus->pfs/dot_general | solution.py:108
  16.1 0.6 copy-done.10
  18.9 0.5 copy-done.8
  19.5 1.4 convolution_bitcast_fusion.2
  20.9 0.8 copy-done.2
  21.7 0.6 while.31
  22.4 26.7 %reduce-scatter.2.cloned.1.call-done = f32[128,2,512]{0,2,1:T(8,128)} async-done(((f32[512,2,512]{0,2,1:T(8,128)}), f32[128,2,512]{0,2,1:T(8,128)}) %reduce-scatter.2.cloned.1.call-update) | async-done | bytes 524304 | tf_op jit(solution)/shard_map/reduce_scatter | solution.py:107
  49.2 2.6 %while.30 = (s32[]{:T(128)}, f32[128,512]{1,0:T(8,128)S(1)}, f32[2,128,512]{2,1,0:T(8,128)S(1)}, f32[2,128]{1,0:T(2,128)S(1)}, f32[2,128,512]{1,2,0:T(8,128)}, /*index=5*/s32[]{:T(128)}, s32[]{:T(128)}) while((s32[]{:T(128)}, f32[128,512]{1,0:T(8,128)S(1)}, f32[2,128,512]{2,1,0:T(8,128)S(1)}, f32[2,128]{1,0:T(2,128)S(1)}, ...), condition=%wide.region_2.3_spmd.clone, body=%wide.region_1.2_spmd.clone.sunk | while | flops 327684 | bytes 2623096 | solution.py:120
  49.2 1.0 constant_dynamic-slice_fusion.6
  50.5 1.0 constant_dynamic-slice_fusion.6
  52.1 24.5 %all_to_all.25 = f32[32,9,512]{2,1,0:T(8,128)S(1)} all-to-all(f32[32,9,512]{2,1,0:T(8,128)S(1)} %pad_maximum_fusion), channel_id=1, replica_groups=mesh['chip'=16,'core'=2,'chan'=4] {'chip','core'}, dimensions={0} | all-to-all | bytes 1179648 | tf_op jit(solution)/shard_map/all_to_all | solution.py:44
  79.6 0.9 select_maximum_fusion
  80.6 3.9 %all-to-all-start.1 = ((f32[32,8,512]{2,1,0:T(8,128)}), f32[32,8,512]{2,1,0:T(8,128)S(1)}, u32[]{:S(2)}, u32[]{:S(2)}) async-start(f32[32,8,512]{2,1,0:T(8,128)} %select_maximum_fusion), calls=%async_computation.2 | async-start | bytes 1048576 | tf_op jit(solution)/shard_map/all_to_all | solution.py:50
  84.8 11.3 %all-to-all-done.1 = f32[32,8,512]{2,1,0:T(8,128)S(1)} async-done(((f32[32,8,512]{2,1,0:T(8,128)}), f32[32,8,512]{2,1,0:T(8,128)S(1)}, u32[]{:S(2)}, u32[]{:S(2)}) %all-to-all-start.1) | async-done | bytes 524320 | tf_op jit(solution)/shard_map/all_to_all | solution.py:50
  96.3 1.0 fusion.92
  97.6 3.8 %convolution_bitcast_fusion.1 = f32[9,128,256]{1,2,0:T(8,128)S(1)} fusion(bf16[2,9,256,512]{2,3,1,0:T(8,128)(2,1)} %copy-done.2, f32[2,128,512]{2,1,0:T(8,128)S(1)} %get-tuple-element.135, f32[128,512]{1,0:T(8,128)S(1)} %mul.231, f32[2,128]{1,0:T(2,128)S(1)} %broadcast_select_fusion.3), kind=kOutput, calls=%fused_computation.21 | convolution fusion | flops 604372992 | bytes 6685696 | tf_op jit(solution)/shard_map/fps,fkcs->kpc/dot_general | solution.py:132
  101.4 0.4 copy.140
  101.8 0.6 copy.151
  102.4 12.8 %all-gather.2.cloned.1.call-done = bf16[2,512,512]{2,1,0:T(8,128)(2,1)} async-done(((bf16[2,128,512]{2,1,0:T(8,128)(2,1)}), bf16[2,512,512]{2,1,0:T(8,128)(2,1)}) %all-gather.2.cloned.1.call-update) | async-done | bytes 1048592 | tf_op jit(solution)/shard_map/all_gather | solution.py:135
  115.2 1.7 fusion.4
  116.9 0.5 fusion.7
  117.5 0.5 fusion.10
  118.0 0.5 fusion.13
  118.7 0.5 fusion.16
  119.3 0.5 fusion.19
  119.8 0.5 fusion.22
  120.4 0.5 fusion.25
  120.9 2.9 %fusion.82 = f32[9,512,64,1]{1,2,3,0:T(8,128)S(1)} fusion(bf16[2,9,512,512]{3,2,0,1:T(8,128)(2,1)S(1)} %fusion.25, bf16[2,64,512]{2,1,0:T(8,128)(2,1)S(1)} %copy-done.3), kind=kOutput, calls=%fused_computation.144 | convolution fusion | flops 603979776 | bytes 10747904 | tf_op jit(solution)/shard_map/fus,fkps->kup/dot_general | solution.py:136
  123.8 0.3 copy.152
  124.3 2.8 %collective-permute-start = (f32[294912]{0:T(1024)S(1)}, f32[294912]{0:T(1024)S(1)}, u32[]{:S(2)}, u32[]{:S(2)}) collective-permute-start(f32[294912]{0:T(1024)S(1)} %broadcast_select_fusion.2), channel_id=1, source_target_pairs={{0,4},{4,0},{1,5},{5,1},{2,6},{6,2},{3,7},{7,3},{8,12},{12,8},{9,1... | collective-permute-start | bytes 3538952 | tf_op jit(solution)/shard_map/ppermute | solution.py:82
  127.1 2.5 %collective-permute-done = f32[294912]{0:T(1024)S(1)} collective-permute-done((f32[294912]{0:T(1024)S(1)}, f32[294912]{0:T(1024)S(1)}, u32[]{:S(2)}, u32[]{:S(2)}) %collective-permute-start) | collective-permute-done | bytes 1179680 | tf_op jit(solution)/shard_map/ppermute | solution.py:82
  129.8 24.1 %all_to_all.27 = f32[16,1,18432]{2,1,0:T(1,128)S(1)} all-to-all(f32[16,1,18432]{2,1,0:T(1,128)S(1)} %bitcast.234), channel_id=1, replica_groups=mesh['chip'=16,'core'=2,'chan'=4] {'chip'}, dimensions={0} | all-to-all | bytes 2359296 | tf_op jit(solution)/shard_map/all_to_all | solution.py:83
  153.9 0.7 reduce_sum.18
  154.6 0.6 broadcast_in_dim.164
  155.2 19.8 %all_to_all.26 = f32[16,1,18432]{2,1,0:T(1,128)S(1)} all-to-all(f32[16,1,18432]{2,1,0:T(1,128)S(1)} %broadcast_in_dim.164), channel_id=1, replica_groups=mesh['chip'=16,'core'=2,'chan'=4] {'chip'}, dimensions={0} | all-to-all | bytes 2359296 | tf_op jit(solution)/shard_map/all_to_all | solution.py:85
  175.1 3.0 %collective-permute-start.1 = (f32[294912]{0:T(1024)S(1)}, f32[294912]{0:T(1024)}, u32[]{:S(2)}, u32[]{:S(2)}) collective-permute-start(f32[294912]{0:T(1024)S(1)} %bitcast.232), channel_id=1, source_target_pairs={{0,4},{4,0},{1,5},{5,1},{2,6},{6,2},{3,7},{7,3},{8,12},{12,8},{9,1... | collective-permute-start | bytes 3538952 | tf_op jit(solution)/shard_map/ppermute | solution.py:86
  178.1 1.0 slice.239
  179.1 0.8 fusion.52
  179.9 0.7 collective-permute-done.1
  180.6 2.4 %broadcast_select_fusion = (f32[294912]{0:T(1024)}, f32[294912]{0:T(1024)S(1)}) fusion(f32[294912]{0:T(1024)} %collective-permute-done.1, f32[294912]{0:T(1024)S(1)} %bitcast.233, pred[]{:T(512)S(6)} %eq.34), kind=kLoop, calls=%fused_computation.60 | loop fusion | flops 589824 | bytes 4718593 | tf_op jit(solution)/shard_map/jit(_where)/select_n | solution.py:88
  183.1 2.4 %reshape.61 = f32[9,64,512]{2,1,0:T(8,128)} reshape(f32[294912]{0:T(1024)} %get-tuple-element.239) | data formatting | bytes 2359296 | tf_op jit(solution)/shard_map/reshape | solution.py:89
  185.5 1.3 reshape.60
  (119 shorter events, 8.3 us)
Async XLA Ops:
  7.2 6.5 %copy-start = (bf16[9,64,512]{2,1,0:T(8,128)(2,1)S(1)}, bf16[9,64,512]{2,1,0:T(8,128)(2,1)}, u32[]{:S(2)}) copy-start(bf16[9,64,512]{2,1,0:T(8,128)(2,1)} %param.12) | copy-start | bytes 1769476
  7.2 6.2 %copy-start.3 = (bf16[2,64,512]{2,1,0:T(8,128)(2,1)S(1)}, bf16[2,64,512]{2,1,0:T(8,128)(2,1)}, u32[]{:S(2)}) copy-start(bf16[2,64,512]{2,1,0:T(8,128)(2,1)} %param.13) | copy-start | bytes 393220
  7.2 41.9 %reduce-scatter.2.cloned.1.call-start = ((), (), s32[]{:S(2)}) async-start(), calls=%async_computation.5 | async-start | bytes 2621440 | tf_op jit(solution)/shard_map/reduce_scatter | solution.py:107
  16.1 0.7 copy-start.10
  16.1 1.1 copy-start.9
  18.4 1.1 copy-start.8
  19.5 2.1 %copy-start.2 = (bf16[2,9,256,512]{2,3,1,0:T(8,128)(2,1)}, bf16[2,9,256,512]{2,3,1,0:T(8,128)(2,1)S(1)}, u32[]{:S(2)}) copy-start(bf16[2,9,256,512]{2,3,1,0:T(8,128)(2,1)S(1)} %fusion.51) | copy-start | bytes 14155780
  51.8 45.8 %copy-start.4 = (f32[2,128,512]{2,1,0:T(8,128)}, f32[2,128,512]{2,1,0:T(8,128)S(1)}, u32[]{:S(2)}) copy-start(f32[2,128,512]{2,1,0:T(8,128)S(1)} %get-tuple-element.135) | copy-start | bytes 1572868
  80.6 15.5 %all-to-all-start.1 = ((f32[32,8,512]{2,1,0:T(8,128)}), f32[32,8,512]{2,1,0:T(8,128)S(1)}, u32[]{:S(2)}, u32[]{:S(2)}) async-start(f32[32,8,512]{2,1,0:T(8,128)} %select_maximum_fusion), calls=%async_computation.2 | async-start | bytes 1048576 | tf_op jit(solution)/shard_map/all_to_all | solution.py:50
  84.5 30.7 %all-gather.2.cloned.1.call-start = ((), (), s32[]{:S(2)}) async-start(), calls=%async_computation.6 | async-start | bytes 1310720 | tf_op jit(solution)/shard_map/all_gather | solution.py:135
  84.7 12.7 %copy-start.11 = (pred[2]{0:T(512)(128)(4,1)S(1)}, pred[2]{0:T(512)(128)(4,1)}, u32[]{:S(2)}) copy-start(pred[2]{0:T(512)(128)(4,1)} %constant.169.clone.1) | copy-start | bytes 10
  96.2 1.4 copy-start.6
  115.2 1.7 copy-start.1
  124.3 5.3 %collective-permute-start = (f32[294912]{0:T(1024)S(1)}, f32[294912]{0:T(1024)S(1)}, u32[]{:S(2)}, u32[]{:S(2)}) collective-permute-start(f32[294912]{0:T(1024)S(1)} %broadcast_select_fusion.2), channel_id=1, source_target_pairs={{0,4},{4,0},{1,5},{5,1},{2,6},{6,2},{3,7},{7,3},{8,12},{12,8},{9,1... | collective-permute-start | bytes 3538952 | tf_op jit(solution)/shard_map/ppermute | solution.py:82
  154.6 23.4 %copy-start.7 = (f32[32,4,512]{2,1,0:T(4,128)S(1)}, f32[32,4,512]{2,1,0:T(4,128)}, u32[]{:S(2)}) copy-start(f32[32,4,512]{2,1,0:T(4,128)} %copy-done.6) | copy-start | bytes 786436
  155.2 23.9 %copy-start.5 = (f32[2,128,512]{2,1,0:T(8,128)S(1)}, f32[2,128,512]{2,1,0:T(8,128)}, u32[]{:S(2)}) copy-start(f32[2,128,512]{2,1,0:T(8,128)} %copy-done.4) | copy-start | bytes 1572868
  175.1 5.6 %collective-permute-start.1 = (f32[294912]{0:T(1024)S(1)}, f32[294912]{0:T(1024)}, u32[]{:S(2)}, u32[]{:S(2)}) collective-permute-start(f32[294912]{0:T(1024)S(1)} %bitcast.232), channel_id=1, source_target_pairs={{0,4},{4,0},{1,5},{5,1},{2,6},{6,2},{3,7},{7,3},{8,12},{12,8},{9,1... | collective-permute-start | bytes 3538952 | tf_op jit(solution)/shard_map/ppermute | solution.py:86
Sparse Core Ops, SparseCore 0:
  16.2 32.8 reduce-scatter.1
  97.5 17.6 all-gather.1

commit v4 on v3

--- a/solution.py
+++ b/solution.py
@@ -33,22 +33,19 @@
     return value
 
 
-def block_scans(factor, forward_value, backward_value, axis):
+def block_scan(factor, value, axis, reverse):
     count = lax.axis_size(axis)
-    rows, cells = forward_value.shape
+    rows, cells = value.shape
     chunk = rows // count
     factor_row = jnp.pad(factor.reshape(count, chunk), ((0, 0), (0, cells - chunk)))[:, None, :]
-    packed = jnp.concatenate(
-        [forward_value.reshape(count, chunk, cells), backward_value.reshape(count, chunk, cells), factor_row], axis=1
-    )
+    packed = jnp.concatenate([value.reshape(count, chunk, cells), factor_row], axis=1)
     gathered = lax.all_to_all(packed, axis, 0, 0, tiled=True)
-    block_factor = gathered[:, 2 * chunk, :chunk][:, :, None]
-    forward_total = scan_chunks(block_factor, gathered[:, :chunk], False)
-    backward_total = scan_chunks(block_factor, gathered[:, chunk : 2 * chunk], True)
-    entering = jnp.pad(forward_total[:-1], ((1, 0), (0, 0), (0, 0)))
-    arriving = jnp.pad(backward_total[1:], ((0, 1), (0, 0), (0, 0)))
-    returned = lax.all_to_all(jnp.concatenate([entering, arriving], axis=1), axis, 0, 0, tiled=True)
-    return returned[:, :chunk].reshape(rows, cells), returned[:, chunk:].reshape(rows, cells)
+    total = scan_chunks(gathered[:, chunk, :chunk][:, :, None], gathered[:, :chunk], reverse)
+    if reverse:
+        shifted = jnp.pad(total[1:], ((0, 1), (0, 0), (0, 0)))
+    else:
+        shifted = jnp.pad(total[:-1], ((1, 0), (0, 0), (0, 0)))
+    return lax.all_to_all(shifted, axis, 0, 0, tiled=True).reshape(rows, cells)
 
 
 def shift_cells(source, row_shift, col_shift, grid_width):
@@ -103,6 +100,7 @@
 
     local_end, local_states = lax.scan(advance, blank_state, (decay, drives))
     decay_total = jnp.prod(decay, axis=0)
+    entering = block_scan(decay_total, local_end, FRAME_AXES, False)
     cot_stack = stencil_stack(cotangent, W, -1)
     injected = lax.psum_scatter(
         jnp.einsum("kup,fkus->pfs", kernel_c, cot_stack, preferred_element_type=jnp.float32),
@@ -110,6 +108,7 @@
         scatter_dimension=0,
         tiled=True,
     )
+    entering, injected = lax.optimization_barrier((entering, injected))
     injected = jnp.moveaxis(injected, 1, 0)
 
     def retreat(carried, frame_pair):
@@ -119,7 +118,7 @@
 
     message, local_adjoint = lax.scan(retreat, blank_state, (decay, injected), reverse=True)
 
-    entering, arriving = block_scans(decay_total, local_end, message, FRAME_AXES)
+    arriving = block_scan(decay_total, message, FRAME_AXES, True)
     cumulative = jnp.cumprod(decay, axis=0)
     states = local_states + cumulative[:, :, None] * entering[None]
     previous = jnp.concatenate([entering[None], states[:-1]], axis=0)

time: 194 us -> 176 us (0.907)
  waiting for transfers between devices: 54.1 us -> 32.4 us
  blocking collectives: 68.3 us -> 61.5 us
  other arithmetic: 22.1 us -> 27 us
  starting transfers between devices: 9.97 us -> 14.4 us
  matrix products: 10.5 us -> 12.9 us
    reduce_scatter x1, waiting for transfers between devices: 26.7 us -> 0.02 us  [body(): lax.psum_scatter(jnp.einsum('kup,fkus->pfs', kernel_c, cot_stack, preferr...]
    all_to_all x1 -> x3, waiting for transfers between devices: 11.3 us -> 28.1 us  [the longest x2 17.5 us: block_scan(): return lax.all_to_all(shifted, axis, 0, 0, tiled=True).reshape(rows, cells)]
    all_gather x1, waiting for transfers between devices: 12.8 us -> 0.02 us  [body(): lax.all_gather(states_bf, 'chan', axis=1, tiled=True)]
    all_to_all x1 -> x3, starting transfers between devices: 3.92 us -> 11.2 us  [the longest x2 7.5 us: block_scan(): return lax.all_to_all(shifted, axis, 0, 0, tiled=True).reshape(rows, cells)]
    unnamed x26, other arithmetic: 12.7 us -> 19.1 us
    all_to_all x1, blocking collectives: 24.5 us -> 20.9 us  [block_scan(): gathered = lax.all_to_all(packed, axis, 0, 0, tiled=True)]
    all_to_all x1, blocking collectives: 24.1 us -> 20.6 us  [pair_then_chip_sum(): pieces = lax.all_to_all(pair_sum, 'chip', 0, 0, tiled=True)]
    ppermute x1, starting transfers between devices: 2.83 us -> 0.27 us  [pair_then_chip_sum(): lax.ppermute(sent, 'core', swap)]
  transfers between devices with their start and end apart: 5 -> 7, of which waited for: 5 -> 5; matrix products, arithmetic and copies ran while one was open for 6% -> 14% of each run, Pallas kernels for 0% -> 0%
where the time goes in v4:
time: 176 us; the launch traced here: 175 us
  blocking collectives  61.5 us (35%)
  waiting for transfers between devices  32.4 us (18%)
  other arithmetic  27 us (15%)
  between operations  14.7 us (8%)
  starting transfers between devices  14.4 us (8%)
  matrix products  12.9 us (7%)
  local copies, waits for them, and re-layouts  12 us (7%)
    all_to_all x1, blocking collectives, block_scan(): gathered = lax.all_to_all(packed, axis, 0, 0, tiled=True)  20.9 us
    all_to_all x1, blocking collectives, pair_then_chip_sum(): pieces = lax.all_to_all(pair_sum, 'chip', 0, 0, tiled=True)  20.6 us
    all_to_all x1, blocking collectives, pair_then_chip_sum(): lax.all_to_all(jnp.broadcast_to(reduced, pieces.shape), 'chip', 0, 0, til...  20 us
    unnamed x26, other arithmetic  19.1 us
    all_to_all x2, waiting for transfers between devices, block_scan(): return lax.all_to_all(shifted, axis, 0, 0, tiled=True).reshape(rows, cells)  17.5 us
    all_to_all x1, waiting for transfers between devices, block_scan(): gathered = lax.all_to_all(packed, axis, 0, 0, tiled=True)  10.6 us
    all_to_all x2, starting transfers between devices, block_scan(): return lax.all_to_all(shifted, axis, 0, 0, tiled=True).reshape(rows, cells)  7.5 us
    dot_general x1, matrix products, body(): jnp.einsum('fps,fkcs->kpc', adjoint_bf, input_stack, preferred_element_ty...  3.81 us
  transfers between devices with their start and end apart: 7, of which 5 were waited for; matrix products, arithmetic and copies ran while one was open for 14% of the time, Pallas kernels for 0%

profile of v4, /device:TPU:1, one launch (start us, length us, event | category | flops | bytes accessed | tf_op | source)
XLA Modules:
  0.0 175.2 jit_solution(10204948672121405517)
XLA Ops:
  7.3 1.1 fusion.60
  8.3 1.0 fusion.63
  9.4 1.0 fusion.66
  10.4 1.0 fusion.69
  11.4 0.9 bitcast_dynamic-update-slice_fusion.4
  12.3 1.0 fusion.72
  13.7 2.4 %convolution_bitcast_fusion = f32[512,2,512]{0,2,1:T(8,128)} fusion(bf16[2,9,64,512]{3,2,1,0:T(8,128)(2,1)S(1)} %fusion.81, bf16[9,64,512]{2,1,0:T(8,128)(2,1)S(1)} %copy-done), kind=kOutput, calls=%fused_computation.20 | convolution fusion | flops 603979776 | bytes 3866624 | tf_op jit(solution)/shard_map/kup,fkus->pfs/dot_general | solution.py:106
  16.1 1.0 copy-done.9
  17.3 0.9 fusion.30
  18.3 1.0 fusion.33
  19.2 1.0 fusion.36
  20.2 1.0 fusion.39
  21.2 1.0 bitcast_dynamic-update-slice_fusion.3
  22.2 1.0 fusion.42
  23.2 1.0 fusion.45
  24.1 1.0 fusion.48
  25.1 1.0 fusion.51
  26.0 3.8 %convolution_bitcast_fusion.2 = f32[2,128,512]{1,2,0:T(8,128)S(1)} fusion(bf16[2,9,256,512]{2,3,1,0:T(8,128)(2,1)} %fusion.51, bf16[9,128,256]{2,1,0:T(8,128)(2,1)S(1)} %copy-done.8), kind=kOutput, calls=%fused_computation.22 | convolution fusion | flops 603979776 | bytes 5832704 | tf_op jit(solution)/shard_map/kpc,fkcs->fps/dot_general | solution.py:94
  29.9 0.6 while.30
  30.9 20.9 %all_to_all.36 = f32[32,5,512]{2,1,0:T(8,128)S(1)} all-to-all(f32[32,5,512]{2,1,0:T(8,128)S(1)} %pad_maximum_fusion.1), channel_id=1, replica_groups=mesh['chip'=16,'core'=2,'chan'=4] {'chip','core'}, dimensions={0} | all-to-all | bytes 655360 | tf_op jit(solution)/shard_map/all_to_all | solution.py:42
  53.5 0.7 pad.131
  54.3 3.7 %all-to-all-start.1 = ((f32[32,4,512]{2,1,0:T(4,128)}), f32[32,4,512]{2,1,0:T(4,128)S(1)}, u32[]{:S(2)}, u32[]{:S(2)}) async-start(f32[32,4,512]{2,1,0:T(4,128)} %pad.131), calls=%async_computation.1 | async-start | bytes 524288 | tf_op jit(solution)/shard_map/all_to_all | solution.py:48
  58.0 8.9 %all-to-all-done.1 = f32[32,4,512]{2,1,0:T(4,128)S(1)} async-done(((f32[32,4,512]{2,1,0:T(4,128)}), f32[32,4,512]{2,1,0:T(4,128)S(1)}, u32[]{:S(2)}, u32[]{:S(2)}) %all-to-all-start.1) | async-done | bytes 262176 | tf_op jit(solution)/shard_map/all_to_all | solution.py:48
  67.1 2.6 %while.31 = (s32[]{:T(128)}, f32[128,512]{1,0:T(8,128)S(1)}, f32[2,128,512]{2,1,0:T(8,128)S(1)}, f32[2,128]{1,0:T(2,128)S(1)}, f32[2,128,512]{1,2,0:T(8,128)}, /*index=5*/s32[]{:T(128)}, s32[]{:T(128)}) while((s32[]{:T(128)}, f32[128,512]{1,0:T(8,128)S(1)}, f32[2,128,512]{2,1,0:T(8,128)S(1)}, f32[2,128]{1,0:T(2,128)S(1)}, ...), condition=%wide.region_5.6_spmd.clone, body=%wide.region_4.5_spmd.clone.sunk | while | flops 327684 | bytes 2623088 | solution.py:119
  67.1 1.0 constant_dynamic-slice_fusion.7
  68.4 1.0 constant_dynamic-slice_fusion.7
  69.8 0.9 pad_maximum_fusion
  70.7 3.7 %all-to-all-start.2 = ((f32[32,5,512]{2,1,0:T(8,128)}), f32[32,5,512]{2,1,0:T(8,128)S(1)}, u32[]{:S(2)}, u32[]{:S(2)}) async-start(f32[32,5,512]{2,1,0:T(8,128)} %pad_maximum_fusion), calls=%async_computation.3 | async-start | bytes 1048576 | tf_op jit(solution)/shard_map/all_to_all | solution.py:42
  74.5 1.0 fusion.92
  75.5 10.6 %all-to-all-done.2 = f32[32,5,512]{2,1,0:T(8,128)S(1)} async-done(((f32[32,5,512]{2,1,0:T(8,128)}), f32[32,5,512]{2,1,0:T(8,128)S(1)}, u32[]{:S(2)}, u32[]{:S(2)}) %all-to-all-start.2) | async-done | bytes 327712 | tf_op jit(solution)/shard_map/all_to_all | solution.py:42
  87.9 0.7 pad.142
  88.6 3.8 %all-to-all-start.3 = ((f32[32,4,512]{2,1,0:T(4,128)}), f32[32,4,512]{2,1,0:T(4,128)S(1)}, u32[]{:S(2)}, u32[]{:S(2)}) async-start(f32[32,4,512]{2,1,0:T(4,128)} %pad.142), calls=%async_computation.4 | async-start | bytes 524288 | tf_op jit(solution)/shard_map/all_to_all | solution.py:48
  92.6 8.6 %all-to-all-done.3 = f32[32,4,512]{2,1,0:T(4,128)S(1)} async-done(((f32[32,4,512]{2,1,0:T(4,128)}), f32[32,4,512]{2,1,0:T(4,128)S(1)}, u32[]{:S(2)}, u32[]{:S(2)}) %all-to-all-start.3) | async-done | bytes 262176 | tf_op jit(solution)/shard_map/all_to_all | solution.py:48
  101.3 3.8 %convolution_bitcast_fusion.1 = f32[9,128,256]{1,2,0:T(8,128)S(1)} fusion(bf16[2,9,256,512]{2,3,1,0:T(8,128)(2,1)} %fusion.51, f32[2,128,512]{2,1,0:T(8,128)S(1)} %get-tuple-element.139, f32[128,512]{1,0:T(8,128)S(1)} %mul.235, f32[2,128]{1,0:T(2,128)S(1)} %broadcast_select_fusion.3), kind=kOutput, calls=%fused_computation.21 | convolution fusion | flops 604372992 | bytes 6685696 | tf_op jit(solution)/shard_map/fps,fkcs->kpc/dot_general | solution.py:131
  105.4 0.6 copy.236
  106.1 1.7 fusion.4
  109.7 0.5 fusion.16
  111.8 2.9 %fusion.82 = f32[9,512,64,1]{1,2,3,0:T(8,128)S(1)} fusion(bf16[2,9,512,512]{3,2,0,1:T(8,128)(2,1)S(1)} %fusion.25, bf16[2,64,512]{2,1,0:T(8,128)(2,1)S(1)} %copy-done.2), kind=kOutput, calls=%fused_computation.142 | convolution fusion | flops 603979776 | bytes 10747904 | tf_op jit(solution)/shard_map/fus,fkps->kup/dot_general | solution.py:135
  115.5 2.7 %collective-permute-done = f32[294912]{0:T(1024)S(1)} collective-permute-done((f32[294912]{0:T(1024)S(1)}, f32[294912]{0:T(1024)S(1)}, u32[]{:S(2)}, u32[]{:S(2)}) %collective-permute-start) | collective-permute-done | bytes 1179680 | tf_op jit(solution)/shard_map/ppermute | solution.py:79
  118.3 20.6 %all_to_all.37 = f32[16,1,18432]{2,1,0:T(1,128)S(1)} all-to-all(f32[16,1,18432]{2,1,0:T(1,128)S(1)} %bitcast.235), channel_id=1, replica_groups=mesh['chip'=16,'core'=2,'chan'=4] {'chip'}, dimensions={0} | all-to-all | bytes 2359296 | tf_op jit(solution)/shard_map/all_to_all | solution.py:80
  139.0 0.7 reduce_sum.18
  139.7 0.6 broadcast_in_dim.169
  140.4 20.0 %all_to_all.35 = f32[16,1,18432]{2,1,0:T(1,128)S(1)} all-to-all(f32[16,1,18432]{2,1,0:T(1,128)S(1)} %broadcast_in_dim.169), channel_id=1, replica_groups=mesh['chip'=16,'core'=2,'chan'=4] {'chip'}, dimensions={0} | all-to-all | bytes 2359296 | tf_op jit(solution)/shard_map/all_to_all | solution.py:82
  160.3 2.8 %collective-permute-start.1 = (f32[294912]{0:T(1024)S(1)}, f32[294912]{0:T(1024)S(1)}, u32[]{:S(2)}, u32[]{:S(2)}) collective-permute-start(f32[294912]{0:T(1024)S(1)} %bitcast.233), channel_id=1, source_target_pairs={{0,4},{4,0},{1,5},{5,1},{2,6},{6,2},{3,7},{7,3},{8,12},{12,8},{9,1... | collective-permute-start | bytes 3538952 | tf_op jit(solution)/shard_map/ppermute | solution.py:83
  163.2 0.8 fusion.52
  164.0 1.6 collective-permute-done.1
  165.8 1.3 reshape.66
  167.1 1.2 reshape.67
  (131 shorter events, 10.8 us)
Async XLA Ops:
  7.2 6.5 %copy-start = (bf16[9,64,512]{2,1,0:T(8,128)(2,1)S(1)}, bf16[9,64,512]{2,1,0:T(8,128)(2,1)}, u32[]{:S(2)}) copy-start(bf16[9,64,512]{2,1,0:T(8,128)(2,1)} %param.12) | copy-start | bytes 1769476
  7.2 6.2 %copy-start.2 = (bf16[2,64,512]{2,1,0:T(8,128)(2,1)S(1)}, bf16[2,64,512]{2,1,0:T(8,128)(2,1)}, u32[]{:S(2)}) copy-start(bf16[2,64,512]{2,1,0:T(8,128)(2,1)} %param.13) | copy-start | bytes 393220
  7.2 59.8 %reduce-scatter.2.cloned.1.call-start = ((), (), s32[]{:S(2)}) async-start(), calls=%async_computation.7 | async-start | bytes 2621440 | tf_op jit(solution)/shard_map/reduce_scatter | solution.py:105
  16.1 1.0 copy-start.9
  23.2 2.9 %copy-start.8 = (bf16[9,128,256]{2,1,0:T(8,128)(2,1)S(1)}, bf16[9,128,256]{2,1,0:T(8,128)(2,1)}, u32[]{:S(2)}) copy-start(bf16[9,128,256]{2,1,0:T(8,128)(2,1)} %param.11) | copy-start | bytes 1769476
  26.0 3.8 %copy-start.10 = (f32[2,128]{1,0:T(2,128)S(1)}, f32[2,128]{1,0:T(2,128)}, u32[]{:S(2)}) copy-start(f32[2,128]{1,0:T(2,128)} %param.10) | copy-start | bytes 3076
  54.3 12.6 %all-to-all-start.1 = ((f32[32,4,512]{2,1,0:T(4,128)}), f32[32,4,512]{2,1,0:T(4,128)S(1)}, u32[]{:S(2)}, u32[]{:S(2)}) async-start(f32[32,4,512]{2,1,0:T(4,128)} %pad.131), calls=%async_computation.1 | async-start | bytes 524288 | tf_op jit(solution)/shard_map/all_to_all | solution.py:48
  67.0 7.5 %copy-start.5 = (f32[128,512]{1,0:T(8,128)}, f32[128,512]{1,0:T(8,128)S(1)}, u32[]{:S(2)}) copy-start(f32[128,512]{1,0:T(8,128)S(1)} %reshape.61) | copy-start | bytes 786436
  69.7 31.6 %copy-start.3 = (f32[2,128,512]{2,1,0:T(8,128)}, f32[2,128,512]{2,1,0:T(8,128)S(1)}, u32[]{:S(2)}) copy-start(f32[2,128,512]{2,1,0:T(8,128)S(1)} %get-tuple-element.139) | copy-start | bytes 1572868
  70.7 15.4 %all-to-all-start.2 = ((f32[32,5,512]{2,1,0:T(8,128)}), f32[32,5,512]{2,1,0:T(8,128)S(1)}, u32[]{:S(2)}, u32[]{:S(2)}) async-start(f32[32,5,512]{2,1,0:T(8,128)} %pad_maximum_fusion), calls=%async_computation.3 | async-start | bytes 1048576 | tf_op jit(solution)/shard_map/all_to_all | solution.py:42
  74.4 31.7 %all-gather.2.cloned.1.call-start = ((), (), s32[]{:S(2)}) async-start(), calls=%async_computation.8 | async-start | bytes 1310720 | tf_op jit(solution)/shard_map/all_gather | solution.py:134
  87.5 5.0 %copy-start.11 = (pred[2]{0:T(512)(128)(4,1)S(1)}, pred[2]{0:T(512)(128)(4,1)}, u32[]{:S(2)}) copy-start(pred[2]{0:T(512)(128)(4,1)} %constant.170.clone.1) | copy-start | bytes 10
  88.6 12.6 %all-to-all-start.3 = ((f32[32,4,512]{2,1,0:T(4,128)}), f32[32,4,512]{2,1,0:T(4,128)S(1)}, u32[]{:S(2)}, u32[]{:S(2)}) async-start(f32[32,4,512]{2,1,0:T(4,128)} %pad.142), calls=%async_computation.4 | async-start | bytes 524288 | tf_op jit(solution)/shard_map/all_to_all | solution.py:48
  106.1 1.7 copy-start.1
  115.2 2.9 %collective-permute-start = (f32[294912]{0:T(1024)S(1)}, f32[294912]{0:T(1024)S(1)}, u32[]{:S(2)}, u32[]{:S(2)}) collective-permute-start(f32[294912]{0:T(1024)S(1)} %broadcast_select_fusion.2), channel_id=1, source_target_pairs={{0,4},{4,0},{1,5},{5,1},{2,6},{6,2},{3,7},{7,3},{8,12},{12,8},{9,1... | collective-permute-start | bytes 3538952 | tf_op jit(solution)/shard_map/ppermute | solution.py:79
  139.7 23.4 %copy-start.7 = (f32[2,128,512]{2,1,0:T(8,128)S(1)}, f32[2,128,512]{2,1,0:T(8,128)}, u32[]{:S(2)}) copy-start(f32[2,128,512]{2,1,0:T(8,128)} %get-tuple-element.262) | copy-start | bytes 1572868
  140.4 22.8 %copy-start.4 = (f32[2,128,512]{2,1,0:T(8,128)S(1)}, f32[2,128,512]{2,1,0:T(8,128)}, u32[]{:S(2)}) copy-start(f32[2,128,512]{2,1,0:T(8,128)} %copy-done.3) | copy-start | bytes 1572868
  140.4 22.8 %copy-start.6 = (f32[128,512]{1,0:T(8,128)S(1)}, f32[128,512]{1,0:T(8,128)}, u32[]{:S(2)}) copy-start(f32[128,512]{1,0:T(8,128)} %copy-done.5) | copy-start | bytes 786436
  160.3 5.3 %collective-permute-start.1 = (f32[294912]{0:T(1024)S(1)}, f32[294912]{0:T(1024)S(1)}, u32[]{:S(2)}, u32[]{:S(2)}) collective-permute-start(f32[294912]{0:T(1024)S(1)} %bitcast.233), channel_id=1, source_target_pairs={{0,4},{4,0},{1,5},{5,1},{2,6},{6,2},{3,7},{7,3},{8,12},{12,8},{9,1... | collective-permute-start | bytes 3538952 | tf_op jit(solution)/shard_map/ppermute | solution.py:83
Sparse Core Ops, SparseCore 0:
  16.2 32.8 reduce-scatter.1
  76.9 23.4 all-gather.1

commit v5 on v4

--- a/solution.py
+++ b/solution.py
@@ -33,19 +33,19 @@
     return value
 
 
-def block_scan(factor, value, axis, reverse):
-    count = lax.axis_size(axis)
+def pack_chunks(factor, value, count):
     rows, cells = value.shape
     chunk = rows // count
     factor_row = jnp.pad(factor.reshape(count, chunk), ((0, 0), (0, cells - chunk)))[:, None, :]
-    packed = jnp.concatenate([value.reshape(count, chunk, cells), factor_row], axis=1)
-    gathered = lax.all_to_all(packed, axis, 0, 0, tiled=True)
+    return jnp.concatenate([value.reshape(count, chunk, cells), factor_row], axis=1)
+
+
+def scan_owned(gathered, reverse):
+    chunk = gathered.shape[1] - 1
     total = scan_chunks(gathered[:, chunk, :chunk][:, :, None], gathered[:, :chunk], reverse)
     if reverse:
-        shifted = jnp.pad(total[1:], ((0, 1), (0, 0), (0, 0)))
-    else:
-        shifted = jnp.pad(total[:-1], ((1, 0), (0, 0), (0, 0)))
-    return lax.all_to_all(shifted, axis, 0, 0, tiled=True).reshape(rows, cells)
+        return jnp.pad(total[1:], ((0, 1), (0, 0), (0, 0)))
+    return jnp.pad(total[:-1], ((1, 0), (0, 0), (0, 0)))
 
 
 def shift_cells(source, row_shift, col_shift, grid_width):
@@ -100,7 +100,10 @@
 
     local_end, local_states = lax.scan(advance, blank_state, (decay, drives))
     decay_total = jnp.prod(decay, axis=0)
-    entering = block_scan(decay_total, local_end, FRAME_AXES, False)
+    blocks = lax.axis_size(FRAME_AXES)
+    rows = local_end.shape[0]
+    chunk = rows // blocks
+    entering_owned = scan_owned(lax.all_to_all(pack_chunks(decay_total, local_end, blocks), FRAME_AXES, 0, 0, tiled=True), False)
     cot_stack = stencil_stack(cotangent, W, -1)
     injected = lax.psum_scatter(
         jnp.einsum("kup,fkus->pfs", kernel_c, cot_stack, preferred_element_type=jnp.float32),
@@ -108,7 +111,7 @@
         scatter_dimension=0,
         tiled=True,
     )
-    entering, injected = lax.optimization_barrier((entering, injected))
+    entering_owned, injected = lax.optimization_barrier((entering_owned, injected))
     injected = jnp.moveaxis(injected, 1, 0)
 
     def retreat(carried, frame_pair):
@@ -118,7 +121,12 @@
 
     message, local_adjoint = lax.scan(retreat, blank_state, (decay, injected), reverse=True)
 
-    arriving = block_scan(decay_total, message, FRAME_AXES, True)
+    exchanged = lax.all_to_all(
+        jnp.concatenate([entering_owned, pack_chunks(decay_total, message, blocks)], axis=1), FRAME_AXES, 0, 0, tiled=True
+    )
+    entering = exchanged[:, :chunk].reshape(rows, cell_count)
+    arriving_owned = scan_owned(exchanged[:, chunk:], True)
+    arriving = lax.all_to_all(arriving_owned, FRAME_AXES, 0, 0, tiled=True).reshape(rows, cell_count)
     cumulative = jnp.cumprod(decay, axis=0)
     states = local_states + cumulative[:, :, None] * entering[None]
     previous = jnp.concatenate([entering[None], states[:-1]], axis=0)

time: 176 us -> 181 us (1.028)
  blocking collectives: 61.5 us -> 43.9 us
  starting transfers between devices: 14.4 us -> 23 us
  waiting for transfers between devices: 32.4 us -> 40.3 us
  other arithmetic: 27 us -> 31.4 us
    all_to_all x1 -> x0, blocking collectives: 20.9 us -> none  [block_scan(): gathered = lax.all_to_all(packed, axis, 0, 0, tiled=True)]
    all_to_all x3, waiting for transfers between devices: 28.1 us -> 37.1 us  [the longest x1 16.7 us: body(): lax.all_to_all(jnp.concatenate([entering_owned, pack_chunks(decay_total,...]
    all_to_all x3, starting transfers between devices: 11.2 us -> 17.1 us  [the longest x1 9.44 us: body(): lax.all_to_all(pack_chunks(decay_total, local_end, blocks), FRAME_AXES, 0...]
    all_to_all x1, blocking collectives: 20.6 us -> 24.1 us  [pair_then_chip_sum(): pieces = lax.all_to_all(pair_sum, 'chip', 0, 0, tiled=True)]
    ppermute x1, starting transfers between devices: 0.27 us -> 2.83 us  [pair_then_chip_sum(): lax.ppermute(sent, 'core', swap)]
    select_n x1, other arithmetic: 0.15 us -> 2.44 us  [pair_then_chip_sum(): second_total = jnp.where(core == 0, partner, total)]
where the time goes in v5:
time: 181 us; the launch traced here: 180 us
  blocking collectives  43.9 us (24%)
  waiting for transfers between devices  40.3 us (22%)
  other arithmetic  31.4 us (17%)
  starting transfers between devices  23 us (13%)
  between operations  14.7 us (8%)
  local copies, waits for them, and re-layouts  13.3 us (7%)
  matrix products  13 us (7%)
    all_to_all x1, blocking collectives, pair_then_chip_sum(): pieces = lax.all_to_all(pair_sum, 'chip', 0, 0, tiled=True)  24.1 us
    all_to_all x1, blocking collectives, pair_then_chip_sum(): lax.all_to_all(jnp.broadcast_to(reduced, pieces.shape), 'chip', 0, 0, til...  19.8 us
    unnamed x26, other arithmetic  19.2 us
    all_to_all x1, waiting for transfers between devices, body(): lax.all_to_all(jnp.concatenate([entering_owned, pack_chunks(decay_total,...  16.7 us
    all_to_all x1, waiting for transfers between devices, body(): lax.all_to_all(pack_chunks(decay_total, local_end, blocks), FRAME_AXES, 0...  11.6 us
    all_to_all x1, starting transfers between devices, body(): lax.all_to_all(pack_chunks(decay_total, local_end, blocks), FRAME_AXES, 0...  9.44 us
    all_to_all x1, waiting for transfers between devices, body(): lax.all_to_all(arriving_owned, FRAME_AXES, 0, 0, tiled=True)  8.81 us
    all_to_all x1, starting transfers between devices, body(): lax.all_to_all(arriving_owned, FRAME_AXES, 0, 0, tiled=True)  3.93 us
  transfers between devices with their start and end apart: 7, of which 5 were waited for; matrix products, arithmetic and copies ran while one was open for 14% of the time, Pallas kernels for 0%

profile of v5, /device:TPU:1, one launch (start us, length us, event | category | flops | bytes accessed | tf_op | source)
XLA Modules:
  0.0 179.8 jit_solution(561136383318113725)
XLA Ops:
  7.3 1.1 fusion.60
  8.3 1.0 fusion.63
  9.4 1.0 fusion.66
  10.4 1.0 fusion.69
  11.4 0.9 bitcast_dynamic-update-slice_fusion.4
  12.3 1.0 fusion.72
  13.7 2.4 %convolution_bitcast_fusion = f32[512,2,512]{0,2,1:T(8,128)} fusion(bf16[2,9,64,512]{3,2,1,0:T(8,128)(2,1)S(1)} %fusion.81, bf16[9,64,512]{2,1,0:T(8,128)(2,1)S(1)} %copy-done), kind=kOutput, calls=%fused_computation.20 | convolution fusion | flops 603979776 | bytes 3866624 | tf_op jit(solution)/shard_map/kup,fkus->pfs/dot_general | solution.py:109
  16.1 1.0 copy-done.9
  17.3 1.0 fusion.30
  18.3 1.0 fusion.33
  19.3 1.0 fusion.36
  20.2 1.0 fusion.39
  21.2 1.0 bitcast_dynamic-update-slice_fusion.3
  22.2 1.0 fusion.42
  23.2 1.0 fusion.45
  24.2 1.0 fusion.48
  25.2 1.0 fusion.51
  26.1 3.8 %convolution_bitcast_fusion.2 = f32[2,128,512]{1,2,0:T(8,128)S(1)} fusion(bf16[2,9,256,512]{2,3,1,0:T(8,128)(2,1)} %fusion.51, bf16[9,128,256]{2,1,0:T(8,128)(2,1)S(1)} %copy-done.8), kind=kOutput, calls=%fused_computation.22 | convolution fusion | flops 603979776 | bytes 5832704 | tf_op jit(solution)/shard_map/kpc,fkcs->fps/dot_general | solution.py:94
  30.0 0.6 while.30
  31.0 0.9 pad_maximum_fusion.1
  31.9 9.4 %all-to-all-start = ((f32[32,5,512]{2,1,0:T(8,128)}), f32[32,5,512]{2,1,0:T(8,128)S(1)}, u32[]{:S(2)}, u32[]{:S(2)}) async-start(f32[32,5,512]{2,1,0:T(8,128)} %pad_maximum_fusion.1), calls=%async_computation | async-start | bytes 1048576 | tf_op jit(solution)/shard_map/all_to_all | solution.py:106
  41.3 11.6 %all-to-all-done = f32[32,5,512]{2,1,0:T(8,128)S(1)} async-done(((f32[32,5,512]{2,1,0:T(8,128)}), f32[32,5,512]{2,1,0:T(8,128)S(1)}, u32[]{:S(2)}, u32[]{:S(2)}) %all-to-all-start) | async-done | bytes 327712 | tf_op jit(solution)/shard_map/all_to_all | solution.py:106
  54.8 2.6 %while.31 = (s32[]{:T(128)}, f32[128,512]{1,0:T(8,128)S(1)}, f32[2,128,512]{2,1,0:T(8,128)S(1)}, f32[2,128]{1,0:T(2,128)S(1)}, f32[2,128,512]{1,2,0:T(8,128)}, /*index=5*/s32[]{:T(128)}, s32[]{:T(128)}) while((s32[]{:T(128)}, f32[128,512]{1,0:T(8,128)S(1)}, f32[2,128,512]{2,1,0:T(8,128)S(1)}, f32[2,128]{1,0:T(2,128)S(1)}, ...), condition=%wide.region_5.6_spmd.clone, body=%wide.region_4.5_spmd.clone.sunk | while | flops 327684 | bytes 2623088 | solution.py:122
  54.8 1.0 constant_dynamic-slice_fusion.7
  56.1 1.0 constant_dynamic-slice_fusion.7
  57.5 1.1 pad_maximum_fusion
  58.6 3.7 %all-to-all-start.1 = ((f32[32,9,512]{2,1,0:T(8,128)}), f32[32,9,512]{2,1,0:T(8,128)S(1)}, u32[]{:S(2)}, u32[]{:S(2)}) async-start(f32[32,9,512]{2,1,0:T(8,128)} %pad_maximum_fusion), calls=%async_computation.2 | async-start | bytes 2097152 | tf_op jit(solution)/shard_map/all_to_all | solution.py:124
  62.4 16.7 %all-to-all-done.1 = f32[32,9,512]{2,1,0:T(8,128)S(1)} async-done(((f32[32,9,512]{2,1,0:T(8,128)}), f32[32,9,512]{2,1,0:T(8,128)S(1)}, u32[]{:S(2)}, u32[]{:S(2)}) %all-to-all-start.1) | async-done | bytes 589856 | tf_op jit(solution)/shard_map/all_to_all | solution.py:124
  80.4 1.0 fusion.92
  82.1 0.7 pad.142
  82.8 3.9 %all-to-all-start.2 = ((f32[32,4,512]{2,1,0:T(4,128)}), f32[32,4,512]{2,1,0:T(4,128)S(1)}, u32[]{:S(2)}, u32[]{:S(2)}) async-start(f32[32,4,512]{2,1,0:T(4,128)} %pad.142), calls=%async_computation.3 | async-start | bytes 524288 | tf_op jit(solution)/shard_map/all_to_all | solution.py:129
  86.9 8.8 %all-to-all-done.2 = f32[32,4,512]{2,1,0:T(4,128)S(1)} async-done(((f32[32,4,512]{2,1,0:T(4,128)}), f32[32,4,512]{2,1,0:T(4,128)S(1)}, u32[]{:S(2)}, u32[]{:S(2)}) %all-to-all-start.2) | async-done | bytes 262176 | tf_op jit(solution)/shard_map/all_to_all | solution.py:129
  95.8 3.9 %convolution_bitcast_fusion.1 = f32[9,128,256]{1,2,0:T(8,128)S(1)} fusion(bf16[2,9,256,512]{2,3,1,0:T(8,128)(2,1)} %fusion.51, f32[2,128,512]{2,1,0:T(8,128)S(1)} %get-tuple-element.139, f32[128,512]{1,0:T(8,128)S(1)} %mul.237, f32[2,128]{1,0:T(2,128)S(1)} %broadcast_select_fusion.3), kind=kOutput, calls=%fused_computation.21 | convolution fusion | flops 604372992 | bytes 6685696 | tf_op jit(solution)/shard_map/fps,fkcs->kpc/dot_general | solution.py:139
  100.7 0.6 all-gather.2.cloned.1.call-done
  101.3 1.7 fusion.4
  107.0 2.9 %fusion.82 = f32[9,512,64,1]{1,2,3,0:T(8,128)S(1)} fusion(bf16[2,9,512,512]{3,2,0,1:T(8,128)(2,1)S(1)} %fusion.25, bf16[2,64,512]{2,1,0:T(8,128)(2,1)S(1)} %copy-done.2), kind=kOutput, calls=%fused_computation.142 | convolution fusion | flops 603979776 | bytes 10747904 | tf_op jit(solution)/shard_map/fus,fkps->kup/dot_general | solution.py:143
  110.4 2.8 %collective-permute-start = (f32[294912]{0:T(1024)S(1)}, f32[294912]{0:T(1024)S(1)}, u32[]{:S(2)}, u32[]{:S(2)}) collective-permute-start(f32[294912]{0:T(1024)S(1)} %broadcast_select_fusion.2), channel_id=1, source_target_pairs={{0,4},{4,0},{1,5},{5,1},{2,6},{6,2},{3,7},{7,3},{8,12},{12,8},{9,1... | collective-permute-start | bytes 3538952 | tf_op jit(solution)/shard_map/ppermute | solution.py:79
  113.3 2.5 %collective-permute-done = f32[294912]{0:T(1024)S(1)} collective-permute-done((f32[294912]{0:T(1024)S(1)}, f32[294912]{0:T(1024)S(1)}, u32[]{:S(2)}, u32[]{:S(2)}) %collective-permute-start) | collective-permute-done | bytes 1179680 | tf_op jit(solution)/shard_map/ppermute | solution.py:79
  115.9 24.1 %all_to_all.31 = f32[16,1,18432]{2,1,0:T(1,128)S(1)} all-to-all(f32[16,1,18432]{2,1,0:T(1,128)S(1)} %bitcast.236), channel_id=1, replica_groups=mesh['chip'=16,'core'=2,'chan'=4] {'chip'}, dimensions={0} | all-to-all | bytes 2359296 | tf_op jit(solution)/shard_map/all_to_all | solution.py:80
  140.0 0.7 reduce_sum.18
  140.7 0.6 broadcast_in_dim.165
  141.4 19.8 %all_to_all.30 = f32[16,1,18432]{2,1,0:T(1,128)S(1)} all-to-all(f32[16,1,18432]{2,1,0:T(1,128)S(1)} %broadcast_in_dim.165), channel_id=1, replica_groups=mesh['chip'=16,'core'=2,'chan'=4] {'chip'}, dimensions={0} | all-to-all | bytes 2359296 | tf_op jit(solution)/shard_map/all_to_all | solution.py:82
  161.2 3.0 %collective-permute-start.1 = (f32[294912]{0:T(1024)S(1)}, f32[294912]{0:T(1024)}, u32[]{:S(2)}, u32[]{:S(2)}) collective-permute-start(f32[294912]{0:T(1024)S(1)} %bitcast.234), channel_id=1, source_target_pairs={{0,4},{4,0},{1,5},{5,1},{2,6},{6,2},{3,7},{7,3},{8,12},{12,8},{9,1... | collective-permute-start | bytes 3538952 | tf_op jit(solution)/shard_map/ppermute | solution.py:83
  164.2 0.8 broadcast_in_dim_reshape.2
  165.0 1.7 fusion.52
  166.8 2.4 %broadcast_select_fusion = (f32[294912]{0:T(1024)S(1)}, f32[294912]{0:T(1024)}) fusion(f32[294912]{0:T(1024)} %collective-permute-done.1, f32[294912]{0:T(1024)S(1)} %bitcast.235, pred[]{:T(512)S(6)} %eq.34), kind=kLoop, calls=%fused_computation.60 | loop fusion | flops 589824 | bytes 4718593 | tf_op jit(solution)/shard_map/jit(_where)/select_n | solution.py:85
  169.2 2.5 %reshape.62 = f32[9,128,256]{2,1,0:T(8,128)} reshape(f32[294912]{0:T(1024)} %get-tuple-element.244) | data formatting | bytes 2359296 | tf_op jit(solution)/shard_map/reshape | solution.py:86
  171.7 1.2 reshape.63
  (131 shorter events, 11.6 us)
Async XLA Ops:
  7.2 6.5 %copy-start = (bf16[9,64,512]{2,1,0:T(8,128)(2,1)S(1)}, bf16[9,64,512]{2,1,0:T(8,128)(2,1)}, u32[]{:S(2)}) copy-start(bf16[9,64,512]{2,1,0:T(8,128)(2,1)} %param.12) | copy-start | bytes 1769476
  7.2 6.2 %copy-start.2 = (bf16[2,64,512]{2,1,0:T(8,128)(2,1)S(1)}, bf16[2,64,512]{2,1,0:T(8,128)(2,1)}, u32[]{:S(2)}) copy-start(bf16[2,64,512]{2,1,0:T(8,128)(2,1)} %param.13) | copy-start | bytes 393220
  7.2 47.5 %reduce-scatter.2.cloned.1.call-start = ((), (), s32[]{:S(2)}) async-start(), calls=%async_computation.6 | async-start | bytes 2621440 | tf_op jit(solution)/shard_map/reduce_scatter | solution.py:108
  16.1 1.0 copy-start.9
  23.2 2.9 %copy-start.8 = (bf16[9,128,256]{2,1,0:T(8,128)(2,1)S(1)}, bf16[9,128,256]{2,1,0:T(8,128)(2,1)}, u32[]{:S(2)}) copy-start(bf16[9,128,256]{2,1,0:T(8,128)(2,1)} %param.11) | copy-start | bytes 1769476
  26.1 3.9 %copy-start.10 = (f32[2,128]{1,0:T(2,128)S(1)}, f32[2,128]{1,0:T(2,128)}, u32[]{:S(2)}) copy-start(f32[2,128]{1,0:T(2,128)} %param.10) | copy-start | bytes 3076
  31.9 21.0 %all-to-all-start = ((f32[32,5,512]{2,1,0:T(8,128)}), f32[32,5,512]{2,1,0:T(8,128)S(1)}, u32[]{:S(2)}, u32[]{:S(2)}) async-start(f32[32,5,512]{2,1,0:T(8,128)} %pad_maximum_fusion.1), calls=%async_computation | async-start | bytes 1048576 | tf_op jit(solution)/shard_map/all_to_all | solution.py:106
  57.4 38.4 %copy-start.3 = (f32[2,128,512]{2,1,0:T(8,128)}, f32[2,128,512]{2,1,0:T(8,128)S(1)}, u32[]{:S(2)}) copy-start(f32[2,128,512]{2,1,0:T(8,128)S(1)} %get-tuple-element.139) | copy-start | bytes 1572868
  58.6 20.5 %all-to-all-start.1 = ((f32[32,9,512]{2,1,0:T(8,128)}), f32[32,9,512]{2,1,0:T(8,128)S(1)}, u32[]{:S(2)}, u32[]{:S(2)}) async-start(f32[32,9,512]{2,1,0:T(8,128)} %pad_maximum_fusion), calls=%async_computation.2 | async-start | bytes 2097152 | tf_op jit(solution)/shard_map/all_to_all | solution.py:124
  62.3 39.0 %all-gather.2.cloned.1.call-start = ((), (), s32[]{:S(2)}) async-start(), calls=%async_computation.7 | async-start | bytes 1310720 | tf_op jit(solution)/shard_map/all_gather | solution.py:142
  80.3 1.3 copy-start.5
  81.8 5.1 %copy-start.11 = (pred[2]{0:T(512)(128)(4,1)S(1)}, pred[2]{0:T(512)(128)(4,1)}, u32[]{:S(2)}) copy-start(pred[2]{0:T(512)(128)(4,1)} %constant.170.clone.1) | copy-start | bytes 10
  82.8 12.9 %all-to-all-start.2 = ((f32[32,4,512]{2,1,0:T(4,128)}), f32[32,4,512]{2,1,0:T(4,128)S(1)}, u32[]{:S(2)}, u32[]{:S(2)}) async-start(f32[32,4,512]{2,1,0:T(4,128)} %pad.142), calls=%async_computation.3 | async-start | bytes 524288 | tf_op jit(solution)/shard_map/all_to_all | solution.py:129
  101.3 1.7 copy-start.1
  110.4 5.3 %collective-permute-start = (f32[294912]{0:T(1024)S(1)}, f32[294912]{0:T(1024)S(1)}, u32[]{:S(2)}, u32[]{:S(2)}) collective-permute-start(f32[294912]{0:T(1024)S(1)} %broadcast_select_fusion.2), channel_id=1, source_target_pairs={{0,4},{4,0},{1,5},{5,1},{2,6},{6,2},{3,7},{7,3},{8,12},{12,8},{9,1... | collective-permute-start | bytes 3538952 | tf_op jit(solution)/shard_map/ppermute | solution.py:79
  140.7 23.4 %copy-start.6 = (f32[32,4,512]{2,1,0:T(4,128)S(1)}, f32[32,4,512]{2,1,0:T(4,128)}, u32[]{:S(2)}) copy-start(f32[32,4,512]{2,1,0:T(4,128)} %copy-done.5) | copy-start | bytes 786436
  141.4 23.6 %copy-start.7 = (f32[2,128,512]{2,1,0:T(8,128)S(1)}, f32[2,128,512]{2,1,0:T(8,128)}, u32[]{:S(2)}) copy-start(f32[2,128,512]{2,1,0:T(8,128)} %get-tuple-element.242) | copy-start | bytes 1572868
  141.4 23.6 %copy-start.4 = (f32[2,128,512]{2,1,0:T(8,128)S(1)}, f32[2,128,512]{2,1,0:T(8,128)}, u32[]{:S(2)}) copy-start(f32[2,128,512]{2,1,0:T(8,128)} %copy-done.3) | copy-start | bytes 1572868
  161.2 5.6 %collective-permute-start.1 = (f32[294912]{0:T(1024)S(1)}, f32[294912]{0:T(1024)}, u32[]{:S(2)}, u32[]{:S(2)}) collective-permute-start(f32[294912]{0:T(1024)S(1)} %bitcast.234), channel_id=1, source_target_pairs={{0,4},{4,0},{1,5},{5,1},{2,6},{6,2},{3,7},{7,3},{8,12},{12,8},{9,1... | collective-permute-start | bytes 3538952 | tf_op jit(solution)/shard_map/ppermute | solution.py:83
Sparse Core Ops, SparseCore 0:
  16.2 32.8 reduce-scatter.1
  81.6 19.6 all-gather.1

commit v6 on v5

--- a/solution.py
+++ b/solution.py
@@ -67,6 +67,17 @@
     return jnp.stack(parts, axis=source.ndim - 2)
 
 
+def stencil_conv(inputs, kernel, width):
+    frames, chans, cells = inputs.shape
+    image = inputs.reshape(frames, chans, cells // width, width)
+    taps = kernel.reshape(3, 3, kernel.shape[1], chans).transpose(2, 3, 0, 1)
+    out = lax.conv_general_dilated(
+        image, taps, (1, 1), ((1, 1), (1, 1)), dimension_numbers=("NCHW", "OIHW", "NCHW"),
+        preferred_element_type=jnp.float32,
+    )
+    return out.reshape(frames, kernel.shape[1], cells)
+
+
 FRAME_AXES = ("chip", "core")
 
 
@@ -90,8 +101,7 @@
     local_rows = kernel_b.shape[1]
     cell_count = inputs.shape[-1]
     blank_state = jnp.zeros((local_rows, cell_count), jnp.float32)
-    input_stack = stencil_stack(inputs, W, 1)
-    drives = jnp.einsum("kpc,fkcs->fps", kernel_b, input_stack, preferred_element_type=jnp.float32)
+    drives = stencil_conv(inputs, kernel_b, W)
 
     def advance(current, frame_pair):
         frame_rate, drive = frame_pair
@@ -136,12 +146,13 @@
     adjoint = local_adjoint + later_decay[:, :, None] * arriving[None]
     decay_grad = jnp.sum(adjoint * previous, axis=2)
     adjoint_bf = adjoint.astype(jnp.bfloat16)
+    input_stack = stencil_stack(inputs, W, 1)
     grad_b_part = jnp.einsum(
         "fps,fkcs->kpc", adjoint_bf, input_stack, preferred_element_type=jnp.float32
     )
-    shifted = stencil_stack(lax.all_gather(states_bf, "chan", axis=1, tiled=True), W, 1)
+    all_states = lax.all_gather(states_bf, "chan", axis=1, tiled=True)
     grad_c_part = jnp.einsum(
-        "fus,fkps->kup", cotangent, shifted, preferred_element_type=jnp.float32
+        "fkus,fps->kup", cot_stack, all_states, preferred_element_type=jnp.float32
     )
     grad_b, grad_c = pair_then_chip_sum(grad_b_part, grad_c_part)
     return (grad_b, grad_c, decay_grad)

time: 181 us -> 172 us (0.950)
  waiting for transfers between devices: 40.3 us -> 34.4 us
  other arithmetic: 31.4 us -> 26.7 us
  local copies, waits for them, and re-layouts: 13.3 us -> 17 us
    unnamed x26 -> x18, other arithmetic: 19.2 us -> 13.8 us
    all_to_all x1, waiting for transfers between devices: 11.6 us -> 6.27 us  [body(): lax.all_to_all(pack_chunks(decay_total, local_end, blocks), FRAME_AXES, 0...]
    dot_general x2 -> x1, matrix products: 6.73 us -> 2.38 us  [body(): jnp.einsum('fkus,fps->kup', cot_stack, all_states, preferred_element_type...]
    all_to_all x1, starting transfers between devices: 3.72 us -> 7.75 us  [body(): lax.all_to_all(jnp.concatenate([entering_owned, pack_chunks(decay_total,...]
    reduce_scatter x1, waiting for transfers between devices: 0.02 us -> 4.02 us  [body(): lax.psum_scatter(jnp.einsum('kup,fkus->pfs', kernel_c, cot_stack, preferr...]
    all_to_all x1, waiting for transfers between devices: 16.7 us -> 13.6 us  [body(): lax.all_to_all(jnp.concatenate([entering_owned, pack_chunks(decay_total,...]
    ppermute x1, starting transfers between devices: 2.83 us -> 0.29 us  [pair_then_chip_sum(): lax.ppermute(sent, 'core', swap)]
    unnamed x29 -> x38, local copies, waits for them, and re-layouts: 2.39 us -> 4.42 us
  transfers between devices with their start and end apart: 7 -> 7, of which waited for: 5 -> 5; matrix products, arithmetic and copies ran while one was open for 14% -> 16% of each run, Pallas kernels for 0% -> 0%
where the time goes in v6:
time: 172 us; the launch traced here: 171 us
  blocking collectives  42.5 us (25%)
  waiting for transfers between devices  34.4 us (20%)
  other arithmetic  26.7 us (16%)
  starting transfers between devices  24.4 us (14%)
  local copies, waits for them, and re-layouts  17 us (10%)
  between operations  14.7 us (9%)
  matrix products  11.2 us (7%)
    all_to_all x1, blocking collectives, pair_then_chip_sum(): pieces = lax.all_to_all(pair_sum, 'chip', 0, 0, tiled=True)  22.7 us
    all_to_all x1, blocking collectives, pair_then_chip_sum(): lax.all_to_all(jnp.broadcast_to(reduced, pieces.shape), 'chip', 0, 0, til...  19.8 us
    unnamed x18, other arithmetic  13.8 us
    all_to_all x1, waiting for transfers between devices, body(): lax.all_to_all(jnp.concatenate([entering_owned, pack_chunks(decay_total,...  13.6 us
    all_to_all x1, starting transfers between devices, body(): lax.all_to_all(pack_chunks(decay_total, local_end, blocks), FRAME_AXES, 0...  9.42 us
    all_to_all x1, waiting for transfers between devices, body(): lax.all_to_all(arriving_owned, FRAME_AXES, 0, 0, tiled=True)  7.81 us
    all_to_all x1, starting transfers between devices, body(): lax.all_to_all(jnp.concatenate([entering_owned, pack_chunks(decay_total,...  7.75 us
    all_to_all x1, waiting for transfers between devices, body(): lax.all_to_all(pack_chunks(decay_total, local_end, blocks), FRAME_AXES, 0...  6.27 us
  transfers between devices with their start and end apart: 7, of which 5 were waited for; matrix products, arithmetic and copies ran while one was open for 16% of the time, Pallas kernels for 0%

profile of v6, /device:TPU:1, one launch (start us, length us, event | category | flops | bytes accessed | tf_op | source)
XLA Modules:
  0.0 171.1 jit_solution(16873624932661601412)
XLA Ops:
  7.3 1.1 fusion.41
  8.3 1.0 fusion.44
  9.4 1.0 fusion.47
  10.4 1.0 fusion.50
  11.4 0.9 bitcast_dynamic-update-slice_fusion.3
  12.8 1.0 copy-done.11
  13.8 2.4 %convolution_bitcast_fusion = f32[512,2,512]{0,2,1:T(8,128)} fusion(bf16[2,9,64,512]{3,2,1,0:T(8,128)(2,1)S(1)} %fusion.62, bf16[9,64,512]{2,1,0:T(8,128)(2,1)S(1)} %copy-done), kind=kOutput, calls=%fused_computation.12 | convolution fusion | flops 603979776 | bytes 3866624 | tf_op jit(solution)/shard_map/kup,fkus->pfs/dot_general | solution.py:119
  16.2 0.6 copy-done.12
  17.9 0.9 copy-done.14
  18.8 1.5 convolution_select_fusion
  20.8 0.6 while.30
  21.5 0.9 pad_maximum_fusion.1
  22.4 9.4 %all-to-all-start = ((f32[32,5,512]{2,1,0:T(8,128)}), f32[32,5,512]{2,1,0:T(8,128)S(1)}, u32[]{:S(2)}, u32[]{:S(2)}) async-start(f32[32,5,512]{2,1,0:T(8,128)} %pad_maximum_fusion.1), calls=%async_computation | async-start | bytes 1048576 | tf_op jit(solution)/shard_map/all_to_all | solution.py:116
  31.8 1.1 fusion.11
  32.9 1.1 fusion.14
  34.0 1.1 fusion.17
  35.1 1.1 fusion.20
  36.3 0.9 bitcast_dynamic-update-slice_fusion.2
  37.2 6.3 %all-to-all-done = f32[32,5,512]{2,1,0:T(8,128)S(1)} async-done(((f32[32,5,512]{2,1,0:T(8,128)}), f32[32,5,512]{2,1,0:T(8,128)S(1)}, u32[]{:S(2)}, u32[]{:S(2)}) %all-to-all-start) | async-done | bytes 327712 | tf_op jit(solution)/shard_map/all_to_all | solution.py:116
  45.2 4.0 %reduce-scatter.2.cloned.1.call-done = f32[128,2,512]{0,2,1:T(8,128)} async-done(((f32[512,2,512]{0,2,1:T(8,128)}), f32[128,2,512]{0,2,1:T(8,128)}) %reduce-scatter.2.cloned.1.call-update) | async-done | bytes 524304 | tf_op jit(solution)/shard_map/reduce_scatter | solution.py:118
  49.3 2.6 %while.31 = (s32[]{:T(128)}, f32[128,512]{1,0:T(8,128)S(1)}, f32[2,128,512]{2,1,0:T(8,128)S(1)}, f32[2,128]{1,0:T(2,128)S(1)}, f32[2,128,512]{1,2,0:T(8,128)}, /*index=5*/s32[]{:T(128)}, s32[]{:T(128)}) while((s32[]{:T(128)}, f32[128,512]{1,0:T(8,128)S(1)}, f32[2,128,512]{2,1,0:T(8,128)S(1)}, f32[2,128]{1,0:T(2,128)S(1)}, ...), condition=%wide.region_5.6_spmd.clone, body=%wide.region_4.5_spmd.clone.sunk | while | flops 327684 | bytes 2623096 | solution.py:132
  49.3 1.0 constant_dynamic-slice_fusion.7
  50.6 1.0 constant_dynamic-slice_fusion.7
  52.0 1.1 pad_maximum_fusion
  53.1 7.7 %all-to-all-start.1 = ((f32[32,9,512]{2,1,0:T(8,128)}), f32[32,9,512]{2,1,0:T(8,128)S(1)}, u32[]{:S(2)}, u32[]{:S(2)}) async-start(f32[32,9,512]{2,1,0:T(8,128)} %pad_maximum_fusion), calls=%async_computation.2 | async-start | bytes 2097152 | tf_op jit(solution)/shard_map/all_to_all | solution.py:134
  60.9 1.1 fusion.23
  62.1 1.1 fusion.26
  63.1 1.1 fusion.29
  64.2 13.6 %all-to-all-done.1 = f32[32,9,512]{2,1,0:T(8,128)S(1)} async-done(((f32[32,9,512]{2,1,0:T(8,128)}), f32[32,9,512]{2,1,0:T(8,128)S(1)}, u32[]{:S(2)}, u32[]{:S(2)}) %all-to-all-start.1) | async-done | bytes 589856 | tf_op jit(solution)/shard_map/all_to_all | solution.py:134
  78.7 2.1 %fusion.71 = (bf16[2,128,512]{2,1,0:T(8,128)(2,1)}, f32[2,128,512]{2,1,0:T(8,128)}) fusion(f32[2,128,512]{2,1,0:T(8,128)} %copy-done.9, f32[128,512]{1,0:T(8,128)S(1)} %mul.241, f32[2,128]{1,0:T(2,128)S(1)} %reduce_window.16), kind=kLoop, calls=%fused_computation.138 | loop fusion | flops 393216 | bytes 1573888 | tf_op jit(solution)/shard_map/convert_element_type | solution.py:143
  81.7 0.7 pad.130
  82.5 3.9 %all-to-all-start.2 = ((f32[32,4,512]{2,1,0:T(4,128)}), f32[32,4,512]{2,1,0:T(4,128)S(1)}, u32[]{:S(2)}, u32[]{:S(2)}) async-start(f32[32,4,512]{2,1,0:T(4,128)} %pad.130), calls=%async_computation.3 | async-start | bytes 524288 | tf_op jit(solution)/shard_map/all_to_all | solution.py:139
  86.5 1.1 fusion.32
  87.6 7.8 %all-to-all-done.2 = f32[32,4,512]{2,1,0:T(4,128)S(1)} async-done(((f32[32,4,512]{2,1,0:T(4,128)}), f32[32,4,512]{2,1,0:T(4,128)S(1)}, u32[]{:S(2)}, u32[]{:S(2)}) %all-to-all-start.2) | async-done | bytes 262176 | tf_op jit(solution)/shard_map/all_to_all | solution.py:139
  95.5 4.9 %convolution_bitcast_fusion.1 = f32[9,128,256]{1,2,0:T(8,128)} fusion(bf16[2,9,256,512]{3,2,0,1:T(8,128)(2,1)} %fusion.32, f32[2,128,512]{2,1,0:T(8,128)S(1)} %get-tuple-element.139, f32[128,512]{1,0:T(8,128)S(1)} %mul.237, f32[2,128]{1,0:T(2,128)S(1)} %broadcast_select_fusion.3), kind=kOutput, calls=%fused_computation.15 | convolution fusion | flops 604372992 | bytes 6685696 | tf_op jit(solution)/shard_map/fps,fkcs->kpc/dot_general | solution.py:150
  100.4 1.6 copy.125
  102.7 2.4 %fusion.3 = f32[9,64,512,1]{2,1,0,3:T(8,128)S(1)} fusion(bf16[2,9,64,512]{3,2,1,0:T(8,128)(2,1)} %copy-done.11, bf16[2,512,512]{2,1,0:T(8,128)(2,1)} %all-gather.2.cloned.1.call-done), kind=kOutput, calls=%fused_computation.27 | convolution fusion | flops 603979776 | bytes 3407872 | tf_op jit(solution)/shard_map/fkus,fps->kup/dot_general | solution.py:154
  105.9 2.6 %collective-permute-done = f32[294912]{0:T(1024)S(1)} collective-permute-done((f32[294912]{0:T(1024)S(1)}, f32[294912]{0:T(1024)S(1)}, u32[]{:S(2)}, u32[]{:S(2)}) %collective-permute-start) | collective-permute-done | bytes 1179680 | tf_op jit(solution)/shard_map/ppermute | solution.py:90
  108.7 22.7 %all_to_all.31 = f32[16,1,18432]{2,1,0:T(1,128)S(1)} all-to-all(f32[16,1,18432]{2,1,0:T(1,128)S(1)} %bitcast.189), channel_id=1, replica_groups=mesh['chip'=16,'core'=2,'chan'=4] {'chip'}, dimensions={0} | all-to-all | bytes 2359296 | tf_op jit(solution)/shard_map/all_to_all | solution.py:91
  131.3 0.7 reduce_sum.18
  132.1 0.6 broadcast_in_dim.121
  132.7 19.8 %all_to_all.30 = f32[16,1,18432]{2,1,0:T(1,128)S(1)} all-to-all(f32[16,1,18432]{2,1,0:T(1,128)S(1)} %broadcast_in_dim.121), channel_id=1, replica_groups=mesh['chip'=16,'core'=2,'chan'=4] {'chip'}, dimensions={0} | all-to-all | bytes 2359296 | tf_op jit(solution)/shard_map/all_to_all | solution.py:93
  152.5 3.0 %collective-permute-start.1 = (f32[294912]{0:T(1024)S(1)}, f32[294912]{0:T(1024)}, u32[]{:S(2)}, u32[]{:S(2)}) collective-permute-start(f32[294912]{0:T(1024)S(1)} %bitcast.187), channel_id=1, source_target_pairs={{0,4},{4,0},{1,5},{5,1},{2,6},{6,2},{3,7},{7,3},{8,12},{12,8},{9,1... | collective-permute-start | bytes 3538952 | tf_op jit(solution)/shard_map/ppermute | solution.py:94
  155.5 0.8 broadcast_in_dim_reshape.2
  156.3 1.7 %fusion.33 = f32[2,128]{1,0:T(2,128)} fusion(f32[1,128,512]{2,1,0:T(8,128)S(1)} %slice.213, f32[1,128,512]{2,1,0:T(8,128)} %broadcast_in_dim_reshape.2, f32[2,128,512]{2,1,0:T(8,128)S(1)} %copy-done.4, f32[128,512]{1,0:T(8,128)S(1)} %copy-done.8, f32[2,128]{1,0:T(2,128)S(1)} %broadcast_select_fusion.3), kind=kLoop, calls=%fused_computation.63 | loop fusion | flops 655104 | bytes 1312768 | tf_op jit(solution)/shard_map/reduce_sum | solution.py:147
  158.1 2.4 %broadcast_select_fusion = (f32[294912]{0:T(1024)}, f32[294912]{0:T(1024)S(1)}) fusion(f32[294912]{0:T(1024)} %collective-permute-done.1, f32[294912]{0:T(1024)S(1)} %bitcast.188, pred[]{:T(512)S(6)} %eq.25), kind=kLoop, calls=%fused_computation.33 | loop fusion | flops 589824 | bytes 4718593 | tf_op jit(solution)/shard_map/jit(_where)/select_n | solution.py:96
  160.5 2.4 %reshape.75 = f32[9,64,512]{2,1,0:T(8,128)} reshape(f32[294912]{0:T(1024)} %get-tuple-element.238) | data formatting | bytes 2359296 | tf_op jit(solution)/shard_map/reshape | solution.py:97
  162.9 1.3 reshape.74
  (137 shorter events, 8.5 us)
Async XLA Ops:
  7.2 6.6 %copy-start = (bf16[9,64,512]{2,1,0:T(8,128)(2,1)S(1)}, bf16[9,64,512]{2,1,0:T(8,128)(2,1)}, u32[]{:S(2)}) copy-start(bf16[9,64,512]{2,1,0:T(8,128)(2,1)} %param.12) | copy-start | bytes 1769476
  7.2 5.2 %copy-start.2 = (bf16[2,64,512]{2,1,0:T(8,128)(2,1)S(1)}, bf16[2,64,512]{2,1,0:T(8,128)(2,1)}, u32[]{:S(2)}) copy-start(bf16[2,64,512]{2,1,0:T(8,128)(2,1)} %param.13) | copy-start | bytes 393220
  7.2 42.0 %reduce-scatter.2.cloned.1.call-start = ((), (), s32[]{:S(2)}) async-start(), calls=%async_computation.6 | async-start | bytes 2621440 | tf_op jit(solution)/shard_map/reduce_scatter | solution.py:118
  12.8 1.0 copy-start.11
  16.2 0.7 copy-start.12
  16.2 1.1 copy-start.1
  17.7 1.1 copy-start.14
  17.7 1.1 copy-start.15
  21.4 1.0 copy-start.9
  22.4 21.0 %all-to-all-start = ((f32[32,5,512]{2,1,0:T(8,128)}), f32[32,5,512]{2,1,0:T(8,128)S(1)}, u32[]{:S(2)}, u32[]{:S(2)}) async-start(f32[32,5,512]{2,1,0:T(8,128)} %pad_maximum_fusion.1), calls=%async_computation | async-start | bytes 1048576 | tf_op jit(solution)/shard_map/all_to_all | solution.py:116
  51.9 43.6 %copy-start.3 = (f32[2,128,512]{2,1,0:T(8,128)}, f32[2,128,512]{2,1,0:T(8,128)S(1)}, u32[]{:S(2)}) copy-start(f32[2,128,512]{2,1,0:T(8,128)S(1)} %get-tuple-element.139) | copy-start | bytes 1572868
  53.1 24.7 %all-to-all-start.1 = ((f32[32,9,512]{2,1,0:T(8,128)}), f32[32,9,512]{2,1,0:T(8,128)S(1)}, u32[]{:S(2)}, u32[]{:S(2)}) async-start(f32[32,9,512]{2,1,0:T(8,128)} %pad_maximum_fusion), calls=%async_computation.2 | async-start | bytes 2097152 | tf_op jit(solution)/shard_map/all_to_all | solution.py:134
  60.9 41.8 %all-gather.2.cloned.1.call-start = ((), (), s32[]{:S(2)}) async-start(), calls=%async_computation.7 | async-start | bytes 1310720 | tf_op jit(solution)/shard_map/all_gather | solution.py:153
  78.5 2.2 %copy-start.5 = (f32[32,4,512]{2,1,0:T(4,128)}, f32[32,4,512]{2,1,0:T(4,128)S(1)}, u32[]{:S(2)}) copy-start(f32[32,4,512]{2,1,0:T(4,128)S(1)} %get-tuple-element.241) | copy-start | bytes 786436
  81.4 5.0 %copy-start.13 = (pred[2]{0:T(512)(128)(4,1)S(1)}, pred[2]{0:T(512)(128)(4,1)}, u32[]{:S(2)}) copy-start(pred[2]{0:T(512)(128)(4,1)} %constant.143.clone.1) | copy-start | bytes 10
  82.5 12.9 %all-to-all-start.2 = ((f32[32,4,512]{2,1,0:T(4,128)}), f32[32,4,512]{2,1,0:T(4,128)S(1)}, u32[]{:S(2)}, u32[]{:S(2)}) async-start(f32[32,4,512]{2,1,0:T(4,128)} %pad.130), calls=%async_computation.3 | async-start | bytes 524288 | tf_op jit(solution)/shard_map/all_to_all | solution.py:139
  95.5 5.0 %copy-start.7 = (f32[128,512]{1,0:T(8,128)}, f32[128,512]{1,0:T(8,128)S(1)}, u32[]{:S(2)}) copy-start(f32[128,512]{1,0:T(8,128)S(1)} %mul.237) | copy-start | bytes 786436
  105.6 2.9 %collective-permute-start = (f32[294912]{0:T(1024)S(1)}, f32[294912]{0:T(1024)S(1)}, u32[]{:S(2)}, u32[]{:S(2)}) collective-permute-start(f32[294912]{0:T(1024)S(1)} %broadcast_select_fusion.2), channel_id=1, source_target_pairs={{0,4},{4,0},{1,5},{5,1},{2,6},{6,2},{3,7},{7,3},{8,12},{12,8},{9,1... | collective-permute-start | bytes 3538952 | tf_op jit(solution)/shard_map/ppermute | solution.py:90
  132.7 22.8 %copy-start.6 = (f32[32,4,512]{2,1,0:T(4,128)S(1)}, f32[32,4,512]{2,1,0:T(4,128)}, u32[]{:S(2)}) copy-start(f32[32,4,512]{2,1,0:T(4,128)} %copy-done.5) | copy-start | bytes 786436
  132.7 23.6 %copy-start.10 = (f32[2,128,512]{2,1,0:T(8,128)S(1)}, f32[2,128,512]{2,1,0:T(8,128)}, u32[]{:S(2)}) copy-start(f32[2,128,512]{2,1,0:T(8,128)} %get-tuple-element.237) | copy-start | bytes 1572868
  132.7 23.6 %copy-start.4 = (f32[2,128,512]{2,1,0:T(8,128)S(1)}, f32[2,128,512]{2,1,0:T(8,128)}, u32[]{:S(2)}) copy-start(f32[2,128,512]{2,1,0:T(8,128)} %copy-done.3) | copy-start | bytes 1572868
  132.7 23.6 %copy-start.8 = (f32[128,512]{1,0:T(8,128)S(1)}, f32[128,512]{1,0:T(8,128)}, u32[]{:S(2)}) copy-start(f32[128,512]{1,0:T(8,128)} %copy-done.7) | copy-start | bytes 786436
  152.5 5.6 %collective-permute-start.1 = (f32[294912]{0:T(1024)S(1)}, f32[294912]{0:T(1024)}, u32[]{:S(2)}, u32[]{:S(2)}) collective-permute-start(f32[294912]{0:T(1024)S(1)} %bitcast.187), channel_id=1, source_target_pairs={{0,4},{4,0},{1,5},{5,1},{2,6},{6,2},{3,7},{7,3},{8,12},{12,8},{9,1... | collective-permute-start | bytes 3538952 | tf_op jit(solution)/shard_map/ppermute | solution.py:94
Sparse Core Ops, SparseCore 0:
  16.3 32.8 reduce-scatter.1
  80.9 17.9 all-gather.1

commit v7 on v6

--- a/solution.py
+++ b/solution.py
@@ -115,14 +115,10 @@
     chunk = rows // blocks
     entering_owned = scan_owned(lax.all_to_all(pack_chunks(decay_total, local_end, blocks), FRAME_AXES, 0, 0, tiled=True), False)
     cot_stack = stencil_stack(cotangent, W, -1)
-    injected = lax.psum_scatter(
-        jnp.einsum("kup,fkus->pfs", kernel_c, cot_stack, preferred_element_type=jnp.float32),
-        "chan",
-        scatter_dimension=0,
-        tiled=True,
-    )
+    all_cotangent = lax.all_gather(cotangent, "chan", axis=1, tiled=True)
+    readout_local = lax.all_to_all(kernel_c, "chan", 2, 1, tiled=True)
+    injected = stencil_conv(all_cotangent, jnp.flip(readout_local, 0).transpose(0, 2, 1), W)
     entering_owned, injected = lax.optimization_barrier((entering_owned, injected))
-    injected = jnp.moveaxis(injected, 1, 0)
 
     def retreat(carried, frame_pair):
         frame_rate, source = frame_pair

time: 172 us -> 201 us (1.17)
  blocking collectives: 42.5 us -> 55 us
  local copies, waits for them, and re-layouts: 17 us -> 28.9 us
  starting transfers between devices: 24.4 us -> 31.8 us
  waiting for transfers between devices: 34.4 us -> 29.8 us
  other arithmetic: 26.7 us -> 28.9 us
    all_gather x0 -> x1, blocking collectives: none -> 11.1 us  [body(): all_cotangent = lax.all_gather(cotangent, 'chan', axis=1, tiled=True)]
    unnamed x38 -> x39, local copies, waits for them, and re-layouts: 4.42 us -> 15.4 us
    all_to_all x1, waiting for transfers between devices: 6.27 us -> 0.01 us  [body(): lax.all_to_all(pack_chunks(decay_total, local_end, blocks), FRAME_AXES, 0...]
    all_to_all x0 -> x1, waiting for transfers between devices: none -> 5.55 us  [body(): readout_local = lax.all_to_all(kernel_c, 'chan', 2, 1, tiled=True)]
    reduce_scatter x1 -> x0, waiting for transfers between devices: 4.02 us -> none  [body(): lax.psum_scatter(jnp.einsum('kup,fkus->pfs', kernel_c, cot_stack, preferr...]
    all_to_all x1, starting transfers between devices: 7.75 us -> 11.4 us  [body(): lax.all_to_all(jnp.concatenate([entering_owned, pack_chunks(decay_total,...]
    all_to_all x0 -> x1, starting transfers between devices: none -> 3.6 us  [body(): readout_local = lax.all_to_all(kernel_c, 'chan', 2, 1, tiled=True)]
    all_to_all x0 -> x2, local copies, waits for them, and re-layouts: none -> 3.14 us  [body(): readout_local = lax.all_to_all(kernel_c, 'chan', 2, 1, tiled=True)]
  transfers between devices with their start and end apart: 7 -> 7, of which waited for: 5 -> 4; matrix products, arithmetic and copies ran while one was open for 16% -> 18% of each run, Pallas kernels for 0% -> 0%
where the time goes in v7:
time: 201 us; the launch traced here: 200 us
  blocking collectives  55 us (27%)
  starting transfers between devices  31.8 us (16%)
  waiting for transfers between devices  29.8 us (15%)
  local copies, waits for them, and re-layouts  28.9 us (14%)
  other arithmetic  28.9 us (14%)
  between operations  14.7 us (7%)
  matrix products  10.4 us (5%)
    all_to_all x1, blocking collectives, pair_then_chip_sum(): pieces = lax.all_to_all(pair_sum, 'chip', 0, 0, tiled=True)  24.1 us
    all_to_all x1, blocking collectives, pair_then_chip_sum(): lax.all_to_all(jnp.broadcast_to(reduced, pieces.shape), 'chip', 0, 0, til...  19.8 us
    unnamed x39, local copies, waits for them, and re-layouts  15.4 us
    unnamed x18, other arithmetic  14.5 us
    all_to_all x1, waiting for transfers between devices, body(): lax.all_to_all(jnp.concatenate([entering_owned, pack_chunks(decay_total,...  13.9 us
    all_to_all x1, starting transfers between devices, body(): lax.all_to_all(jnp.concatenate([entering_owned, pack_chunks(decay_total,...  11.4 us
    all_gather x1, blocking collectives, body(): all_cotangent = lax.all_gather(cotangent, 'chan', axis=1, tiled=True)  11.1 us
    all_to_all x1, starting transfers between devices, body(): lax.all_to_all(pack_chunks(decay_total, local_end, blocks), FRAME_AXES, 0...  9.42 us
  transfers between devices with their start and end apart: 7, of which 4 were waited for; matrix products, arithmetic and copies ran while one was open for 18% of the time, Pallas kernels for 0%

profile of v7, /device:TPU:1, one launch (start us, length us, event | category | flops | bytes accessed | tf_op | source)
XLA Modules:
  0.0 199.8 jit_solution(8911270325838182981)
XLA Ops:
  7.2 1.3 copy.146
  9.5 1.5 convolution_select_fusion.1
  12.8 0.9 pad_maximum_fusion.1
  13.8 9.4 %all-to-all-start = ((f32[32,5,512]{2,1,0:T(8,128)}), f32[32,5,512]{2,1,0:T(8,128)S(1)}, u32[]{:S(2)}, u32[]{:S(2)}) async-start(f32[32,5,512]{2,1,0:T(8,128)} %pad_maximum_fusion.1), calls=%async_computation | async-start | bytes 1048576 | tf_op jit(solution)/shard_map/all_to_all | solution.py:116
  23.4 11.1 %all_gather.6 = bf16[2,256,512]{2,0,1:T(2,128)(2,1)S(1)} all-gather(bf16[2,64,512]{2,0,1:T(2,128)(2,1)S(1)} %copy.161), channel_id=1, replica_groups=mesh['chip'=16,'core'=2,'chan'=4] {'chan'}, dimensions={1}, use_global_device_ids=true | all-gather | bytes 655360 | tf_op jit(solution)/shard_map/all_gather | solution.py:118
  36.1 2.8 %copy.165 = bf16[9,64,512]{1,0,2:T(8,128)(2,1)} copy(bf16[9,64,512]{2,1,0:T(8,128)(2,1)S(1)} %copy-done.9) | data formatting | bytes 1179648 | tf_op args[3]
  38.9 4.0 %reshape.112 = bf16[4,2,36864]{2,1,0:T(2,128)(2,1)} reshape(bf16[512,9,64]{2,1,0:T(8,128)(2,1)} %bitcast.181) | data formatting | bytes 1179648
  43.0 1.1 fusion.14
  44.0 0.8 fusion.44
  44.8 1.1 fusion.17
  45.9 1.1 fusion.20
  47.0 1.1 fusion.23
  48.2 0.9 bitcast_dynamic-update-slice_fusion.2
  49.0 0.8 fusion.47
  49.8 0.8 fusion.50
  50.6 0.8 fusion.53
  52.0 0.8 fusion.56
  52.8 0.8 fusion.59
  53.5 0.8 fusion.62
  54.3 0.9 fusion.7
  55.2 1.1 fusion.26
  56.3 3.6 %all-to-all-start.1 = ((bf16[4,2,36864]{2,1,0:T(2,128)(2,1)}), bf16[4,2,36864]{2,1,0:T(2,128)(2,1)S(1)}, u32[]{:S(2)}, u32[]{:S(2)}) async-start(bf16[4,2,36864]{2,1,0:T(2,128)(2,1)} %reshape.112), calls=%async_computation.1 | async-start | bytes 1179648 | tf_op jit(solution)/shard_map/all_to_all | solution.py:119
  61.6 5.5 %all-to-all-done.1 = bf16[4,2,36864]{2,1,0:T(2,128)(2,1)S(1)} async-done(((bf16[4,2,36864]{2,1,0:T(2,128)(2,1)}), bf16[4,2,36864]{2,1,0:T(2,128)(2,1)S(1)}, u32[]{:S(2)}, u32[]{:S(2)}) %all-to-all-start.1) | async-done | bytes 589856 | tf_op jit(solution)/shard_map/all_to_all | solution.py:119
  67.2 2.5 %reshape.113 = bf16[512,9,64]{2,1,0:T(8,128)(2,1)} reshape(bf16[4,2,36864]{2,1,0:T(2,128)(2,1)S(1)} %all-to-all-done.1) | data formatting | bytes 1179648
  69.6 3.0 %copy.185 = bf16[9,64,4,128]{3,2,1,0:T(4,128)(2,1)S(1)} copy(bf16[9,64,4,128]{1,0,3,2:T(8,128)(2,1)} %bitcast.180) | data formatting | bytes 1179648 | tf_op jit(solution)/shard_map/all_to_all | solution.py:119
  73.3 2.7 %convolution_select_fusion = f32[8,16,9,128]{3,1,2,0:T(8,128)S(1)} fusion(bf16[3,3,128,256]{2,3,1,0:T(8,128)(2,1)S(1)} %bitcast.199, bf16[256,8,2,8,11]{0,1,4,3,2:T(8,128)(2,1)} %fusion.7, pred[16,9]{0,1:T(8,128)(4,1)S(1)} %copy-done.13), kind=kOutput, calls=%fused_computation.16 | convolution fusion | flops 623001600 | bytes 1900688 | tf_op jit(solution)/shard_map/conv_general_dilated | solution.py:74
  77.2 1.1 pad_maximum_fusion
  78.4 11.4 %all-to-all-start.2 = ((f32[32,9,512]{2,1,0:T(8,128)}), f32[32,9,512]{2,1,0:T(8,128)S(1)}, u32[]{:S(2)}, u32[]{:S(2)}) async-start(f32[32,9,512]{2,1,0:T(8,128)} %pad_maximum_fusion), calls=%async_computation.2 | async-start | bytes 2097152 | tf_op jit(solution)/shard_map/all_to_all | solution.py:130
  89.9 0.8 fusion.65
  90.7 1.1 fusion.29
  91.8 1.1 fusion.32
  92.8 13.9 %all-to-all-done.2 = f32[32,9,512]{2,1,0:T(8,128)S(1)} async-done(((f32[32,9,512]{2,1,0:T(8,128)}), f32[32,9,512]{2,1,0:T(8,128)S(1)}, u32[]{:S(2)}, u32[]{:S(2)}) %all-to-all-start.2) | async-done | bytes 589856 | tf_op jit(solution)/shard_map/all_to_all | solution.py:130
  107.6 2.0 %fusion.74 = (bf16[2,128,512]{2,1,0:T(8,128)(2,1)}, f32[2,128,512]{2,1,0:T(8,128)}) fusion(f32[2,128,512]{2,1,0:T(8,128)} %copy-done.7, f32[128,512]{1,0:T(8,128)S(1)} %mul.241, f32[2,128]{1,0:T(2,128)S(1)} %reduce_window.16), kind=kLoop, calls=%fused_computation.142 | loop fusion | flops 393216 | bytes 1573888 | tf_op jit(solution)/shard_map/convert_element_type | solution.py:139
  110.6 0.8 pad.129
  111.4 3.9 %all-to-all-start.3 = ((f32[32,4,512]{2,1,0:T(4,128)}), f32[32,4,512]{2,1,0:T(4,128)S(1)}, u32[]{:S(2)}, u32[]{:S(2)}) async-start(f32[32,4,512]{2,1,0:T(4,128)} %pad.129), calls=%async_computation.3 | async-start | bytes 524288 | tf_op jit(solution)/shard_map/all_to_all | solution.py:135
  115.4 1.1 fusion.35
  116.5 7.8 %all-to-all-done.3 = f32[32,4,512]{2,1,0:T(4,128)S(1)} async-done(((f32[32,4,512]{2,1,0:T(4,128)}), f32[32,4,512]{2,1,0:T(4,128)S(1)}, u32[]{:S(2)}, u32[]{:S(2)}) %all-to-all-start.3) | async-done | bytes 262176 | tf_op jit(solution)/shard_map/all_to_all | solution.py:135
  125.1 3.8 %convolution_bitcast_fusion = f32[9,128,256]{1,2,0:T(8,128)S(1)} fusion(bf16[2,9,256,512]{3,2,0,1:T(8,128)(2,1)} %fusion.35, f32[2,128,512]{2,1,0:T(8,128)S(1)} %get-tuple-element.139, f32[128,512]{1,0:T(8,128)S(1)} %mul.237, f32[2,128]{1,0:T(2,128)S(1)} %broadcast_select_fusion.3), kind=kOutput, calls=%fused_computation.15 | convolution fusion | flops 604372992 | bytes 6685696 | tf_op jit(solution)/shard_map/fps,fkcs->kpc/dot_general | solution.py:146
  129.9 2.4 %fusion.4 = f32[9,64,512,1]{2,1,3,0:T(8,128)S(1)} fusion(bf16[2,9,64,512]{3,2,0,1:T(8,128)(2,1)} %fusion.65, bf16[2,512,512]{2,1,0:T(8,128)(2,1)} %all-gather.2.cloned.1.call-done), kind=kOutput, calls=%fused_computation.28 | convolution fusion | flops 603979776 | bytes 3407872 | tf_op jit(solution)/shard_map/fkus,fps->kup/dot_general | solution.py:150
  133.3 2.5 %collective-permute-done = f32[294912]{0:T(1024)S(1)} collective-permute-done((f32[294912]{0:T(1024)S(1)}, f32[294912]{0:T(1024)S(1)}, u32[]{:S(2)}, u32[]{:S(2)}) %collective-permute-start) | collective-permute-done | bytes 1179680 | tf_op jit(solution)/shard_map/ppermute | solution.py:90
  135.9 24.1 %all_to_all.49 = f32[16,1,18432]{2,1,0:T(1,128)S(1)} all-to-all(f32[16,1,18432]{2,1,0:T(1,128)S(1)} %bitcast.186), channel_id=1, replica_groups=mesh['chip'=16,'core'=2,'chan'=4] {'chip'}, dimensions={0} | all-to-all | bytes 2359296 | tf_op jit(solution)/shard_map/all_to_all | solution.py:91
  161.4 19.8 %all_to_all.48 = f32[16,1,18432]{2,1,0:T(1,128)S(1)} all-to-all(f32[16,1,18432]{2,1,0:T(1,128)S(1)} %broadcast_in_dim.121), channel_id=1, replica_groups=mesh['chip'=16,'core'=2,'chan'=4] {'chip'}, dimensions={0} | all-to-all | bytes 2359296 | tf_op jit(solution)/shard_map/all_to_all | solution.py:93
  181.2 3.0 %collective-permute-start.1 = (f32[294912]{0:T(1024)S(1)}, f32[294912]{0:T(1024)}, u32[]{:S(2)}, u32[]{:S(2)}) collective-permute-start(f32[294912]{0:T(1024)S(1)} %bitcast.184), channel_id=1, source_target_pairs={{0,4},{4,0},{1,5},{5,1},{2,6},{6,2},{3,7},{7,3},{8,12},{12,8},{9,1... | collective-permute-start | bytes 3538952 | tf_op jit(solution)/shard_map/ppermute | solution.py:94
  184.1 0.8 broadcast_in_dim_reshape.2
  185.0 1.7 fusion.36
  186.7 2.4 %broadcast_select_fusion = (f32[294912]{0:T(1024)S(1)}, f32[294912]{0:T(1024)}) fusion(f32[294912]{0:T(1024)} %collective-permute-done.1, f32[294912]{0:T(1024)S(1)} %bitcast.185, pred[]{:T(512)S(6)} %eq.25), kind=kLoop, calls=%fused_computation.36 | loop fusion | flops 589824 | bytes 4718593 | tf_op jit(solution)/shard_map/jit(_where)/select_n | solution.py:96
  189.2 2.5 %reshape.86 = f32[9,128,256]{2,1,0:T(8,128)} reshape(f32[294912]{0:T(1024)} %get-tuple-element.254) | data formatting | bytes 2359296 | tf_op jit(solution)/shard_map/reshape | solution.py:97
  191.7 1.2 reshape.87
  (148 shorter events, 16.0 us)
Async XLA Ops:
  7.2 1.8 copy-start
  8.8 0.7 copy-start.12
  11.2 0.7 copy-start.10
  12.5 1.2 copy-start.7
  12.6 10.6 %copy-start.2 = (bf16[2,64,512]{2,1,0:T(8,128)(2,1)S(1)}, bf16[2,64,512]{2,1,0:T(8,128)(2,1)}, u32[]{:S(2)}) copy-start(bf16[2,64,512]{2,1,0:T(8,128)(2,1)} %param.13) | copy-start | bytes 393220
  13.8 42.5 %all-to-all-start = ((f32[32,5,512]{2,1,0:T(8,128)}), f32[32,5,512]{2,1,0:T(8,128)S(1)}, u32[]{:S(2)}, u32[]{:S(2)}) async-start(f32[32,5,512]{2,1,0:T(8,128)} %pad_maximum_fusion.1), calls=%async_computation | async-start | bytes 1048576 | tf_op jit(solution)/shard_map/all_to_all | solution.py:116
  35.0 1.1 copy-start.9
  38.9 4.0 %copy-start.1 = (bf16[2,256,512]{2,1,0:T(8,128)(2,1)S(1)}, bf16[2,256,512]{2,1,0:T(8,128)(2,1)}, u32[]{:S(2)}) copy-start(bf16[2,256,512]{2,1,0:T(8,128)(2,1)} %param.9) | copy-start | bytes 1572868
  56.3 10.9 %all-to-all-start.1 = ((bf16[4,2,36864]{2,1,0:T(2,128)(2,1)}), bf16[4,2,36864]{2,1,0:T(2,128)(2,1)S(1)}, u32[]{:S(2)}, u32[]{:S(2)}) async-start(bf16[4,2,36864]{2,1,0:T(2,128)(2,1)} %reshape.112), calls=%async_computation.1 | async-start | bytes 1179648 | tf_op jit(solution)/shard_map/all_to_all | solution.py:119
  72.7 0.7 copy-start.13
  78.4 28.3 %all-to-all-start.2 = ((f32[32,9,512]{2,1,0:T(8,128)}), f32[32,9,512]{2,1,0:T(8,128)S(1)}, u32[]{:S(2)}, u32[]{:S(2)}) async-start(f32[32,9,512]{2,1,0:T(8,128)} %pad_maximum_fusion), calls=%async_computation.2 | async-start | bytes 2097152 | tf_op jit(solution)/shard_map/all_to_all | solution.py:130
  89.8 40.1 %all-gather.2.cloned.1.call-start = ((), (), s32[]{:S(2)}) async-start(), calls=%async_computation.6 | async-start | bytes 1310720 | tf_op jit(solution)/shard_map/all_gather | solution.py:149
  107.5 2.2 %copy-start.3 = (f32[32,4,512]{2,1,0:T(4,128)}, f32[32,4,512]{2,1,0:T(4,128)S(1)}, u32[]{:S(2)}) copy-start(f32[32,4,512]{2,1,0:T(4,128)S(1)} %get-tuple-element.256) | copy-start | bytes 786436
  110.4 5.0 %copy-start.11 = (pred[2]{0:T(512)(128)(4,1)S(1)}, pred[2]{0:T(512)(128)(4,1)}, u32[]{:S(2)}) copy-start(pred[2]{0:T(512)(128)(4,1)} %constant.143.clone.1) | copy-start | bytes 10
  111.4 12.9 %all-to-all-start.3 = ((f32[32,4,512]{2,1,0:T(4,128)}), f32[32,4,512]{2,1,0:T(4,128)S(1)}, u32[]{:S(2)}, u32[]{:S(2)}) async-start(f32[32,4,512]{2,1,0:T(4,128)} %pad.129), calls=%async_computation.3 | async-start | bytes 524288 | tf_op jit(solution)/shard_map/all_to_all | solution.py:135
  124.4 0.7 copy-start.5
  132.8 2.9 %collective-permute-start = (f32[294912]{0:T(1024)S(1)}, f32[294912]{0:T(1024)S(1)}, u32[]{:S(2)}, u32[]{:S(2)}) collective-permute-start(f32[294912]{0:T(1024)S(1)} %broadcast_select_fusion.2), channel_id=1, source_target_pairs={{0,4},{4,0},{1,5},{5,1},{2,6},{6,2},{3,7},{7,3},{8,12},{12,8},{9,1... | collective-permute-start | bytes 3538952 | tf_op jit(solution)/shard_map/ppermute | solution.py:90
  161.3 22.8 %copy-start.4 = (f32[32,4,512]{2,1,0:T(4,128)S(1)}, f32[32,4,512]{2,1,0:T(4,128)}, u32[]{:S(2)}) copy-start(f32[32,4,512]{2,1,0:T(4,128)} %copy-done.3) | copy-start | bytes 786436
  161.3 23.6 %copy-start.8 = (f32[2,128,512]{2,1,0:T(8,128)S(1)}, f32[2,128,512]{2,1,0:T(8,128)}, u32[]{:S(2)}) copy-start(f32[2,128,512]{2,1,0:T(8,128)} %get-tuple-element.252) | copy-start | bytes 1572868
  161.3 23.6 %copy-start.6 = (f32[128,512]{1,0:T(8,128)S(1)}, f32[128,512]{1,0:T(8,128)}, u32[]{:S(2)}) copy-start(f32[128,512]{1,0:T(8,128)} %copy-done.5) | copy-start | bytes 786436
  181.2 5.6 %collective-permute-start.1 = (f32[294912]{0:T(1024)S(1)}, f32[294912]{0:T(1024)}, u32[]{:S(2)}, u32[]{:S(2)}) collective-permute-start(f32[294912]{0:T(1024)S(1)} %bitcast.184), channel_id=1, source_target_pairs={{0,4},{4,0},{1,5},{5,1},{2,6},{6,2},{3,7},{7,3},{8,12},{12,8},{9,1... | collective-permute-start | bytes 3538952 | tf_op jit(solution)/shard_map/ppermute | solution.py:94
Sparse Core Ops, SparseCore 0:
  109.8 17.7 all-gather.1

commit v8 on v6

--- a/solution.py
+++ b/solution.py
@@ -83,14 +83,16 @@
 
 def pair_then_chip_sum(first, second):
     core = lax.axis_index("core")
+    chips = lax.axis_size("chip")
     swap = [(0, 1), (1, 0)]
-    first_flat, second_flat = first.reshape(-1), second.reshape(-1)
-    kept = jnp.where(core == 0, first_flat, second_flat)
-    sent = jnp.where(core == 0, second_flat, first_flat)
-    pair_sum = (kept + lax.ppermute(sent, "core", swap)).reshape(lax.axis_size("chip"), -1)
+    shape = (chips, first.size // (chips * first.shape[-1]), first.shape[-1])
+    first_rows, second_rows = first.reshape(shape), second.reshape(shape)
+    kept = jnp.where(core == 0, first_rows, second_rows)
+    sent = jnp.where(core == 0, second_rows, first_rows)
+    pair_sum = kept + lax.ppermute(sent, "core", swap)
     pieces = lax.all_to_all(pair_sum, "chip", 0, 0, tiled=True)
     reduced = jnp.sum(pieces, axis=0, keepdims=True)
-    total = lax.all_to_all(jnp.broadcast_to(reduced, pieces.shape), "chip", 0, 0, tiled=True).reshape(-1)
+    total = lax.all_to_all(jnp.broadcast_to(reduced, pieces.shape), "chip", 0, 0, tiled=True)
     partner = lax.ppermute(total, "core", swap)
     first_total = jnp.where(core == 0, total, partner)
     second_total = jnp.where(core == 0, partner, total)

time: 172 us -> 177 us (1.029)
  other arithmetic: 26.7 us -> 32 us
  local copies, waits for them, and re-layouts: 17 us -> 12 us
  starting transfers between devices: 24.4 us -> 26.2 us
    unnamed x18, other arithmetic: 13.8 us -> 19.1 us
    unnamed x38 -> x30, local copies, waits for them, and re-layouts: 4.42 us -> 2.49 us
    ppermute x1, starting transfers between devices: 0.29 us -> 2.1 us  [pair_then_chip_sum(): pair_sum = kept + lax.ppermute(sent, 'core', swap)]
  transfers between devices with their start and end apart: 7 -> 7, of which waited for: 5 -> 5; matrix products, arithmetic and copies ran while one was open for 16% -> 14% of each run, Pallas kernels for 0% -> 0%
where the time goes in v8:
time: 177 us; the launch traced here: 176 us
  blocking collectives  43.9 us (25%)
  waiting for transfers between devices  34.3 us (19%)
  other arithmetic  32 us (18%)
  starting transfers between devices  26.2 us (15%)
  between operations  14.6 us (8%)
  matrix products  12.7 us (7%)
  local copies, waits for them, and re-layouts  12 us (7%)
    all_to_all x1, blocking collectives, pair_then_chip_sum(): pieces = lax.all_to_all(pair_sum, 'chip', 0, 0, tiled=True)  24.1 us
    all_to_all x1, blocking collectives, pair_then_chip_sum(): lax.all_to_all(jnp.broadcast_to(reduced, pieces.shape), 'chip', 0, 0, til...  19.8 us
    unnamed x18, other arithmetic  19.1 us
    all_to_all x1, waiting for transfers between devices, body(): lax.all_to_all(jnp.concatenate([entering_owned, pack_chunks(decay_total,...  13.6 us
    all_to_all x1, starting transfers between devices, body(): lax.all_to_all(pack_chunks(decay_total, local_end, blocks), FRAME_AXES, 0...  9.43 us
    all_to_all x1, waiting for transfers between devices, body(): lax.all_to_all(arriving_owned, FRAME_AXES, 0, 0, tiled=True)  7.82 us
    all_to_all x1, starting transfers between devices, body(): lax.all_to_all(jnp.concatenate([entering_owned, pack_chunks(decay_total,...  7.72 us
    all_to_all x1, waiting for transfers between devices, body(): lax.all_to_all(pack_chunks(decay_total, local_end, blocks), FRAME_AXES, 0...  6.28 us
  transfers between devices with their start and end apart: 7, of which 5 were waited for; matrix products, arithmetic and copies ran while one was open for 14% of the time, Pallas kernels for 0%

profile of v8, /device:TPU:1, one launch (start us, length us, event | category | flops | bytes accessed | tf_op | source)
XLA Modules:
  0.0 175.8 jit_solution(7630881423396523398)
XLA Ops:
  7.3 1.7 fusion.41
  9.0 1.7 fusion.44
  10.7 1.7 fusion.47
  12.3 1.7 fusion.50
  14.0 1.6 bitcast_dynamic-update-slice_fusion.3
  15.6 0.8 fusion.53
  16.3 0.8 fusion.56
  17.1 0.8 fusion.59
  17.9 0.8 fusion.62
  18.6 3.6 %convolution_bitcast_fusion = f32[512,2,512]{0,2,1:T(8,128)} fusion(bf16[2,9,64,512]{3,2,1,0:T(8,128)(2,1)} %fusion.62, bf16[9,64,512]{2,1,0:T(8,128)(2,1)S(1)} %copy-done), kind=kOutput, calls=%fused_computation.12 | convolution fusion | flops 603979776 | bytes 3866624 | tf_op jit(solution)/shard_map/kup,fkus->pfs/dot_general | solution.py:121
  22.3 0.6 copy-done.9
  24.0 0.9 copy-done.11
  24.9 1.5 convolution_select_fusion
  27.6 0.9 pad_maximum_fusion.1
  28.5 9.4 %all-to-all-start = ((f32[32,5,512]{2,1,0:T(8,128)}), f32[32,5,512]{2,1,0:T(8,128)S(1)}, u32[]{:S(2)}, u32[]{:S(2)}) async-start(f32[32,5,512]{2,1,0:T(8,128)} %pad_maximum_fusion.1), calls=%async_computation | async-start | bytes 1048576 | tf_op jit(solution)/shard_map/all_to_all | solution.py:118
  37.9 1.0 fusion.10
  39.0 1.1 fusion.13
  40.1 1.1 fusion.16
  41.2 1.1 fusion.19
  42.4 0.9 bitcast_dynamic-update-slice_fusion.2
  43.3 6.3 %all-to-all-done = f32[32,5,512]{2,1,0:T(8,128)S(1)} async-done(((f32[32,5,512]{2,1,0:T(8,128)}), f32[32,5,512]{2,1,0:T(8,128)S(1)}, u32[]{:S(2)}, u32[]{:S(2)}) %all-to-all-start) | async-done | bytes 327712 | tf_op jit(solution)/shard_map/all_to_all | solution.py:118
  51.3 4.0 %reduce-scatter.2.cloned.1.call-done = f32[128,2,512]{0,2,1:T(8,128)} async-done(((f32[512,2,512]{0,2,1:T(8,128)}), f32[128,2,512]{0,2,1:T(8,128)}) %reduce-scatter.2.cloned.1.call-update) | async-done | bytes 524304 | tf_op jit(solution)/shard_map/reduce_scatter | solution.py:120
  55.4 2.6 %while.31 = (s32[]{:T(128)}, f32[128,512]{1,0:T(8,128)S(1)}, f32[2,128,512]{2,1,0:T(8,128)S(1)}, f32[2,128]{1,0:T(2,128)S(1)}, f32[2,128,512]{1,2,0:T(8,128)}, /*index=5*/s32[]{:T(128)}, s32[]{:T(128)}) while((s32[]{:T(128)}, f32[128,512]{1,0:T(8,128)S(1)}, f32[2,128,512]{2,1,0:T(8,128)S(1)}, f32[2,128]{1,0:T(2,128)S(1)}, ...), condition=%wide.region_5.6_spmd.clone, body=%wide.region_4.5_spmd.clone.sunk | while | flops 327684 | bytes 2623096 | solution.py:134
  55.4 1.0 constant_dynamic-slice_fusion.7
  56.7 1.0 constant_dynamic-slice_fusion.7
  58.1 1.1 pad_maximum_fusion
  59.2 7.7 %all-to-all-start.1 = ((f32[32,9,512]{2,1,0:T(8,128)}), f32[32,9,512]{2,1,0:T(8,128)S(1)}, u32[]{:S(2)}, u32[]{:S(2)}) async-start(f32[32,9,512]{2,1,0:T(8,128)} %pad_maximum_fusion), calls=%async_computation.2 | async-start | bytes 2097152 | tf_op jit(solution)/shard_map/all_to_all | solution.py:136
  67.0 1.1 fusion.22
  68.2 1.1 fusion.25
  69.2 1.1 fusion.28
  70.3 13.6 %all-to-all-done.1 = f32[32,9,512]{2,1,0:T(8,128)S(1)} async-done(((f32[32,9,512]{2,1,0:T(8,128)}), f32[32,9,512]{2,1,0:T(8,128)S(1)}, u32[]{:S(2)}, u32[]{:S(2)}) %all-to-all-start.1) | async-done | bytes 589856 | tf_op jit(solution)/shard_map/all_to_all | solution.py:136
  84.7 2.0 %fusion.71 = (bf16[2,128,512]{2,1,0:T(8,128)(2,1)}, f32[2,128,512]{2,1,0:T(8,128)}) fusion(f32[2,128,512]{2,1,0:T(8,128)} %copy-done.7, f32[128,512]{1,0:T(8,128)S(1)} %mul.241, f32[2,128]{1,0:T(2,128)S(1)} %reduce_window.16), kind=kLoop, calls=%fused_computation.138 | loop fusion | flops 393216 | bytes 1573888 | tf_op jit(solution)/shard_map/convert_element_type | solution.py:145
  87.8 0.8 pad.130
  88.5 3.9 %all-to-all-start.2 = ((f32[32,4,512]{2,1,0:T(4,128)}), f32[32,4,512]{2,1,0:T(4,128)S(1)}, u32[]{:S(2)}, u32[]{:S(2)}) async-start(f32[32,4,512]{2,1,0:T(4,128)} %pad.130), calls=%async_computation.3 | async-start | bytes 524288 | tf_op jit(solution)/shard_map/all_to_all | solution.py:141
  92.6 1.1 fusion.31
  93.6 7.8 %all-to-all-done.2 = f32[32,4,512]{2,1,0:T(4,128)S(1)} async-done(((f32[32,4,512]{2,1,0:T(4,128)}), f32[32,4,512]{2,1,0:T(4,128)S(1)}, u32[]{:S(2)}, u32[]{:S(2)}) %all-to-all-start.2) | async-done | bytes 262176 | tf_op jit(solution)/shard_map/all_to_all | solution.py:141
  101.5 4.1 %fusion.35 = f32[9,256,128,1]{1,2,3,0:T(8,128)S(1)} fusion(bf16[2,9,256,512]{3,2,0,1:T(8,128)(2,1)} %fusion.31, f32[2,128,512]{2,1,0:T(8,128)S(1)} %get-tuple-element.139, f32[128,512]{1,0:T(8,128)S(1)} %mul.237, f32[2,128]{1,0:T(2,128)S(1)} %broadcast_select_fusion.3), kind=kOutput, calls=%fused_computation.76 | convolution fusion | flops 604372992 | bytes 6685696 | tf_op jit(solution)/shard_map/fps,fkcs->kpc/dot_general | solution.py:152
  105.7 3.4 %convolution_bitcast_fusion.1 = f32[9,64,512]{2,1,0:T(8,128)} fusion(bf16[2,9,64,512]{3,2,1,0:T(8,128)(2,1)} %fusion.62, bf16[2,512,512]{2,1,0:T(8,128)(2,1)} %all-gather.2.cloned.1.call-done), kind=kOutput, calls=%fused_computation.15 | convolution fusion | flops 603979776 | bytes 3407872 | tf_op jit(solution)/shard_map/fkus,fps->kup/dot_general | solution.py:156
  109.1 1.4 reshape.59
  110.7 2.1 %collective-permute-start = (f32[16,72,256]{2,1,0:T(8,128)S(1)}, f32[16,72,256]{2,1,0:T(8,128)S(1)}, u32[]{:S(2)}, u32[]{:S(2)}) collective-permute-start(f32[16,72,256]{2,1,0:T(8,128)S(1)} %broadcast_select_fusion.2), channel_id=1, source_target_pairs={{0,4},{4,0},{1,5},{5,1},{2,6},{6,2},{3,7},{7,3},{8,12},{12,8},{9,1... | collective-permute-start | bytes 3538952 | tf_op jit(solution)/shard_map/ppermute | solution.py:92
  112.8 2.5 %collective-permute-done = f32[16,72,256]{2,1,0:T(8,128)S(1)} collective-permute-done((f32[16,72,256]{2,1,0:T(8,128)S(1)}, f32[16,72,256]{2,1,0:T(8,128)S(1)}, u32[]{:S(2)}, u32[]{:S(2)}) %collective-permute-start) | collective-permute-done | bytes 1179680 | tf_op jit(solution)/shard_map/ppermute | solution.py:92
  115.5 24.1 %all_to_all.26 = f32[16,72,256]{2,1,0:T(8,128)S(1)} all-to-all(f32[16,72,256]{2,1,0:T(8,128)S(1)} %select_add_fusion), channel_id=1, replica_groups=mesh['chip'=16,'core'=2,'chan'=4] {'chip'}, dimensions={0} | all-to-all | bytes 2359296 | tf_op jit(solution)/shard_map/all_to_all | solution.py:93
  139.8 19.8 %all_to_all.25 = f32[16,72,256]{2,1,0:T(8,128)S(1)} all-to-all(f32[16,72,256]{2,1,0:T(8,128)S(1)} %broadcast_in_dim.121), channel_id=1, replica_groups=mesh['chip'=16,'core'=2,'chan'=4] {'chip'}, dimensions={0} | all-to-all | bytes 2359296 | tf_op jit(solution)/shard_map/all_to_all | solution.py:95
  159.6 3.0 %collective-permute-start.1 = (f32[16,72,256]{2,1,0:T(8,128)S(1)}, f32[16,72,256]{2,1,0:T(8,128)}, u32[]{:S(2)}, u32[]{:S(2)}) collective-permute-start(f32[16,72,256]{2,1,0:T(8,128)S(1)} %all_to_all.25), channel_id=1, source_target_pairs={{0,4},{4,0},{1,5},{5,1},{2,6},{6,2},{3,7},{7,3},{8,12},{12,8},{9,1... | collective-permute-start | bytes 3538952 | tf_op jit(solution)/shard_map/ppermute | solution.py:96
  162.6 0.8 broadcast_in_dim_reshape.2
  163.4 1.7 fusion.32
  165.2 2.5 %broadcast_select_fusion = (f32[16,72,256]{2,1,0:T(8,128)S(1)}, f32[16,72,256]{2,1,0:T(8,128)}) fusion(f32[16,72,256]{2,1,0:T(8,128)} %collective-permute-done.1, f32[16,72,256]{2,1,0:T(8,128)S(1)} %all_to_all.25, pred[]{:T(512)S(6)} %eq.25), kind=kLoop, calls=%fused_computation.32 | loop fusion | flops 589824 | bytes 4718593 | tf_op jit(solution)/shard_map/jit(_where)/select_n | solution.py:98
  167.6 1.3 reshape.61
  (128 shorter events, 7.7 us)
Async XLA Ops:
  7.2 11.5 %copy-start = (bf16[9,64,512]{2,1,0:T(8,128)(2,1)S(1)}, bf16[9,64,512]{2,1,0:T(8,128)(2,1)}, u32[]{:S(2)}) copy-start(bf16[9,64,512]{2,1,0:T(8,128)(2,1)} %param.12) | copy-start | bytes 1769476
  7.2 8.4 %copy-start.2 = (bf16[2,64,512]{2,1,0:T(8,128)(2,1)S(1)}, bf16[2,64,512]{2,1,0:T(8,128)(2,1)}, u32[]{:S(2)}) copy-start(bf16[2,64,512]{2,1,0:T(8,128)(2,1)} %param.13) | copy-start | bytes 393220
  7.2 48.1 %reduce-scatter.2.cloned.1.call-start = ((), (), s32[]{:S(2)}) async-start(), calls=%async_computation.6 | async-start | bytes 2621440 | tf_op jit(solution)/shard_map/reduce_scatter | solution.py:120
  22.3 0.7 copy-start.9
  22.3 1.1 copy-start.1
  23.8 1.1 copy-start.11
  23.9 1.1 copy-start.12
  27.5 15.7 %copy-start.7 = (f32[2,128,512]{2,1,0:T(8,128)}, f32[2,128,512]{2,1,0:T(8,128)S(1)}, u32[]{:S(2)}) copy-start(f32[2,128,512]{2,1,0:T(8,128)S(1)} %get-tuple-element.142) | copy-start | bytes 1572868
  28.5 21.0 %all-to-all-start = ((f32[32,5,512]{2,1,0:T(8,128)}), f32[32,5,512]{2,1,0:T(8,128)S(1)}, u32[]{:S(2)}, u32[]{:S(2)}) async-start(f32[32,5,512]{2,1,0:T(8,128)} %pad_maximum_fusion.1), calls=%async_computation | async-start | bytes 1048576 | tf_op jit(solution)/shard_map/all_to_all | solution.py:118
  59.2 24.6 %all-to-all-start.1 = ((f32[32,9,512]{2,1,0:T(8,128)}), f32[32,9,512]{2,1,0:T(8,128)S(1)}, u32[]{:S(2)}, u32[]{:S(2)}) async-start(f32[32,9,512]{2,1,0:T(8,128)} %pad_maximum_fusion), calls=%async_computation.2 | async-start | bytes 2097152 | tf_op jit(solution)/shard_map/all_to_all | solution.py:136
  66.9 38.8 %all-gather.2.cloned.1.call-start = ((), (), s32[]{:S(2)}) async-start(), calls=%async_computation.7 | async-start | bytes 1310720 | tf_op jit(solution)/shard_map/all_gather | solution.py:155
  84.6 2.2 %copy-start.5 = (f32[32,4,512]{2,1,0:T(4,128)}, f32[32,4,512]{2,1,0:T(4,128)S(1)}, u32[]{:S(2)}) copy-start(f32[32,4,512]{2,1,0:T(4,128)S(1)} %get-tuple-element.221) | copy-start | bytes 786436
  87.5 5.0 %copy-start.10 = (pred[2]{0:T(512)(128)(4,1)S(1)}, pred[2]{0:T(512)(128)(4,1)}, u32[]{:S(2)}) copy-start(pred[2]{0:T(512)(128)(4,1)} %constant.143.clone.1) | copy-start | bytes 10
  88.5 12.9 %all-to-all-start.2 = ((f32[32,4,512]{2,1,0:T(4,128)}), f32[32,4,512]{2,1,0:T(4,128)S(1)}, u32[]{:S(2)}, u32[]{:S(2)}) async-start(f32[32,4,512]{2,1,0:T(4,128)} %pad.130), calls=%async_computation.3 | async-start | bytes 524288 | tf_op jit(solution)/shard_map/all_to_all | solution.py:141
  101.5 4.1 %copy-start.3 = (f32[128,512]{1,0:T(8,128)}, f32[128,512]{1,0:T(8,128)S(1)}, u32[]{:S(2)}) copy-start(f32[128,512]{1,0:T(8,128)S(1)} %mul.237) | copy-start | bytes 786436
  110.7 4.6 %collective-permute-start = (f32[16,72,256]{2,1,0:T(8,128)S(1)}, f32[16,72,256]{2,1,0:T(8,128)S(1)}, u32[]{:S(2)}, u32[]{:S(2)}) collective-permute-start(f32[16,72,256]{2,1,0:T(8,128)S(1)} %broadcast_select_fusion.2), channel_id=1, source_target_pairs={{0,4},{4,0},{1,5},{5,1},{2,6},{6,2},{3,7},{7,3},{8,12},{12,8},{9,1... | collective-permute-start | bytes 3538952 | tf_op jit(solution)/shard_map/ppermute | solution.py:92
  139.8 22.8 %copy-start.6 = (f32[32,4,512]{2,1,0:T(4,128)S(1)}, f32[32,4,512]{2,1,0:T(4,128)}, u32[]{:S(2)}) copy-start(f32[32,4,512]{2,1,0:T(4,128)} %copy-done.5) | copy-start | bytes 786436
  139.8 23.6 %copy-start.8 = (f32[2,128,512]{2,1,0:T(8,128)S(1)}, f32[2,128,512]{2,1,0:T(8,128)}, u32[]{:S(2)}) copy-start(f32[2,128,512]{2,1,0:T(8,128)} %get-tuple-element.217) | copy-start | bytes 1572868
  139.8 23.6 %copy-start.4 = (f32[128,512]{1,0:T(8,128)S(1)}, f32[128,512]{1,0:T(8,128)}, u32[]{:S(2)}) copy-start(f32[128,512]{1,0:T(8,128)} %copy-done.3) | copy-start | bytes 786436
  159.6 5.6 %collective-permute-start.1 = (f32[16,72,256]{2,1,0:T(8,128)S(1)}, f32[16,72,256]{2,1,0:T(8,128)}, u32[]{:S(2)}, u32[]{:S(2)}) collective-permute-start(f32[16,72,256]{2,1,0:T(8,128)S(1)} %all_to_all.25), channel_id=1, source_target_pairs={{0,4},{4,0},{1,5},{5,1},{2,6},{6,2},{3,7},{7,3},{8,12},{12,8},{9,1... | collective-permute-start | bytes 3538952 | tf_op jit(solution)/shard_map/ppermute | solution.py:96
Sparse Core Ops, SparseCore 0:
  22.4 32.8 reduce-scatter.1
  86.9 17.9 all-gather.1

commit v9 on v7

--- a/solution.py
+++ b/solution.py
@@ -78,6 +78,13 @@
     return out.reshape(frames, kernel.shape[1], cells)
 
 
+def gather_by_all_to_all(value, axis):
+    count = lax.axis_size(axis)
+    copies = jnp.broadcast_to(value[None], (count, *value.shape))
+    blocks = jnp.moveaxis(lax.all_to_all(copies, axis, 0, 0, tiled=True), 0, 1)
+    return blocks.reshape(value.shape[0], count * value.shape[1], *value.shape[2:])
+
+
 FRAME_AXES = ("chip", "core")
 
 
@@ -115,9 +122,13 @@
     chunk = rows // blocks
     entering_owned = scan_owned(lax.all_to_all(pack_chunks(decay_total, local_end, blocks), FRAME_AXES, 0, 0, tiled=True), False)
     cot_stack = stencil_stack(cotangent, W, -1)
-    all_cotangent = lax.all_gather(cotangent, "chan", axis=1, tiled=True)
-    readout_local = lax.all_to_all(kernel_c, "chan", 2, 1, tiled=True)
-    injected = stencil_conv(all_cotangent, jnp.flip(readout_local, 0).transpose(0, 2, 1), W)
+    chans = lax.axis_size("chan")
+    taps, outs, states_local = kernel_c.shape[0], kernel_c.shape[1], kernel_b.shape[1]
+    readout_blocks = jnp.moveaxis(kernel_c.reshape(taps, outs, chans, states_local), 2, 0)
+    readout_local = lax.all_to_all(readout_blocks, "chan", 0, 0, tiled=True)
+    readout_local = readout_local.transpose(1, 3, 0, 2).reshape(taps, states_local, chans * outs)
+    all_cotangent = gather_by_all_to_all(cotangent, "chan")
+    injected = stencil_conv(all_cotangent, jnp.flip(readout_local, 0), W)
     entering_owned, injected = lax.optimization_barrier((entering_owned, injected))
 
     def retreat(carried, frame_pair):
@@ -146,7 +157,7 @@
     grad_b_part = jnp.einsum(
         "fps,fkcs->kpc", adjoint_bf, input_stack, preferred_element_type=jnp.float32
     )
-    all_states = lax.all_gather(states_bf, "chan", axis=1, tiled=True)
+    all_states = gather_by_all_to_all(states_bf, "chan")
     grad_c_part = jnp.einsum(
         "fkus,fps->kup", cot_stack, all_states, preferred_element_type=jnp.float32
     )

time: 201 us -> 184 us (0.915)
  waiting for transfers between devices: 29.8 us -> 44.7 us
  blocking collectives: 55 us -> 40.2 us
  between operations: 14.7 us -> 1.42 us
  other arithmetic: 28.9 us -> 23.7 us
  starting transfers between devices: 31.8 us -> 35.9 us
    all_to_all x1 -> x3, waiting for transfers between devices: 5.55 us -> 18.7 us  [the longest x2 16.5 us: gather_by_all_to_all(): blocks = jnp.moveaxis(lax.all_to_all(copies, axis, 0, 0, tiled=True), 0, 1)]
    all_gather x1 -> x0, blocking collectives: 11.1 us -> none  [body(): all_cotangent = lax.all_gather(cotangent, 'chan', axis=1, tiled=True)]
    all_to_all x1 -> x3, starting transfers between devices: 3.6 us -> 12 us  [the longest x2 8.55 us: gather_by_all_to_all(): blocks = jnp.moveaxis(lax.all_to_all(copies, axis, 0, 0, tiled=True), 0, 1)]
    unnamed x39 -> x47, local copies, waits for them, and re-layouts: 15.4 us -> 8.48 us
    all_to_all x1, starting transfers between devices: 11.4 us -> 6.48 us  [body(): lax.all_to_all(jnp.concatenate([entering_owned, pack_chunks(decay_total,...]
    unnamed x18, other arithmetic: 14.5 us -> 10.4 us
    all_to_all x1, blocking collectives: 24.1 us -> 20.3 us  [pair_then_chip_sum(): pieces = lax.all_to_all(pair_sum, 'chip', 0, 0, tiled=True)]
    transpose x0 -> x3, local copies, waits for them, and re-layouts: none -> 3.14 us  [the longest x2 2.17 us: gather_by_all_to_all(): blocks = jnp.moveaxis(lax.all_to_all(copies, axis, 0, 0, tiled=True), 0, 1)]
  transfers between devices with their start and end apart: 7 -> 8, of which waited for: 4 -> 7; matrix products, arithmetic and copies ran while one was open for 18% -> 16% of each run, Pallas kernels for 0% -> 0%
where the time goes in v9:
time: 184 us; the launch traced here: 183 us
  waiting for transfers between devices  44.7 us (24%)
  blocking collectives  40.2 us (22%)
  starting transfers between devices  35.9 us (20%)
  local copies, waits for them, and re-layouts  27.1 us (15%)
  other arithmetic  23.7 us (13%)
  matrix products  10 us (5%)
    all_to_all x1, blocking collectives, pair_then_chip_sum(): pieces = lax.all_to_all(pair_sum, 'chip', 0, 0, tiled=True)  20.3 us
    all_to_all x1, blocking collectives, pair_then_chip_sum(): lax.all_to_all(jnp.broadcast_to(reduced, pieces.shape), 'chip', 0, 0, til...  19.8 us
    all_to_all x2, waiting for transfers between devices, gather_by_all_to_all(): blocks = jnp.moveaxis(lax.all_to_all(copies, axis, 0, 0, tiled=True), 0, 1)  16.5 us
    all_to_all x1, waiting for transfers between devices, body(): lax.all_to_all(jnp.concatenate([entering_owned, pack_chunks(decay_total,...  14 us
    unnamed x18, other arithmetic  10.4 us
    all_to_all x1, starting transfers between devices, body(): lax.all_to_all(pack_chunks(decay_total, local_end, blocks), FRAME_AXES, 0...  9.42 us
    all_to_all x2, starting transfers between devices, gather_by_all_to_all(): blocks = jnp.moveaxis(lax.all_to_all(copies, axis, 0, 0, tiled=True), 0, 1)  8.55 us
    unnamed x47, local copies, waits for them, and re-layouts  8.48 us
  transfers between devices with their start and end apart: 8, of which 7 were waited for; matrix products, arithmetic and copies ran while one was open for 16% of the time, Pallas kernels for 0%

profile of v9, /device:TPU:1, one launch (start us, length us, event | category | flops | bytes accessed | tf_op | source)
XLA Modules:
  0.0 183.1 jit_solution(6394500089734994743)
XLA Ops:
  0.7 1.3 copy.142
  2.9 1.5 convolution_select_fusion.1
  6.3 0.9 pad_maximum_fusion.1
  7.2 9.4 %all-to-all-start = ((f32[32,5,512]{2,1,0:T(8,128)}), f32[32,5,512]{2,1,0:T(8,128)S(1)}, u32[]{:S(2)}, u32[]{:S(2)}) async-start(f32[32,5,512]{2,1,0:T(8,128)} %pad_maximum_fusion.1), calls=%async_computation | async-start | bytes 1048576 | tf_op jit(solution)/shard_map/all_to_all | solution.py:123
  18.5 0.8 fusion.42
  23.7 0.8 fusion.60
  24.7 1.0 copy.160
  25.6 1.1 fusion.24
  26.7 1.6 all-to-all-done
  28.2 0.8 broadcast_in_dim.129
  29.1 4.2 %all-to-all-start.1 = ((bf16[4,2,64,512]{3,2,1,0:T(8,128)(2,1)}), bf16[4,2,64,512]{3,2,1,0:T(8,128)(2,1)S(1)}, u32[]{:S(2)}, u32[]{:S(2)}) async-start(bf16[4,2,64,512]{3,2,1,0:T(8,128)(2,1)} %broadcast_in_dim.129), calls=%async_computation.1 | async-start | bytes 1048576 | tf_op jit(solution)/shard_map/all_to_all | solution.py:84
  34.6 8.2 %all-to-all-done.1 = bf16[4,2,64,512]{3,2,1,0:T(8,128)(2,1)S(1)} async-done(((bf16[4,2,64,512]{3,2,1,0:T(8,128)(2,1)}), bf16[4,2,64,512]{3,2,1,0:T(8,128)(2,1)S(1)}, u32[]{:S(2)}, u32[]{:S(2)}) %all-to-all-start.1) | async-done | bytes 524320 | tf_op jit(solution)/shard_map/all_to_all | solution.py:84
  42.8 0.8 copy-done.10
  43.6 3.5 %all-to-all-start.2 = ((bf16[4,9,64,128]{3,2,1,0:T(8,128)(2,1)}), bf16[4,9,64,128]{3,2,1,0:T(8,128)(2,1)S(1)}, u32[]{:S(2)}, u32[]{:S(2)}) async-start(bf16[4,9,64,128]{3,2,1,0:T(8,128)(2,1)} %copy.160), calls=%async_computation.2 | async-start | bytes 1179648 | tf_op jit(solution)/shard_map/all_to_all | solution.py:128
  48.2 0.8 copy.157
  49.0 1.6 reshape_reshape.3
  50.7 1.6 copy.185
  52.3 1.1 pad.133.clone
  53.4 0.9 fusion.5
  54.3 2.2 %all-to-all-done.2 = bf16[4,9,64,128]{3,2,1,0:T(8,128)(2,1)S(1)} async-done(((bf16[4,9,64,128]{3,2,1,0:T(8,128)(2,1)}), bf16[4,9,64,128]{3,2,1,0:T(8,128)(2,1)S(1)}, u32[]{:S(2)}, u32[]{:S(2)}) %all-to-all-start.2) | async-done | bytes 589856 | tf_op jit(solution)/shard_map/all_to_all | solution.py:128
  56.6 0.9 rev.9
  57.9 2.6 %convolution_select_fusion = f32[8,16,9,128]{3,1,2,0:T(8,128)S(1)} fusion(bf16[3,3,128,256]{2,3,1,0:T(8,128)(2,1)} %bitcast.199, bf16[256,8,2,8,11]{0,1,4,3,2:T(8,128)(2,1)S(1)} %copy-done.15, pred[16,9]{0,1:T(8,128)(4,1)S(1)} %copy-done.19), kind=kOutput, calls=%fused_computation.16 | convolution fusion | flops 623001600 | bytes 1900688 | tf_op jit(solution)/shard_map/conv_general_dilated | solution.py:74
  61.7 1.1 pad_maximum_fusion
  62.9 6.5 %all-to-all-start.3 = ((f32[32,9,512]{2,1,0:T(8,128)}), f32[32,9,512]{2,1,0:T(8,128)S(1)}, u32[]{:S(2)}, u32[]{:S(2)}) async-start(f32[32,9,512]{2,1,0:T(8,128)} %pad_maximum_fusion), calls=%async_computation.3 | async-start | bytes 2097152 | tf_op jit(solution)/shard_map/all_to_all | solution.py:141
  69.4 0.8 fusion.63
  70.2 1.0 fusion.27
  71.3 1.0 fusion.30
  72.3 14.0 %all-to-all-done.3 = f32[32,9,512]{2,1,0:T(8,128)S(1)} async-done(((f32[32,9,512]{2,1,0:T(8,128)}), f32[32,9,512]{2,1,0:T(8,128)S(1)}, u32[]{:S(2)}, u32[]{:S(2)}) %all-to-all-start.3) | async-done | bytes 589856 | tf_op jit(solution)/shard_map/all_to_all | solution.py:141
  88.8 3.9 %all-to-all-start.4 = ((f32[32,4,512]{2,1,0:T(4,128)}), f32[32,4,512]{2,1,0:T(4,128)S(1)}, u32[]{:S(2)}, u32[]{:S(2)}) async-start(f32[32,4,512]{2,1,0:T(4,128)} %pad.129), calls=%async_computation.4 | async-start | bytes 524288 | tf_op jit(solution)/shard_map/all_to_all | solution.py:146
  92.8 0.9 fusion.72
  93.8 7.9 %all-to-all-done.4 = f32[32,4,512]{2,1,0:T(4,128)S(1)} async-done(((f32[32,4,512]{2,1,0:T(4,128)}), f32[32,4,512]{2,1,0:T(4,128)S(1)}, u32[]{:S(2)}, u32[]{:S(2)}) %all-to-all-start.4) | async-done | bytes 262176 | tf_op jit(solution)/shard_map/all_to_all | solution.py:146
  101.7 1.1 broadcast_in_dim.134
  102.7 4.4 %all-to-all-start.5 = ((bf16[4,2,128,512]{3,2,1,0:T(8,128)(2,1)}), bf16[4,2,128,512]{3,2,1,0:T(8,128)(2,1)}, u32[]{:S(2)}, u32[]{:S(2)}) async-start(bf16[4,2,128,512]{3,2,1,0:T(8,128)(2,1)} %broadcast_in_dim.134), calls=%async_computation.5 | async-start | bytes 2097152 | tf_op jit(solution)/shard_map/all_to_all | solution.py:84
  107.2 1.1 fusion.33
  109.0 3.8 %convolution_bitcast_fusion = f32[9,128,256]{1,2,0:T(8,128)S(1)} fusion(bf16[2,9,256,512]{3,2,0,1:T(8,128)(2,1)} %fusion.33, f32[2,128,512]{2,1,0:T(8,128)S(1)} %get-tuple-element.139, f32[128,512]{1,0:T(8,128)S(1)} %mul.237, f32[2,128]{1,0:T(2,128)S(1)} %broadcast_select_fusion.3), kind=kOutput, calls=%fused_computation.15 | convolution fusion | flops 604372992 | bytes 6685696 | tf_op jit(solution)/shard_map/fps,fkcs->kpc/dot_general | solution.py:157
  113.8 8.3 %all-to-all-done.5 = bf16[4,2,128,512]{3,2,1,0:T(8,128)(2,1)} async-done(((bf16[4,2,128,512]{3,2,1,0:T(8,128)(2,1)}), bf16[4,2,128,512]{3,2,1,0:T(8,128)(2,1)}, u32[]{:S(2)}, u32[]{:S(2)}) %all-to-all-start.5) | async-done | bytes 1048608 | tf_op jit(solution)/shard_map/all_to_all | solution.py:84
  122.2 1.3 copy.175
  123.5 2.1 %fusion.73 = f32[9,64,512,1]{2,1,3,0:T(8,128)S(1)} fusion(bf16[2,9,64,512]{3,2,0,1:T(8,128)(2,1)} %fusion.63, bf16[2,512,512,1]{2,1,0,3:T(8,128)(2,1)S(1)} %bitcast.198), kind=kOutput, calls=%fused_computation.141 | convolution fusion | flops 603979776 | bytes 3407872 | tf_op jit(solution)/shard_map/fkus,fps->kup/dot_general | solution.py:161
  126.0 1.1 collective-permute-start
  127.2 2.5 %collective-permute-done = f32[294912]{0:T(1024)S(1)} collective-permute-done((f32[294912]{0:T(1024)S(1)}, f32[294912]{0:T(1024)S(1)}, u32[]{:S(2)}, u32[]{:S(2)}) %collective-permute-start) | collective-permute-done | bytes 1179680 | tf_op jit(solution)/shard_map/ppermute | solution.py:97
  129.8 20.3 %all_to_all.46 = f32[16,1,18432]{2,1,0:T(1,128)S(1)} all-to-all(f32[16,1,18432]{2,1,0:T(1,128)S(1)} %bitcast.184), channel_id=1, replica_groups=mesh['chip'=16,'core'=2,'chan'=4] {'chip'}, dimensions={0} | all-to-all | bytes 2359296 | tf_op jit(solution)/shard_map/all_to_all | solution.py:98
  151.6 19.8 %all_to_all.45 = f32[16,1,18432]{2,1,0:T(1,128)S(1)} all-to-all(f32[16,1,18432]{2,1,0:T(1,128)S(1)} %broadcast_in_dim.135), channel_id=1, replica_groups=mesh['chip'=16,'core'=2,'chan'=4] {'chip'}, dimensions={0} | all-to-all | bytes 2359296 | tf_op jit(solution)/shard_map/all_to_all | solution.py:100
  171.4 3.0 %collective-permute-start.1 = (f32[294912]{0:T(1024)S(1)}, f32[294912]{0:T(1024)}, u32[]{:S(2)}, u32[]{:S(2)}) collective-permute-start(f32[294912]{0:T(1024)S(1)} %bitcast.182), channel_id=1, source_target_pairs={{0,4},{4,0},{1,5},{5,1},{2,6},{6,2},{3,7},{7,3},{8,12},{12,8},{9,1... | collective-permute-start | bytes 3538952 | tf_op jit(solution)/shard_map/ppermute | solution.py:101
  174.3 0.8 broadcast_in_dim_reshape.2
  175.2 1.7 fusion.34
  176.9 2.4 %broadcast_select_fusion = (f32[294912]{0:T(1024)S(1)}, f32[294912]{0:T(1024)}) fusion(f32[294912]{0:T(1024)} %collective-permute-done.1, f32[294912]{0:T(1024)S(1)} %bitcast.183, pred[]{:T(512)S(6)} %eq.25), kind=kLoop, calls=%fused_computation.34 | loop fusion | flops 589824 | bytes 4718593 | tf_op jit(solution)/shard_map/jit(_where)/select_n | solution.py:103
  179.4 2.5 %reshape.96 = f32[9,128,256]{2,1,0:T(8,128)} reshape(f32[294912]{0:T(1024)} %get-tuple-element.254) | data formatting | bytes 2359296 | tf_op jit(solution)/shard_map/reshape | solution.py:104
  181.9 1.2 reshape.97
  (161 shorter events, 20.7 us)
Async XLA Ops:
  0.6 1.8 copy-start
  2.3 0.7 copy-start.19
  4.7 0.7 copy-start.17
  6.0 1.2 copy-start.12
  6.1 10.6 %copy-start.1 = (bf16[2,256,512]{2,1,0:T(8,128)(2,1)S(1)}, bf16[2,256,512]{2,1,0:T(8,128)(2,1)}, u32[]{:S(2)}) copy-start(bf16[2,256,512]{2,1,0:T(8,128)(2,1)} %param.9) | copy-start | bytes 1572868
  7.2 21.0 %all-to-all-start = ((f32[32,5,512]{2,1,0:T(8,128)}), f32[32,5,512]{2,1,0:T(8,128)S(1)}, u32[]{:S(2)}, u32[]{:S(2)}) async-start(f32[32,5,512]{2,1,0:T(8,128)} %pad_maximum_fusion.1), calls=%async_computation | async-start | bytes 1048576 | tf_op jit(solution)/shard_map/all_to_all | solution.py:123
  17.6 0.9 copy-start.2
  18.5 5.3 %copy-start.3 = (bf16[2,9,256,512]{3,2,0,1:T(8,128)(2,1)}, bf16[2,9,256,512]{3,2,0,1:T(8,128)(2,1)S(1)}, u32[]{:S(2)}) copy-start(bf16[2,9,256,512]{3,2,0,1:T(8,128)(2,1)S(1)} %bitcast_dynamic-update-slice_fusion.2) | copy-start | bytes 14155780
  18.5 6.0 %copy-start.16 = (bf16[9,64,512]{2,1,0:T(8,128)(2,1)S(1)}, bf16[9,64,512]{2,1,0:T(8,128)(2,1)}, u32[]{:S(2)}) copy-start(bf16[9,64,512]{2,1,0:T(8,128)(2,1)} %param.12) | copy-start | bytes 1769476
  29.1 13.8 %all-to-all-start.1 = ((bf16[4,2,64,512]{3,2,1,0:T(8,128)(2,1)}), bf16[4,2,64,512]{3,2,1,0:T(8,128)(2,1)S(1)}, u32[]{:S(2)}, u32[]{:S(2)}) async-start(bf16[4,2,64,512]{3,2,1,0:T(8,128)(2,1)} %broadcast_in_dim.129), calls=%async_computation.1 | async-start | bytes 1048576 | tf_op jit(solution)/shard_map/all_to_all | solution.py:84
  42.8 0.8 copy-start.10
  43.6 12.9 %all-to-all-start.2 = ((bf16[4,9,64,128]{3,2,1,0:T(8,128)(2,1)}), bf16[4,9,64,128]{3,2,1,0:T(8,128)(2,1)S(1)}, u32[]{:S(2)}, u32[]{:S(2)}) async-start(bf16[4,9,64,128]{3,2,1,0:T(8,128)(2,1)} %copy.160), calls=%async_computation.2 | async-start | bytes 1179648 | tf_op jit(solution)/shard_map/all_to_all | solution.py:128
  47.1 1.0 copy-start.11
  56.6 1.3 copy-start.15
  61.6 46.7 %copy-start.4 = (f32[2,128,512]{2,1,0:T(8,128)}, f32[2,128,512]{2,1,0:T(8,128)S(1)}, u32[]{:S(2)}) copy-start(f32[2,128,512]{2,1,0:T(8,128)S(1)} %get-tuple-element.139) | copy-start | bytes 1572868
  62.9 23.4 %all-to-all-start.3 = ((f32[32,9,512]{2,1,0:T(8,128)}), f32[32,9,512]{2,1,0:T(8,128)S(1)}, u32[]{:S(2)}, u32[]{:S(2)}) async-start(f32[32,9,512]{2,1,0:T(8,128)} %pad_maximum_fusion), calls=%async_computation.3 | async-start | bytes 2097152 | tf_op jit(solution)/shard_map/all_to_all | solution.py:141
  87.4 5.3 %copy-start.6 = (f32[32,4,512]{2,1,0:T(4,128)}, f32[32,4,512]{2,1,0:T(4,128)S(1)}, u32[]{:S(2)}) copy-start(f32[32,4,512]{2,1,0:T(4,128)S(1)} %get-tuple-element.256) | copy-start | bytes 786436
  87.9 4.9 %copy-start.13 = (f32[2,128,512]{2,1,0:T(8,128)S(1)}, f32[2,128,512]{2,1,0:T(8,128)}, u32[]{:S(2)}) copy-start(f32[2,128,512]{2,1,0:T(8,128)} %copy-done.12) | copy-start | bytes 1572868
  88.8 12.9 %all-to-all-start.4 = ((f32[32,4,512]{2,1,0:T(4,128)}), f32[32,4,512]{2,1,0:T(4,128)S(1)}, u32[]{:S(2)}, u32[]{:S(2)}) async-start(f32[32,4,512]{2,1,0:T(4,128)} %pad.129), calls=%async_computation.4 | async-start | bytes 524288 | tf_op jit(solution)/shard_map/all_to_all | solution.py:146
  102.7 4.4 %copy-start.18 = (pred[2]{0:T(512)(128)(4,1)S(1)}, pred[2]{0:T(512)(128)(4,1)}, u32[]{:S(2)}) copy-start(pred[2]{0:T(512)(128)(4,1)} %constant.143.clone.1) | copy-start | bytes 10
  102.7 19.4 %all-to-all-start.5 = ((bf16[4,2,128,512]{3,2,1,0:T(8,128)(2,1)}), bf16[4,2,128,512]{3,2,1,0:T(8,128)(2,1)}, u32[]{:S(2)}, u32[]{:S(2)}) async-start(bf16[4,2,128,512]{3,2,1,0:T(8,128)(2,1)} %broadcast_in_dim.134), calls=%async_computation.5 | async-start | bytes 2097152 | tf_op jit(solution)/shard_map/all_to_all | solution.py:84
  108.3 0.7 copy-start.8
  126.0 3.6 %collective-permute-start = (f32[294912]{0:T(1024)S(1)}, f32[294912]{0:T(1024)S(1)}, u32[]{:S(2)}, u32[]{:S(2)}) collective-permute-start(f32[294912]{0:T(1024)S(1)} %broadcast_select_fusion.2), channel_id=1, source_target_pairs={{0,4},{4,0},{1,5},{5,1},{2,6},{6,2},{3,7},{7,3},{8,12},{12,8},{9,1... | collective-permute-start | bytes 3538952 | tf_op jit(solution)/shard_map/ppermute | solution.py:97
  151.5 22.8 %copy-start.7 = (f32[32,4,512]{2,1,0:T(4,128)S(1)}, f32[32,4,512]{2,1,0:T(4,128)}, u32[]{:S(2)}) copy-start(f32[32,4,512]{2,1,0:T(4,128)} %copy-done.6) | copy-start | bytes 786436
  151.5 23.6 %copy-start.14 = (f32[2,128,512]{2,1,0:T(8,128)S(1)}, f32[2,128,512]{2,1,0:T(8,128)}, u32[]{:S(2)}) copy-start(f32[2,128,512]{2,1,0:T(8,128)} %get-tuple-element.252) | copy-start | bytes 1572868
  151.5 23.6 %copy-start.5 = (f32[2,128,512]{2,1,0:T(8,128)S(1)}, f32[2,128,512]{2,1,0:T(8,128)}, u32[]{:S(2)}) copy-start(f32[2,128,512]{2,1,0:T(8,128)} %copy-done.4) | copy-start | bytes 1572868
  151.5 23.6 %copy-start.9 = (f32[128,512]{1,0:T(8,128)S(1)}, f32[128,512]{1,0:T(8,128)}, u32[]{:S(2)}) copy-start(f32[128,512]{1,0:T(8,128)} %copy-done.8) | copy-start | bytes 786436
  171.4 5.6 %collective-permute-start.1 = (f32[294912]{0:T(1024)S(1)}, f32[294912]{0:T(1024)}, u32[]{:S(2)}, u32[]{:S(2)}) collective-permute-start(f32[294912]{0:T(1024)S(1)} %bitcast.182), channel_id=1, source_target_pairs={{0,4},{4,0},{1,5},{5,1},{2,6},{6,2},{3,7},{7,3},{8,12},{12,8},{9,1... | collective-permute-start | bytes 3538952 | tf_op jit(solution)/shard_map/ppermute | solution.py:101

commit v10 on v6

--- a/solution.py
+++ b/solution.py
@@ -108,7 +108,7 @@
         current = frame_rate[:, None] * current + drive
         return (current, current)
 
-    local_end, local_states = lax.scan(advance, blank_state, (decay, drives))
+    local_end, local_states = lax.scan(advance, blank_state, (decay, drives), unroll=True)
     decay_total = jnp.prod(decay, axis=0)
     blocks = lax.axis_size(FRAME_AXES)
     rows = local_end.shape[0]
@@ -116,20 +116,19 @@
     entering_owned = scan_owned(lax.all_to_all(pack_chunks(decay_total, local_end, blocks), FRAME_AXES, 0, 0, tiled=True), False)
     cot_stack = stencil_stack(cotangent, W, -1)
     injected = lax.psum_scatter(
-        jnp.einsum("kup,fkus->pfs", kernel_c, cot_stack, preferred_element_type=jnp.float32),
+        stencil_conv(cotangent, jnp.flip(kernel_c, 0).transpose(0, 2, 1), W),
         "chan",
-        scatter_dimension=0,
+        scatter_dimension=1,
         tiled=True,
     )
     entering_owned, injected = lax.optimization_barrier((entering_owned, injected))
-    injected = jnp.moveaxis(injected, 1, 0)
 
     def retreat(carried, frame_pair):
         frame_rate, source = frame_pair
         adjoint = source + carried
         return (frame_rate[:, None] * adjoint, adjoint)
 
-    message, local_adjoint = lax.scan(retreat, blank_state, (decay, injected), reverse=True)
+    message, local_adjoint = lax.scan(retreat, blank_state, (decay, injected), reverse=True, unroll=True)
 
     exchanged = lax.all_to_all(
         jnp.concatenate([entering_owned, pack_chunks(decay_total, message, blocks)], axis=1), FRAME_AXES, 0, 0, tiled=True

time: 172 us -> 184 us (1.070)
  local copies, waits for them, and re-layouts: 17 us -> 21.7 us
  other arithmetic: 26.7 us -> 30.9 us
  waiting for transfers between devices: 34.4 us -> 36.7 us
  matrix products: 11.2 us -> 8.95 us
    reduce_scatter x1, waiting for transfers between devices: 4.02 us -> 12.5 us  [body(): lax.psum_scatter(stencil_conv(cotangent, jnp.flip(kernel_c, 0).transpose(...]
    all_to_all x1, waiting for transfers between devices: 6.27 us -> 0.01 us  [body(): lax.all_to_all(pack_chunks(decay_total, local_end, blocks), FRAME_AXES, 0...]
    conv_general_dilated x4 -> x7, local copies, waits for them, and re-layouts: 0.34 us -> 3 us  [stencil_conv(): lax.conv_general_dilated(image, taps, (1, 1), ((1, 1), (1, 1)), dimension...]
    dynamic_slice x8 -> x0, local copies, waits for them, and re-layouts: 2.51 us -> none  [body(): local_end, local_states = lax.scan(advance, blank_state, (decay, drives))]
    dot_general x1 -> x0, matrix products: 2.36 us -> none  [body(): jnp.einsum('kup,fkus->pfs', kernel_c, cot_stack, preferred_element_type=j...]
    add x0 -> x2, other arithmetic: none -> 2.12 us  [the longest x1 1.98 us: retreat(): adjoint = source + carried]
    unnamed x18 -> x16, other arithmetic: 13.8 us -> 14.5 us
    unnamed x38 -> x47, local copies, waits for them, and re-layouts: 4.42 us -> 3.9 us
  transfers between devices with their start and end apart: 7 -> 7, of which waited for: 5 -> 4; matrix products, arithmetic and copies ran while one was open for 16% -> 21% of each run, Pallas kernels for 0% -> 0%
where the time goes in v10:
time: 184 us; the launch traced here: 183 us
  blocking collectives  43.9 us (24%)
  waiting for transfers between devices  36.7 us (20%)
  other arithmetic  30.9 us (17%)
  starting transfers between devices  25.7 us (14%)
  local copies, waits for them, and re-layouts  21.7 us (12%)
  between operations  14.8 us (8%)
  matrix products  8.95 us (5%)
    all_to_all x1, blocking collectives, pair_then_chip_sum(): pieces = lax.all_to_all(pair_sum, 'chip', 0, 0, tiled=True)  24.1 us
    all_to_all x1, blocking collectives, pair_then_chip_sum(): lax.all_to_all(jnp.broadcast_to(reduced, pieces.shape), 'chip', 0, 0, til...  19.8 us
    unnamed x16, other arithmetic  14.5 us
    all_to_all x1, waiting for transfers between devices, body(): lax.all_to_all(jnp.concatenate([entering_owned, pack_chunks(decay_total,...  13.9 us
    reduce_scatter x1, waiting for transfers between devices, body(): lax.psum_scatter(stencil_conv(cotangent, jnp.flip(kernel_c, 0).transpose(...  12.5 us
    all_to_all x1, starting transfers between devices, body(): lax.all_to_all(pack_chunks(decay_total, local_end, blocks), FRAME_AXES, 0...  9.47 us
    all_to_all x1, waiting for transfers between devices, body(): lax.all_to_all(arriving_owned, FRAME_AXES, 0, 0, tiled=True)  7.81 us
    all_to_all x1, starting transfers between devices, body(): lax.all_to_all(jnp.concatenate([entering_owned, pack_chunks(decay_total,...  7.73 us
  transfers between devices with their start and end apart: 7, of which 4 were waited for; matrix products, arithmetic and copies ran while one was open for 21% of the time, Pallas kernels for 0%

profile of v10, /device:TPU:1, one launch (start us, length us, event | category | flops | bytes accessed | tf_op | source)
XLA Modules:
  0.0 182.7 jit_solution(4309360398659074634)
XLA Ops:
  7.2 1.3 copy.111
  9.5 1.5 convolution_select_fusion.1
  13.0 0.9 pad_maximum_fusion.1
  13.9 9.5 %all-to-all-start = ((f32[32,5,512]{2,1,0:T(8,128)}), f32[32,5,512]{2,1,0:T(8,128)}, u32[]{:S(2)}, u32[]{:S(2)}) async-start(f32[32,5,512]{2,1,0:T(8,128)} %pad_maximum_fusion.1), calls=%async_computation | async-start | bytes 1048576 | tf_op jit(solution)/shard_map/all_to_all | solution.py:116
  24.5 1.1 convolution_select_fusion
  25.6 1.4 copy.127
  27.1 1.2 copy.128
  28.4 1.9 %copy.129 = f32[2,512,512]{2,1,0:T(8,128)} copy(f32[2,512,512]{1,2,0:T(8,128)S(1)} %bitcast.152) | data formatting | bytes 4194304 | tf_op jit(solution)/shard_map/reshape | solution.py:78
  30.3 0.8 fusion.42
  31.1 0.8 fusion.45
  31.8 0.8 fusion.48
  32.6 0.8 fusion.51
  34.0 0.8 fusion.54
  35.6 1.0 fusion.9
  36.6 1.1 fusion.12
  37.7 1.1 fusion.15
  38.9 1.1 fusion.18
  40.0 0.9 bitcast_dynamic-update-slice_fusion
  42.1 1.1 fusion.21
  43.1 0.9 slice.228
  44.1 0.9 slice.230
  45.6 1.1 slice.229
  46.7 1.2 slice_add_fusion.1
  48.8 12.5 %reduce-scatter.2.cloned.1.call-done = f32[2,128,512]{2,1,0:T(8,128)} async-done(((f32[2,512,512]{2,1,0:T(8,128)}), f32[2,128,512]{2,1,0:T(8,128)}) %reduce-scatter.2.cloned.1.call-update) | async-done | bytes 524304 | tf_op jit(solution)/shard_map/reduce_scatter | solution.py:118
  61.2 2.0 %multiply_add_fusion.4 = (f32[1,128,512]{2,1,0:T(8,128)S(1)}, f32[1,128,512]{2,1,0:T(8,128)S(1)}, f32[1,128,512]{2,1,0:T(8,128)S(1)}, f32[1,128,512]{2,1,0:T(8,128)}, f32[1,128,512]{2,1,0:T(8,128)}) fusion(f32[128]{0:T(128)S(1)} %get-tuple-element.23, f32[2,128,512]{2,1,0:T(8,128)} %reduce-scatter.2.cloned.1.call-done, f32[1,128,512]{2,1,0:T(8,128)S(1)} %copy.142, ...), kind=kLoop, calls=%fused_computation.79 | loop fusion | flops 327680 | bytes 2360320 | tf_op jit(solution)/shard_map/eval_jaxpr/add | solution.py:128
  63.5 1.1 pad_maximum_fusion
  64.7 7.7 %all-to-all-start.1 = ((f32[32,9,512]{2,1,0:T(8,128)}), f32[32,9,512]{2,1,0:T(8,128)S(1)}, u32[]{:S(2)}, u32[]{:S(2)}) async-start(f32[32,9,512]{2,1,0:T(8,128)} %pad_maximum_fusion), calls=%async_computation.2 | async-start | bytes 2097152 | tf_op jit(solution)/shard_map/all_to_all | solution.py:133
  72.5 0.8 fusion.63
  73.3 1.1 fusion.24
  74.4 1.1 fusion.27
  75.5 13.9 %all-to-all-done.1 = f32[32,9,512]{2,1,0:T(8,128)S(1)} async-done(((f32[32,9,512]{2,1,0:T(8,128)}), f32[32,9,512]{2,1,0:T(8,128)S(1)}, u32[]{:S(2)}, u32[]{:S(2)}) %all-to-all-start.1) | async-done | bytes 589856 | tf_op jit(solution)/shard_map/all_to_all | solution.py:133
  90.2 2.0 %fusion.73 = (bf16[2,128,512]{2,1,0:T(8,128)(2,1)}, f32[2,128,512]{2,1,0:T(8,128)}) fusion(f32[128,512]{1,0:T(8,128)S(1)} %mul.278, f32[2,128]{1,0:T(2,128)S(1)} %reduce_window.16, f32[1,128,512]{2,1,0:T(8,128)} %get-tuple-element.26, f32[1,128,512]{2,1,0:T(8,128)} %get-tuple-element.27), kind=kLoop, calls=%fused_computation.141 | loop fusion | flops 524288 | bytes 1573888 | tf_op jit(solution)/shard_map/convert_element_type | solution.py:142
  93.3 0.8 pad.129
  94.0 3.9 %all-to-all-start.2 = ((f32[32,4,512]{2,1,0:T(4,128)}), f32[32,4,512]{2,1,0:T(4,128)S(1)}, u32[]{:S(2)}, u32[]{:S(2)}) async-start(f32[32,4,512]{2,1,0:T(4,128)} %pad.129), calls=%async_computation.3 | async-start | bytes 524288 | tf_op jit(solution)/shard_map/all_to_all | solution.py:138
  98.1 1.1 fusion.30
  99.1 7.8 %all-to-all-done.2 = f32[32,4,512]{2,1,0:T(4,128)S(1)} async-done(((f32[32,4,512]{2,1,0:T(4,128)}), f32[32,4,512]{2,1,0:T(4,128)S(1)}, u32[]{:S(2)}, u32[]{:S(2)}) %all-to-all-start.2) | async-done | bytes 262176 | tf_op jit(solution)/shard_map/all_to_all | solution.py:138
  107.1 3.9 %convolution_bitcast_fusion = f32[9,128,256]{1,2,0:T(8,128)S(1)} fusion(bf16[2,9,256,512]{3,2,0,1:T(8,128)(2,1)} %fusion.30, f32[1,128,512]{2,1,0:T(8,128)S(1)} %get-tuple-element.18, f32[1,128,512]{2,1,0:T(8,128)S(1)} %get-tuple-element.17, f32[128,512]{1,0:T(8,128)S(1)} %mul.270, f32[2,128]{1,0:T(2,128)S(1)} %broadcast_select_fusion.3), kind=kOutput, calls=%fused_computation.4 | convolution fusion | flops 604504064 | bytes 6685696 | tf_op jit(solution)/shard_map/fps,fkcs->kpc/dot_general | solution.py:149
  112.0 2.4 %fusion.1 = f32[9,64,512,1]{2,1,3,0:T(8,128)S(1)} fusion(bf16[2,9,64,512]{3,2,0,1:T(8,128)(2,1)} %fusion.63, bf16[2,512,512]{2,1,0:T(8,128)(2,1)} %all-gather.2.cloned.1.call-done), kind=kOutput, calls=%fused_computation.16 | convolution fusion | flops 603979776 | bytes 3407872 | tf_op jit(solution)/shard_map/fkus,fps->kup/dot_general | solution.py:153
  114.9 1.3 collective-permute-start
  116.2 2.5 %collective-permute-done = f32[294912]{0:T(1024)S(1)} collective-permute-done((f32[294912]{0:T(1024)S(1)}, f32[294912]{0:T(1024)S(1)}, u32[]{:S(2)}, u32[]{:S(2)}) %collective-permute-start) | collective-permute-done | bytes 1179680 | tf_op jit(solution)/shard_map/ppermute | solution.py:90
  118.8 24.1 %all_to_all.30 = f32[16,1,18432]{2,1,0:T(1,128)S(1)} all-to-all(f32[16,1,18432]{2,1,0:T(1,128)S(1)} %bitcast.155), channel_id=1, replica_groups=mesh['chip'=16,'core'=2,'chan'=4] {'chip'}, dimensions={0} | all-to-all | bytes 2359296 | tf_op jit(solution)/shard_map/all_to_all | solution.py:91
  144.3 19.8 %all_to_all.31 = f32[16,1,18432]{2,1,0:T(1,128)S(1)} all-to-all(f32[16,1,18432]{2,1,0:T(1,128)S(1)} %broadcast_in_dim.112), channel_id=1, replica_groups=mesh['chip'=16,'core'=2,'chan'=4] {'chip'}, dimensions={0} | all-to-all | bytes 2359296 | tf_op jit(solution)/shard_map/all_to_all | solution.py:93
  164.1 3.0 %collective-permute-start.1 = (f32[294912]{0:T(1024)S(1)}, f32[294912]{0:T(1024)}, u32[]{:S(2)}, u32[]{:S(2)}) collective-permute-start(f32[294912]{0:T(1024)S(1)} %bitcast.153), channel_id=1, source_target_pairs={{0,4},{4,0},{1,5},{5,1},{2,6},{6,2},{3,7},{7,3},{8,12},{12,8},{9,1... | collective-permute-start | bytes 3538952 | tf_op jit(solution)/shard_map/ppermute | solution.py:94
  167.1 0.8 broadcast_in_dim_reshape.2
  167.9 1.7 fusion.31
  169.7 2.4 %broadcast_select_fusion = (f32[294912]{0:T(1024)S(1)}, f32[294912]{0:T(1024)}) fusion(f32[294912]{0:T(1024)} %collective-permute-done.1, f32[294912]{0:T(1024)S(1)} %bitcast.154, pred[]{:T(512)S(6)} %eq.25), kind=kLoop, calls=%fused_computation.23 | loop fusion | flops 589824 | bytes 4718593 | tf_op jit(solution)/shard_map/jit(_where)/select_n | solution.py:96
  172.1 2.5 %reshape.194 = f32[9,128,256]{2,1,0:T(8,128)} reshape(f32[294912]{0:T(1024)} %get-tuple-element.14) | data formatting | bytes 2359296 | tf_op jit(solution)/shard_map/reshape | solution.py:97
  174.6 1.2 reshape.195
  (146 shorter events, 13.4 us)
Async XLA Ops:
  7.2 1.8 copy-start
  8.8 0.7 copy-start.19
  11.3 0.8 copy-start.11
  11.3 0.8 copy-start.13
  11.6 0.8 copy-start.17
  12.8 10.8 %copy-start.2 = (bf16[2,64,512]{2,1,0:T(8,128)(2,1)S(1)}, bf16[2,64,512]{2,1,0:T(8,128)(2,1)}, u32[]{:S(2)}) copy-start(bf16[2,64,512]{2,1,0:T(8,128)(2,1)} %param.9) | copy-start | bytes 393220
  13.9 29.3 %all-to-all-start = ((f32[32,5,512]{2,1,0:T(8,128)}), f32[32,5,512]{2,1,0:T(8,128)}, u32[]{:S(2)}, u32[]{:S(2)}) async-start(f32[32,5,512]{2,1,0:T(8,128)} %pad_maximum_fusion.1), calls=%async_computation | async-start | bytes 1048576 | tf_op jit(solution)/shard_map/all_to_all | solution.py:116
  23.4 1.1 copy-start.16
  23.4 37.9 %reduce-scatter.2.cloned.1.call-start = ((), (), s32[]{:S(2)}) async-start(), calls=%async_computation.6 | async-start | bytes 2621440 | tf_op jit(solution)/shard_map/reduce_scatter | solution.py:118
  30.3 5.3 %copy-start.1 = (bf16[2,256,512]{2,1,0:T(8,128)(2,1)S(1)}, bf16[2,256,512]{2,1,0:T(8,128)(2,1)}, u32[]{:S(2)}) copy-start(bf16[2,256,512]{2,1,0:T(8,128)(2,1)} %param.5) | copy-start | bytes 1572868
  38.9 2.8 %copy-start.14 = (f32[1,128,8,64]{1,2,3,0:T(8,128)S(1)}, f32[1,128,8,64]{1,2,3,0:T(8,128)}, u32[]{:S(2)}) copy-start(f32[1,128,8,64]{1,2,3,0:T(8,128)} %copy-done.13) | copy-start | bytes 786436
  40.0 1.7 copy-start.12
  63.2 43.8 %copy-start.3 = (f32[1,128,512]{2,1,0:T(8,128)}, f32[1,128,512]{2,1,0:T(8,128)S(1)}, u32[]{:S(2)}) copy-start(f32[1,128,512]{2,1,0:T(8,128)S(1)} %get-tuple-element.18) | copy-start | bytes 786436
  63.2 43.8 %copy-start.5 = (f32[1,128,512]{2,1,0:T(8,128)}, f32[1,128,512]{2,1,0:T(8,128)S(1)}, u32[]{:S(2)}) copy-start(f32[1,128,512]{2,1,0:T(8,128)S(1)} %get-tuple-element.17) | copy-start | bytes 786436
  64.7 24.6 %all-to-all-start.1 = ((f32[32,9,512]{2,1,0:T(8,128)}), f32[32,9,512]{2,1,0:T(8,128)S(1)}, u32[]{:S(2)}, u32[]{:S(2)}) async-start(f32[32,9,512]{2,1,0:T(8,128)} %pad_maximum_fusion), calls=%async_computation.2 | async-start | bytes 2097152 | tf_op jit(solution)/shard_map/all_to_all | solution.py:133
  72.4 39.6 %all-gather.2.cloned.1.call-start = ((), (), s32[]{:S(2)}) async-start(), calls=%async_computation.7 | async-start | bytes 1310720 | tf_op jit(solution)/shard_map/all_gather | solution.py:152
  90.1 2.2 %copy-start.9 = (f32[32,4,512]{2,1,0:T(4,128)}, f32[32,4,512]{2,1,0:T(4,128)S(1)}, u32[]{:S(2)}) copy-start(f32[32,4,512]{2,1,0:T(4,128)S(1)} %get-tuple-element.16) | copy-start | bytes 786436
  93.0 5.0 %copy-start.18 = (pred[2]{0:T(512)(128)(4,1)S(1)}, pred[2]{0:T(512)(128)(4,1)}, u32[]{:S(2)}) copy-start(pred[2]{0:T(512)(128)(4,1)} %constant.96.clone.1) | copy-start | bytes 10
  94.0 12.9 %all-to-all-start.2 = ((f32[32,4,512]{2,1,0:T(4,128)}), f32[32,4,512]{2,1,0:T(4,128)S(1)}, u32[]{:S(2)}, u32[]{:S(2)}) async-start(f32[32,4,512]{2,1,0:T(4,128)} %pad.129), calls=%async_computation.3 | async-start | bytes 524288 | tf_op jit(solution)/shard_map/all_to_all | solution.py:138
  107.0 3.9 %copy-start.7 = (f32[128,512]{1,0:T(8,128)}, f32[128,512]{1,0:T(8,128)S(1)}, u32[]{:S(2)}) copy-start(f32[128,512]{1,0:T(8,128)S(1)} %mul.270) | copy-start | bytes 786436
  114.9 3.8 %collective-permute-start = (f32[294912]{0:T(1024)S(1)}, f32[294912]{0:T(1024)S(1)}, u32[]{:S(2)}, u32[]{:S(2)}) collective-permute-start(f32[294912]{0:T(1024)S(1)} %broadcast_select_fusion.2), channel_id=1, source_target_pairs={{0,4},{4,0},{1,5},{5,1},{2,6},{6,2},{3,7},{7,3},{8,12},{12,8},{9,1... | collective-permute-start | bytes 3538952 | tf_op jit(solution)/shard_map/ppermute | solution.py:90
  144.2 22.8 %copy-start.10 = (f32[32,4,512]{2,1,0:T(4,128)S(1)}, f32[32,4,512]{2,1,0:T(4,128)}, u32[]{:S(2)}) copy-start(f32[32,4,512]{2,1,0:T(4,128)} %copy-done.9) | copy-start | bytes 786436
  144.2 23.6 %copy-start.15 = (f32[2,128,512]{2,1,0:T(8,128)S(1)}, f32[2,128,512]{2,1,0:T(8,128)}, u32[]{:S(2)}) copy-start(f32[2,128,512]{2,1,0:T(8,128)} %get-tuple-element.10) | copy-start | bytes 1572868
  144.2 23.6 %copy-start.4 = (f32[1,128,512]{2,1,0:T(8,128)S(1)}, f32[1,128,512]{2,1,0:T(8,128)}, u32[]{:S(2)}) copy-start(f32[1,128,512]{2,1,0:T(8,128)} %copy-done.3) | copy-start | bytes 786436
  144.3 23.6 %copy-start.6 = (f32[1,128,512]{2,1,0:T(8,128)S(1)}, f32[1,128,512]{2,1,0:T(8,128)}, u32[]{:S(2)}) copy-start(f32[1,128,512]{2,1,0:T(8,128)} %copy-done.5) | copy-start | bytes 786436
  144.3 23.6 %copy-start.8 = (f32[128,512]{1,0:T(8,128)S(1)}, f32[128,512]{1,0:T(8,128)}, u32[]{:S(2)}) copy-start(f32[128,512]{1,0:T(8,128)} %copy-done.7) | copy-start | bytes 786436
  164.1 5.6 %collective-permute-start.1 = (f32[294912]{0:T(1024)S(1)}, f32[294912]{0:T(1024)}, u32[]{:S(2)}, u32[]{:S(2)}) collective-permute-start(f32[294912]{0:T(1024)S(1)} %bitcast.153), channel_id=1, source_target_pairs={{0,4},{4,0},{1,5},{5,1},{2,6},{6,2},{3,7},{7,3},{8,12},{12,8},{9,1... | collective-permute-start | bytes 3538952 | tf_op jit(solution)/shard_map/ppermute | solution.py:94
Sparse Core Ops, SparseCore 0:
  30.4 30.8 reduce-scatter.1
  92.4 18.0 all-gather.1

commit v11 on v6

--- a/solution.py
+++ b/solution.py
@@ -108,7 +108,7 @@
         current = frame_rate[:, None] * current + drive
         return (current, current)
 
-    local_end, local_states = lax.scan(advance, blank_state, (decay, drives))
+    local_end, local_states = lax.scan(advance, blank_state, (decay, drives), unroll=True)
     decay_total = jnp.prod(decay, axis=0)
     blocks = lax.axis_size(FRAME_AXES)
     rows = local_end.shape[0]
@@ -129,7 +129,7 @@
         adjoint = source + carried
         return (frame_rate[:, None] * adjoint, adjoint)
 
-    message, local_adjoint = lax.scan(retreat, blank_state, (decay, injected), reverse=True)
+    message, local_adjoint = lax.scan(retreat, blank_state, (decay, injected), reverse=True, unroll=True)
 
     exchanged = lax.all_to_all(
         jnp.concatenate([entering_owned, pack_chunks(decay_total, message, blocks)], axis=1), FRAME_AXES, 0, 0, tiled=True

time: 172 us -> 179 us (1.041)
  other arithmetic: 26.7 us -> 32.6 us
  waiting for transfers between devices: 34.4 us -> 32.5 us
  starting transfers between devices: 24.4 us -> 26.2 us
    unnamed x18 -> x16, other arithmetic: 13.8 us -> 19 us
    dynamic_slice x8 -> x0, local copies, waits for them, and re-layouts: 2.51 us -> none  [body(): local_end, local_states = lax.scan(advance, blank_state, (decay, drives))]
    add x0 -> x2, other arithmetic: none -> 1.99 us  [the longest x1 1.84 us: retreat(): adjoint = source + carried]
    unnamed x38 -> x54, local copies, waits for them, and re-layouts: 4.42 us -> 5.86 us
  transfers between devices with their start and end apart: 7 -> 7, of which waited for: 5 -> 5; matrix products, arithmetic and copies ran while one was open for 16% -> 14% of each run, Pallas kernels for 0% -> 0%
where the time goes in v11:
time: 179 us; the launch traced here: 178 us
  blocking collectives  43.9 us (25%)
  other arithmetic  32.6 us (18%)
  waiting for transfers between devices  32.5 us (18%)
  starting transfers between devices  26.2 us (15%)
  local copies, waits for them, and re-layouts  17.3 us (10%)
  between operations  14.8 us (8%)
  matrix products  11.3 us (6%)
    all_to_all x1, blocking collectives, pair_then_chip_sum(): pieces = lax.all_to_all(pair_sum, 'chip', 0, 0, tiled=True)  24 us
    all_to_all x1, blocking collectives, pair_then_chip_sum(): lax.all_to_all(jnp.broadcast_to(reduced, pieces.shape), 'chip', 0, 0, til...  19.8 us
    unnamed x16, other arithmetic  19 us
    all_to_all x1, waiting for transfers between devices, body(): lax.all_to_all(jnp.concatenate([entering_owned, pack_chunks(decay_total,...  13.6 us
    all_to_all x1, starting transfers between devices, body(): lax.all_to_all(pack_chunks(decay_total, local_end, blocks), FRAME_AXES, 0...  9.42 us
    all_to_all x1, starting transfers between devices, body(): lax.all_to_all(jnp.concatenate([entering_owned, pack_chunks(decay_total,...  7.88 us
    all_to_all x1, waiting for transfers between devices, body(): lax.all_to_all(arriving_owned, FRAME_AXES, 0, 0, tiled=True)  7.81 us
    all_to_all x1, waiting for transfers between devices, body(): lax.all_to_all(pack_chunks(decay_total, local_end, blocks), FRAME_AXES, 0...  6.16 us
  transfers between devices with their start and end apart: 7, of which 5 were waited for; matrix products, arithmetic and copies ran while one was open for 14% of the time, Pallas kernels for 0%

profile of v11, /device:TPU:1, one launch (start us, length us, event | category | flops | bytes accessed | tf_op | source)
XLA Modules:
  0.0 178.4 jit_solution(17472478531204618685)
XLA Ops:
  7.3 1.7 fusion.39
  9.0 1.7 fusion.42
  10.7 1.7 fusion.45
  12.4 1.7 fusion.48
  14.0 1.6 bitcast_dynamic-update-slice_fusion.1
  15.6 0.8 fusion.51
  16.4 0.8 fusion.54
  17.1 0.8 fusion.57
  17.9 0.8 fusion.60
  18.7 3.6 %convolution_bitcast_fusion = f32[512,2,512]{0,2,1:T(8,128)} fusion(bf16[2,9,64,512]{3,2,1,0:T(8,128)(2,1)} %fusion.60, bf16[9,64,512]{2,1,0:T(8,128)(2,1)S(1)} %copy-done), kind=kOutput, calls=%fused_computation | convolution fusion | flops 603979776 | bytes 3866624 | tf_op jit(solution)/shard_map/kup,fkus->pfs/dot_general | solution.py:119
  22.3 1.0 copy-done.1
  24.0 0.9 copy-done.22
  24.9 1.5 convolution_select_fusion
  29.2 0.9 pad_maximum_fusion.1
  30.1 9.4 %all-to-all-start = ((f32[32,5,512]{2,1,0:T(8,128)}), f32[32,5,512]{2,1,0:T(8,128)S(1)}, u32[]{:S(2)}, u32[]{:S(2)}) async-start(f32[32,5,512]{2,1,0:T(8,128)} %pad_maximum_fusion.1), calls=%async_computation | async-start | bytes 1048576 | tf_op jit(solution)/shard_map/all_to_all | solution.py:116
  39.6 1.0 fusion.9
  40.6 1.1 fusion.12
  41.7 1.1 fusion.15
  42.9 1.1 fusion.18
  44.1 0.9 bitcast_dynamic-update-slice_fusion
  45.0 6.2 %all-to-all-done = f32[32,5,512]{2,1,0:T(8,128)S(1)} async-done(((f32[32,5,512]{2,1,0:T(8,128)}), f32[32,5,512]{2,1,0:T(8,128)S(1)}, u32[]{:S(2)}, u32[]{:S(2)}) %all-to-all-start) | async-done | bytes 327712 | tf_op jit(solution)/shard_map/all_to_all | solution.py:116
  53.0 2.3 %reduce-scatter.2.cloned.1.call-done = f32[128,2,512]{0,2,1:T(8,128)} async-done(((f32[512,2,512]{0,2,1:T(8,128)}), f32[128,2,512]{0,2,1:T(8,128)}) %reduce-scatter.2.cloned.1.call-update) | async-done | bytes 524304 | tf_op jit(solution)/shard_map/reduce_scatter | solution.py:118
  55.3 1.8 %multiply_add_fusion.3 = (f32[1,128,512]{1,2,0:T(8,128)S(1)}, f32[1,128,512]{1,2,0:T(8,128)S(1)}, f32[1,128,512]{1,2,0:T(8,128)S(1)}, f32[1,128,512]{1,2,0:T(8,128)S(1)}, f32[1,128,512]{1,2,0:T(8,128)}) fusion(f32[128]{0:T(128)S(1)} %copy-done.20, f32[2,128,512]{1,2,0:T(8,128)} %bitcast.176, f32[1,128,8,64]{1,3,2,0:T(8,128)S(1)} %copy.144, ...), kind=kLoop, calls=%fused_computation.75 | loop fusion | flops 327680 | bytes 2360320 | tf_op jit(solution)/shard_map/eval_jaxpr/add | solution.py:129
  58.0 1.1 pad_maximum_fusion
  59.2 7.9 %all-to-all-start.1 = ((f32[32,9,512]{2,1,0:T(8,128)}), f32[32,9,512]{2,1,0:T(8,128)S(1)}, u32[]{:S(2)}, u32[]{:S(2)}) async-start(f32[32,9,512]{2,1,0:T(8,128)} %pad_maximum_fusion), calls=%async_computation.2 | async-start | bytes 2097152 | tf_op jit(solution)/shard_map/all_to_all | solution.py:134
  67.2 1.1 fusion.21
  68.3 1.0 fusion.24
  69.4 1.0 fusion.27
  70.4 13.6 %all-to-all-done.1 = f32[32,9,512]{2,1,0:T(8,128)S(1)} async-done(((f32[32,9,512]{2,1,0:T(8,128)}), f32[32,9,512]{2,1,0:T(8,128)S(1)}, u32[]{:S(2)}, u32[]{:S(2)}) %all-to-all-start.1) | async-done | bytes 589856 | tf_op jit(solution)/shard_map/all_to_all | solution.py:134
  85.0 0.8 copy-done.8
  85.8 0.9 fusion.70
  87.8 0.8 pad.130
  88.5 3.9 %all-to-all-start.2 = ((f32[32,4,512]{2,1,0:T(4,128)}), f32[32,4,512]{2,1,0:T(4,128)S(1)}, u32[]{:S(2)}, u32[]{:S(2)}) async-start(f32[32,4,512]{2,1,0:T(4,128)} %pad.130), calls=%async_computation.3 | async-start | bytes 524288 | tf_op jit(solution)/shard_map/all_to_all | solution.py:139
  92.5 1.1 fusion.30
  93.6 7.8 %all-to-all-done.2 = f32[32,4,512]{2,1,0:T(4,128)S(1)} async-done(((f32[32,4,512]{2,1,0:T(4,128)}), f32[32,4,512]{2,1,0:T(4,128)S(1)}, u32[]{:S(2)}, u32[]{:S(2)}) %all-to-all-start.2) | async-done | bytes 262176 | tf_op jit(solution)/shard_map/all_to_all | solution.py:139
  102.4 3.8 %convolution_bitcast_fusion.1 = f32[9,128,256]{1,2,0:T(8,128)S(1)} fusion(bf16[2,9,256,512]{3,2,0,1:T(8,128)(2,1)} %fusion.30, f32[1,128,512]{1,2,0:T(8,128)S(1)} %get-tuple-element.18, f32[1,128,512]{1,2,0:T(8,128)S(1)} %get-tuple-element.17, f32[128,512]{0,1:T(8,128)S(1)} %copy.140, f32[2,128]{1,0:T(2,128)S(1)} %broadcast_select_fusion.3), kind=kOutput, calls=%fused_computation.3 | convolution fusion | flops 604504064 | bytes 6685696 | tf_op jit(solution)/shard_map/fps,fkcs->kpc/dot_general | solution.py:150
  107.1 2.4 %fusion.1 = f32[9,64,512,1]{2,1,0,3:T(8,128)S(1)} fusion(bf16[2,9,64,512]{3,2,1,0:T(8,128)(2,1)} %fusion.60, bf16[2,512,512]{1,2,0:T(8,128)(2,1)} %all-gather.2.cloned.1.call-done), kind=kOutput, calls=%fused_computation.15 | convolution fusion | flops 603979776 | bytes 3407872 | tf_op jit(solution)/shard_map/fkus,fps->kup/dot_general | solution.py:154
  110.0 1.9 %collective-permute-start = (f32[294912]{0:T(1024)S(1)}, f32[294912]{0:T(1024)S(1)}, u32[]{:S(2)}, u32[]{:S(2)}) collective-permute-start(f32[294912]{0:T(1024)S(1)} %broadcast_select_fusion.2), channel_id=1, source_target_pairs={{0,4},{4,0},{1,5},{5,1},{2,6},{6,2},{3,7},{7,3},{8,12},{12,8},{9,1... | collective-permute-start | bytes 3538952 | tf_op jit(solution)/shard_map/ppermute | solution.py:90
  111.9 2.5 %collective-permute-done = f32[294912]{0:T(1024)S(1)} collective-permute-done((f32[294912]{0:T(1024)S(1)}, f32[294912]{0:T(1024)S(1)}, u32[]{:S(2)}, u32[]{:S(2)}) %collective-permute-start) | collective-permute-done | bytes 1179680 | tf_op jit(solution)/shard_map/ppermute | solution.py:90
  114.5 24.0 %all_to_all.30 = f32[16,1,18432]{2,1,0:T(1,128)S(1)} all-to-all(f32[16,1,18432]{2,1,0:T(1,128)S(1)} %bitcast.169), channel_id=1, replica_groups=mesh['chip'=16,'core'=2,'chan'=4] {'chip'}, dimensions={0} | all-to-all | bytes 2359296 | tf_op jit(solution)/shard_map/all_to_all | solution.py:91
  138.6 0.7 reduce_sum.18
  140.0 19.8 %all_to_all.31 = f32[16,1,18432]{2,1,0:T(1,128)S(1)} all-to-all(f32[16,1,18432]{2,1,0:T(1,128)S(1)} %broadcast_in_dim.112), channel_id=1, replica_groups=mesh['chip'=16,'core'=2,'chan'=4] {'chip'}, dimensions={0} | all-to-all | bytes 2359296 | tf_op jit(solution)/shard_map/all_to_all | solution.py:93
  159.8 3.0 %collective-permute-start.1 = (f32[294912]{0:T(1024)S(1)}, f32[294912]{0:T(1024)}, u32[]{:S(2)}, u32[]{:S(2)}) collective-permute-start(f32[294912]{0:T(1024)S(1)} %bitcast.167), channel_id=1, source_target_pairs={{0,4},{4,0},{1,5},{5,1},{2,6},{6,2},{3,7},{7,3},{8,12},{12,8},{9,1... | collective-permute-start | bytes 3538952 | tf_op jit(solution)/shard_map/ppermute | solution.py:94
  162.7 0.8 broadcast_in_dim_reshape.2
  163.5 1.1 copy.148
  165.3 2.4 %broadcast_select_fusion = (f32[294912]{0:T(1024)}, f32[294912]{0:T(1024)S(1)}) fusion(f32[294912]{0:T(1024)} %collective-permute-done.1, f32[294912]{0:T(1024)S(1)} %bitcast.168, pred[]{:T(512)S(6)} %eq.25), kind=kLoop, calls=%fused_computation.21 | loop fusion | flops 589824 | bytes 4718593 | tf_op jit(solution)/shard_map/jit(_where)/select_n | solution.py:96
  167.8 2.4 %reshape.183 = f32[9,64,512]{2,1,0:T(8,128)} reshape(f32[294912]{0:T(1024)} %get-tuple-element.13) | data formatting | bytes 2359296 | tf_op jit(solution)/shard_map/reshape | solution.py:97
  170.2 1.3 reshape.182
  (147 shorter events, 12.0 us)
Async XLA Ops:
  7.2 11.5 %copy-start = (bf16[9,64,512]{2,1,0:T(8,128)(2,1)S(1)}, bf16[9,64,512]{2,1,0:T(8,128)(2,1)}, u32[]{:S(2)}) copy-start(bf16[9,64,512]{2,1,0:T(8,128)(2,1)} %param.8) | copy-start | bytes 1769476
  7.2 8.4 %copy-start.2 = (bf16[2,64,512]{2,1,0:T(8,128)(2,1)S(1)}, bf16[2,64,512]{2,1,0:T(8,128)(2,1)}, u32[]{:S(2)}) copy-start(bf16[2,64,512]{2,1,0:T(8,128)(2,1)} %param.9) | copy-start | bytes 393220
  7.2 48.1 %reduce-scatter.2.cloned.1.call-start = ((), (), s32[]{:S(2)}) async-start(), calls=%async_computation.6 | async-start | bytes 2621440 | tf_op jit(solution)/shard_map/reduce_scatter | solution.py:118
  7.2 35.6 %copy-start.15 = (pred[512]{0:T(512)(128)(4,1)}, pred[512]{0:T(512)(128)(4,1)S(1)}, u32[]{:S(2)}) copy-start(pred[512]{0:T(512)(128)(4,1)S(1)} %compare_and_fusion.1) | copy-start | bytes 1540
  7.3 34.4 %copy-start.11 = (pred[512]{0:T(512)(128)(4,1)}, pred[512]{0:T(512)(128)(4,1)S(1)}, u32[]{:S(2)}) copy-start(pred[512]{0:T(512)(128)(4,1)S(1)} %compare_and_fusion) | copy-start | bytes 1540
  7.3 36.8 %copy-start.13 = (pred[512]{0:T(512)(128)(4,1)}, pred[512]{0:T(512)(128)(4,1)S(1)}, u32[]{:S(2)}) copy-start(pred[512]{0:T(512)(128)(4,1)S(1)} %fusion.67) | copy-start | bytes 1540
  22.3 1.0 copy-start.1
  23.8 1.1 copy-start.22
  23.9 1.1 copy-start.23
  26.5 0.7 copy-start.17
  27.9 1.1 copy-start.9
  30.1 21.0 %all-to-all-start = ((f32[32,5,512]{2,1,0:T(8,128)}), f32[32,5,512]{2,1,0:T(8,128)S(1)}, u32[]{:S(2)}, u32[]{:S(2)}) async-start(f32[32,5,512]{2,1,0:T(8,128)} %pad_maximum_fusion.1), calls=%async_computation | async-start | bytes 1048576 | tf_op jit(solution)/shard_map/all_to_all | solution.py:116
  52.6 2.7 %copy-start.19 = (f32[128]{0:T(128)S(1)}, f32[128]{0:T(128)}, u32[]{:S(2)}) copy-start(f32[128]{0:T(128)} %get-tuple-element.22) | copy-start | bytes 1540
  52.6 2.7 %copy-start.20 = (f32[128]{0:T(128)S(1)}, f32[128]{0:T(128)}, u32[]{:S(2)}) copy-start(f32[128]{0:T(128)} %get-tuple-element.23) | copy-start | bytes 1540
  57.2 0.7 copy-start.10
  59.2 8.0 %copy-start.12 = (pred[512]{0:T(512)(128)(4,1)S(1)}, pred[512]{0:T(512)(128)(4,1)}, u32[]{:S(2)}) copy-start(pred[512]{0:T(512)(128)(4,1)} %copy-done.11) | copy-start | bytes 1540
  59.2 9.0 %copy-start.18 = (f32[2,128]{1,0:T(2,128)S(1)}, f32[2,128]{1,0:T(2,128)}, u32[]{:S(2)}) copy-start(f32[2,128]{1,0:T(2,128)} %param.6) | copy-start | bytes 3076
  59.2 9.1 %copy-start.16 = (pred[512]{0:T(512)(128)(4,1)S(1)}, pred[512]{0:T(512)(128)(4,1)}, u32[]{:S(2)}) copy-start(pred[512]{0:T(512)(128)(4,1)} %copy-done.15) | copy-start | bytes 1540
  59.2 24.8 %all-to-all-start.1 = ((f32[32,9,512]{2,1,0:T(8,128)}), f32[32,9,512]{2,1,0:T(8,128)S(1)}, u32[]{:S(2)}, u32[]{:S(2)}) async-start(f32[32,9,512]{2,1,0:T(8,128)} %pad_maximum_fusion), calls=%async_computation.2 | async-start | bytes 2097152 | tf_op jit(solution)/shard_map/all_to_all | solution.py:134
  67.1 2.3 %copy-start.14 = (pred[512]{0:T(512)(128)(4,1)S(1)}, pred[512]{0:T(512)(128)(4,1)}, u32[]{:S(2)}) copy-start(pred[512]{0:T(512)(128)(4,1)} %copy-done.13) | copy-start | bytes 1540
  67.1 40.0 %all-gather.2.cloned.1.call-start = ((), (), s32[]{:S(2)}) async-start(), calls=%async_computation.7 | async-start | bytes 1310720 | tf_op jit(solution)/shard_map/all_gather | solution.py:153
  84.8 2.0 %copy-start.5 = (f32[32,4,512]{2,1,0:T(4,128)}, f32[32,4,512]{2,1,0:T(4,128)S(1)}, u32[]{:S(2)}) copy-start(f32[32,4,512]{2,1,0:T(4,128)S(1)} %get-tuple-element.16) | copy-start | bytes 786436
  84.8 1.0 copy-start.8
  87.5 5.0 %copy-start.21 = (pred[2]{0:T(512)(128)(4,1)S(1)}, pred[2]{0:T(512)(128)(4,1)}, u32[]{:S(2)}) copy-start(pred[2]{0:T(512)(128)(4,1)} %constant.96.clone.1) | copy-start | bytes 10
  88.5 12.9 %all-to-all-start.2 = ((f32[32,4,512]{2,1,0:T(4,128)}), f32[32,4,512]{2,1,0:T(4,128)S(1)}, u32[]{:S(2)}, u32[]{:S(2)}) async-start(f32[32,4,512]{2,1,0:T(4,128)} %pad.130), calls=%async_computation.3 | async-start | bytes 524288 | tf_op jit(solution)/shard_map/all_to_all | solution.py:139
  101.6 0.7 copy-start.3
  110.0 4.4 %collective-permute-start = (f32[294912]{0:T(1024)S(1)}, f32[294912]{0:T(1024)S(1)}, u32[]{:S(2)}, u32[]{:S(2)}) collective-permute-start(f32[294912]{0:T(1024)S(1)} %broadcast_select_fusion.2), channel_id=1, source_target_pairs={{0,4},{4,0},{1,5},{5,1},{2,6},{6,2},{3,7},{7,3},{8,12},{12,8},{9,1... | collective-permute-start | bytes 3538952 | tf_op jit(solution)/shard_map/ppermute | solution.py:90
  139.9 22.8 %copy-start.6 = (f32[32,4,512]{2,1,0:T(4,128)S(1)}, f32[32,4,512]{2,1,0:T(4,128)}, u32[]{:S(2)}) copy-start(f32[32,4,512]{2,1,0:T(4,128)} %copy-done.5) | copy-start | bytes 786436
  139.9 24.7 %copy-start.7 = (f32[2,128,512]{1,2,0:T(8,128)S(1)}, f32[2,128,512]{1,2,0:T(8,128)}, u32[]{:S(2)}) copy-start(f32[2,128,512]{1,2,0:T(8,128)} %get-tuple-element.10) | copy-start | bytes 1572868
  159.8 4.9 %copy-start.4 = (f32[128,512]{0,1:T(8,128)S(1)}, f32[128,512]{0,1:T(8,128)}, u32[]{:S(2)}) copy-start(f32[128,512]{0,1:T(8,128)} %copy-done.3) | copy-start | bytes 786436
  159.8 5.6 %collective-permute-start.1 = (f32[294912]{0:T(1024)S(1)}, f32[294912]{0:T(1024)}, u32[]{:S(2)}, u32[]{:S(2)}) collective-permute-start(f32[294912]{0:T(1024)S(1)} %bitcast.167), channel_id=1, source_target_pairs={{0,4},{4,0},{1,5},{5,1},{2,6},{6,2},{3,7},{7,3},{8,12},{12,8},{9,1... | collective-permute-start | bytes 3538952 | tf_op jit(solution)/shard_map/ppermute | solution.py:94
Sparse Core Ops, SparseCore 0:
  22.4 32.8 reduce-scatter.1
  86.9 20.0 all-gather.1

commit v12 on v7

--- a/solution.py
+++ b/solution.py
@@ -78,6 +78,19 @@
     return out.reshape(frames, kernel.shape[1], cells)
 
 
+def gather_readout(cotangent, kernel_c, states_local, axis):
+    count = lax.axis_size(axis)
+    me = lax.axis_index(axis)
+    cot_blocks = [cotangent]
+    kernel_blocks = [lax.dynamic_slice_in_dim(kernel_c, me * states_local, states_local, axis=2)]
+    for step in range(1, count):
+        pairs = [(source, (source + step) % count) for source in range(count)]
+        wanted = lax.dynamic_slice_in_dim(kernel_c, ((me + step) % count) * states_local, states_local, axis=2)
+        cot_blocks.append(lax.ppermute(cotangent, axis, pairs))
+        kernel_blocks.append(lax.ppermute(wanted, axis, pairs))
+    return jnp.concatenate(cot_blocks, axis=1), jnp.concatenate(kernel_blocks, axis=1)
+
+
 FRAME_AXES = ("chip", "core")
 
 
@@ -115,8 +128,7 @@
     chunk = rows // blocks
     entering_owned = scan_owned(lax.all_to_all(pack_chunks(decay_total, local_end, blocks), FRAME_AXES, 0, 0, tiled=True), False)
     cot_stack = stencil_stack(cotangent, W, -1)
-    all_cotangent = lax.all_gather(cotangent, "chan", axis=1, tiled=True)
-    readout_local = lax.all_to_all(kernel_c, "chan", 2, 1, tiled=True)
+    all_cotangent, readout_local = gather_readout(cotangent, kernel_c, kernel_b.shape[1], "chan")
     injected = stencil_conv(all_cotangent, jnp.flip(readout_local, 0).transpose(0, 2, 1), W)
     entering_owned, injected = lax.optimization_barrier((entering_owned, injected))
 

time: 201 us -> 175 us (0.87)
  local copies, waits for them, and re-layouts: 28.9 us -> 17.4 us
  blocking collectives: 55 us -> 43.8 us
  other arithmetic: 28.9 us -> 25.2 us
  starting transfers between devices: 31.8 us -> 35.3 us
  waiting for transfers between devices: 29.8 us -> 26.5 us
    all_gather x1 -> x0, blocking collectives: 11.1 us -> none  [body(): all_cotangent = lax.all_gather(cotangent, 'chan', axis=1, tiled=True)]
    unnamed x39 -> x46, local copies, waits for them, and re-layouts: 15.4 us -> 5.87 us
    ppermute x0 -> x6, starting transfers between devices: none -> 8.73 us  [the longest x3 5.87 us: gather_readout(): cot_blocks.append(lax.ppermute(cotangent, axis, pairs))]
    all_to_all x1 -> x0, waiting for transfers between devices: 5.55 us -> none  [body(): readout_local = lax.all_to_all(kernel_c, 'chan', 2, 1, tiled=True)]
    unnamed x18, other arithmetic: 14.5 us -> 9.22 us
    all_to_all x1 -> x0, starting transfers between devices: 3.6 us -> none  [body(): readout_local = lax.all_to_all(kernel_c, 'chan', 2, 1, tiled=True)]
    all_to_all x2 -> x0, local copies, waits for them, and re-layouts: 3.14 us -> none  [body(): readout_local = lax.all_to_all(kernel_c, 'chan', 2, 1, tiled=True)]
    all_to_all x1, starting transfers between devices: 11.4 us -> 8.37 us  [body(): lax.all_to_all(jnp.concatenate([entering_owned, pack_chunks(decay_total,...]
  transfers between devices with their start and end apart: 7 -> 12, of which waited for: 4 -> 4; matrix products, arithmetic and copies ran while one was open for 18% -> 19% of each run, Pallas kernels for 0% -> 0%
where the time goes in v12:
time: 175 us; the launch traced here: 174 us
  blocking collectives  43.8 us (25%)
  starting transfers between devices  35.3 us (20%)
  waiting for transfers between devices  26.5 us (15%)
  other arithmetic  25.2 us (14%)
  local copies, waits for them, and re-layouts  17.4 us (10%)
  between operations  14.9 us (9%)
  matrix products  10.4 us (6%)
    all_to_all x1, blocking collectives, pair_then_chip_sum(): pieces = lax.all_to_all(pair_sum, 'chip', 0, 0, tiled=True)  24 us
    all_to_all x1, blocking collectives, pair_then_chip_sum(): lax.all_to_all(jnp.broadcast_to(reduced, pieces.shape), 'chip', 0, 0, til...  19.8 us
    all_to_all x1, waiting for transfers between devices, body(): lax.all_to_all(jnp.concatenate([entering_owned, pack_chunks(decay_total,...  13.9 us
    all_to_all x1, starting transfers between devices, body(): lax.all_to_all(pack_chunks(decay_total, local_end, blocks), FRAME_AXES, 0...  9.57 us
    unnamed x18, other arithmetic  9.22 us
    all_to_all x1, starting transfers between devices, body(): lax.all_to_all(jnp.concatenate([entering_owned, pack_chunks(decay_total,...  8.37 us
    all_to_all x1, waiting for transfers between devices, body(): lax.all_to_all(arriving_owned, FRAME_AXES, 0, 0, tiled=True)  7.81 us
    unnamed x46, local copies, waits for them, and re-layouts  5.87 us
  transfers between devices with their start and end apart: 12, of which 4 were waited for; matrix products, arithmetic and copies ran while one was open for 19% of the time, Pallas kernels for 0%

profile of v12, /device:TPU:1, one launch (start us, length us, event | category | flops | bytes accessed | tf_op | source)
XLA Modules:
  0.0 173.7 jit_solution(12581001715232015699)
XLA Ops:
  7.2 1.1 copy.99
  8.3 2.2 %collective-permute-start = (bf16[2,64,512]{1,2,0:T(8,128)(2,1)S(1)}, bf16[2,64,512]{1,2,0:T(8,128)(2,1)S(1)}, u32[]{:S(2)}, u32[]{:S(2)}) collective-permute-start(bf16[2,64,512]{1,2,0:T(8,128)(2,1)S(1)} %copy.99), channel_id=1, source_target_pairs={{0,1},{1,2},{2,3},{3,0},{4,5},{5,6},{6,7},{7,4},{8,9},{9,10},{10,1... | collective-permute-start | bytes 393224 | tf_op jit(solution)/shard_map/ppermute | solution.py:89
  10.5 2.6 %collective-permute-start.1 = (bf16[2,64,512]{1,2,0:T(8,128)(2,1)S(1)}, bf16[2,64,512]{1,2,0:T(8,128)(2,1)}, u32[]{:S(2)}, u32[]{:S(2)}) collective-permute-start(bf16[2,64,512]{1,2,0:T(8,128)(2,1)S(1)} %copy.99), channel_id=1, source_target_pairs={{0,2},{1,3},{2,0},{3,1},{4,6},{5,7},{6,4},{7,5},{8,10},{9,11},{10,... | collective-permute-start | bytes 393224 | tf_op jit(solution)/shard_map/ppermute | solution.py:89
  13.1 1.1 collective-permute-start.2
  14.2 1.2 copy.81
  16.4 1.5 convolution_select_fusion.1
  18.9 0.6 while.30
  19.8 0.9 pad_maximum_fusion.2
  20.7 9.6 %all-to-all-start = ((f32[32,5,512]{2,1,0:T(8,128)}), f32[32,5,512]{2,1,0:T(8,128)S(1)}, u32[]{:S(2)}, u32[]{:S(2)}) async-start(f32[32,5,512]{2,1,0:T(8,128)} %pad_maximum_fusion.2), calls=%async_computation | async-start | bytes 1048576 | tf_op jit(solution)/shard_map/all_to_all | solution.py:129
  30.4 0.8 constant_dynamic-slice_fusion.7
  32.2 1.1 fusion.14
  33.3 1.1 fusion.17
  34.5 1.1 fusion.20
  35.6 1.1 fusion.23
  36.7 0.9 bitcast_dynamic-update-slice_fusion.2
  37.6 1.1 fusion.26
  39.4 2.0 %collective-permute-start.5 = (bf16[9,64,128]{2,1,0:T(8,128)(2,1)}, bf16[9,64,128]{2,1,0:T(8,128)(2,1)S(1)}, u32[]{:S(2)}, u32[]{:S(2)}) collective-permute-start(bf16[9,64,128]{2,1,0:T(8,128)(2,1)} %get-tuple-element.239), channel_id=1, source_target_pairs={{0,3},{1,0},{2,1},{3,2},{4,7},{5,4},{6,5},{7,6},{8,11},{9,8},{10,9... | collective-permute-start | bytes 442376 | tf_op jit(solution)/shard_map/ppermute | solution.py:90
  41.3 1.4 pad_maximum_fusion.3
  43.2 2.3 %collective-permute-done.5 = bf16[9,64,128]{2,1,0:T(8,128)(2,1)S(1)} collective-permute-done((bf16[9,64,128]{2,1,0:T(8,128)(2,1)}, bf16[9,64,128]{2,1,0:T(8,128)(2,1)S(1)}, u32[]{:S(2)}, u32[]{:S(2)}) %collective-permute-start.5) | collective-permute-done | bytes 147488 | tf_op jit(solution)/shard_map/ppermute | solution.py:90
  45.4 1.0 pad_maximum_fusion.1
  46.5 0.9 rev.9
  47.3 2.6 %convolution_select_fusion = f32[8,16,9,128]{3,1,2,0:T(8,128)S(1)} fusion(bf16[3,3,128,256]{2,3,1,0:T(8,128)(2,1)} %bitcast.190, bf16[256,8,2,8,11]{0,1,4,3,2:T(8,128)(2,1)S(1)} %fusion.7, pred[16,9]{0,1:T(8,128)(4,1)S(1)} %copy-done.18), kind=kOutput, calls=%fused_computation.16 | convolution fusion | flops 623001600 | bytes 1900688 | tf_op jit(solution)/shard_map/conv_general_dilated | solution.py:74
  52.1 0.7 while.31
  53.0 1.1 pad_maximum_fusion
  54.1 8.4 %all-to-all-start.1 = ((f32[32,9,512]{2,1,0:T(8,128)}), f32[32,9,512]{2,1,0:T(8,128)S(1)}, u32[]{:S(2)}, u32[]{:S(2)}) async-start(f32[32,9,512]{2,1,0:T(8,128)} %pad_maximum_fusion), calls=%async_computation.1 | async-start | bytes 2097152 | tf_op jit(solution)/shard_map/all_to_all | solution.py:142
  62.5 0.8 fusion.65
  63.4 1.1 fusion.29
  64.5 1.0 fusion.32
  65.5 13.9 %all-to-all-done.1 = f32[32,9,512]{2,1,0:T(8,128)S(1)} async-done(((f32[32,9,512]{2,1,0:T(8,128)}), f32[32,9,512]{2,1,0:T(8,128)S(1)}, u32[]{:S(2)}, u32[]{:S(2)}) %all-to-all-start.1) | async-done | bytes 589856 | tf_op jit(solution)/shard_map/all_to_all | solution.py:142
  80.3 2.1 %fusion.74 = (bf16[2,128,512]{2,1,0:T(8,128)(2,1)}, f32[2,128,512]{2,1,0:T(8,128)}) fusion(f32[2,128,512]{2,1,0:T(8,128)} %copy-done.9, f32[128,512]{1,0:T(8,128)S(1)} %mul.257, f32[2,128]{1,0:T(2,128)S(1)} %reduce_window.16), kind=kLoop, calls=%fused_computation.148 | loop fusion | flops 393216 | bytes 1573888 | tf_op jit(solution)/shard_map/convert_element_type | solution.py:151
  83.3 0.8 pad.129
  84.1 3.9 %all-to-all-start.2 = ((f32[32,4,512]{2,1,0:T(4,128)}), f32[32,4,512]{2,1,0:T(4,128)S(1)}, u32[]{:S(2)}, u32[]{:S(2)}) async-start(f32[32,4,512]{2,1,0:T(4,128)} %pad.129), calls=%async_computation.2 | async-start | bytes 524288 | tf_op jit(solution)/shard_map/all_to_all | solution.py:147
  88.1 1.1 fusion.35
  89.2 7.8 %all-to-all-done.2 = f32[32,4,512]{2,1,0:T(4,128)S(1)} async-done(((f32[32,4,512]{2,1,0:T(4,128)}), f32[32,4,512]{2,1,0:T(4,128)S(1)}, u32[]{:S(2)}, u32[]{:S(2)}) %all-to-all-start.2) | async-done | bytes 262176 | tf_op jit(solution)/shard_map/all_to_all | solution.py:147
  97.1 0.7 copy-done.7
  97.8 3.8 %convolution_bitcast_fusion = f32[9,128,256]{1,2,0:T(8,128)S(1)} fusion(bf16[2,9,256,512]{3,2,0,1:T(8,128)(2,1)} %fusion.35, f32[2,128,512]{2,1,0:T(8,128)S(1)} %get-tuple-element.139, f32[128,512]{1,0:T(8,128)S(1)} %mul.253, f32[2,128]{1,0:T(2,128)S(1)} %broadcast_select_fusion.3), kind=kOutput, calls=%fused_computation.15 | convolution fusion | flops 604372992 | bytes 6685696 | tf_op jit(solution)/shard_map/fps,fkcs->kpc/dot_general | solution.py:158
  102.7 2.4 %fusion.4 = f32[9,64,512,1]{2,1,3,0:T(8,128)S(1)} fusion(bf16[2,9,64,512]{3,2,0,1:T(8,128)(2,1)} %fusion.65, bf16[2,512,512]{2,1,0:T(8,128)(2,1)} %all-gather.2.cloned.1.call-done), kind=kOutput, calls=%fused_computation.28 | convolution fusion | flops 603979776 | bytes 3407872 | tf_op jit(solution)/shard_map/fkus,fps->kup/dot_general | solution.py:162
  105.5 1.7 collective-permute-start.6
  107.3 2.5 %collective-permute-done.6 = f32[294912]{0:T(1024)S(1)} collective-permute-done((f32[294912]{0:T(1024)S(1)}, f32[294912]{0:T(1024)S(1)}, u32[]{:S(2)}, u32[]{:S(2)}) %collective-permute-start.6) | collective-permute-done | bytes 1179680 | tf_op jit(solution)/shard_map/ppermute | solution.py:103
  109.9 24.0 %all_to_all.31 = f32[16,1,18432]{2,1,0:T(1,128)S(1)} all-to-all(f32[16,1,18432]{2,1,0:T(1,128)S(1)} %bitcast.179), channel_id=1, replica_groups=mesh['chip'=16,'core'=2,'chan'=4] {'chip'}, dimensions={0} | all-to-all | bytes 2359296 | tf_op jit(solution)/shard_map/all_to_all | solution.py:104
  133.9 0.7 reduce_sum.18
  135.3 19.8 %all_to_all.30 = f32[16,1,18432]{2,1,0:T(1,128)S(1)} all-to-all(f32[16,1,18432]{2,1,0:T(1,128)S(1)} %broadcast_in_dim.121), channel_id=1, replica_groups=mesh['chip'=16,'core'=2,'chan'=4] {'chip'}, dimensions={0} | all-to-all | bytes 2359296 | tf_op jit(solution)/shard_map/all_to_all | solution.py:106
  155.1 3.0 %collective-permute-start.7 = (f32[294912]{0:T(1024)S(1)}, f32[294912]{0:T(1024)}, u32[]{:S(2)}, u32[]{:S(2)}) collective-permute-start(f32[294912]{0:T(1024)S(1)} %bitcast.177), channel_id=1, source_target_pairs={{0,4},{4,0},{1,5},{5,1},{2,6},{6,2},{3,7},{7,3},{8,12},{12,8},{9,1... | collective-permute-start | bytes 3538952 | tf_op jit(solution)/shard_map/ppermute | solution.py:107
  158.1 0.8 broadcast_in_dim_reshape.2
  158.9 1.7 fusion.36
  160.7 2.4 %broadcast_select_fusion = (f32[294912]{0:T(1024)S(1)}, f32[294912]{0:T(1024)}) fusion(f32[294912]{0:T(1024)} %collective-permute-done.7, f32[294912]{0:T(1024)S(1)} %bitcast.178, pred[]{:T(512)S(6)} %eq.29), kind=kLoop, calls=%fused_computation.37 | loop fusion | flops 589824 | bytes 4718593 | tf_op jit(solution)/shard_map/jit(_where)/select_n | solution.py:109
  163.2 2.5 %reshape.86 = f32[9,128,256]{2,1,0:T(8,128)} reshape(f32[294912]{0:T(1024)} %get-tuple-element.234) | data formatting | bytes 2359296 | tf_op jit(solution)/shard_map/reshape | solution.py:110
  165.7 1.2 reshape.87
  (164 shorter events, 11.8 us)
Async XLA Ops:
  7.2 8.7 %copy-start = (bf16[9,128,256]{2,1,0:T(8,128)(2,1)S(1)}, bf16[9,128,256]{2,1,0:T(8,128)(2,1)}, u32[]{:S(2)}) copy-start(bf16[9,128,256]{2,1,0:T(8,128)(2,1)} %param.11) | copy-start | bytes 1769476
  8.3 31.0 %collective-permute-start = (bf16[2,64,512]{1,2,0:T(8,128)(2,1)S(1)}, bf16[2,64,512]{1,2,0:T(8,128)(2,1)S(1)}, u32[]{:S(2)}, u32[]{:S(2)}) collective-permute-start(bf16[2,64,512]{1,2,0:T(8,128)(2,1)S(1)} %copy.99), channel_id=1, source_target_pairs={{0,1},{1,2},{2,3},{3,0},{4,5},{5,6},{6,7},{7,4},{8,9},{9,10},{10,1... | collective-permute-start | bytes 393224 | tf_op jit(solution)/shard_map/ppermute | solution.py:89
  10.5 30.8 %collective-permute-start.1 = (bf16[2,64,512]{1,2,0:T(8,128)(2,1)S(1)}, bf16[2,64,512]{1,2,0:T(8,128)(2,1)}, u32[]{:S(2)}, u32[]{:S(2)}) collective-permute-start(bf16[2,64,512]{1,2,0:T(8,128)(2,1)S(1)} %copy.99), channel_id=1, source_target_pairs={{0,2},{1,3},{2,0},{3,1},{4,6},{5,7},{6,4},{7,5},{8,10},{9,11},{10,... | collective-permute-start | bytes 393224 | tf_op jit(solution)/shard_map/ppermute | solution.py:89
  13.1 28.2 %collective-permute-start.2 = (bf16[2,64,512]{1,2,0:T(8,128)(2,1)S(1)}, bf16[2,64,512]{1,2,0:T(8,128)(2,1)}, u32[]{:S(2)}, u32[]{:S(2)}) collective-permute-start(bf16[2,64,512]{1,2,0:T(8,128)(2,1)S(1)} %copy.99), channel_id=1, source_target_pairs={{0,3},{1,0},{2,1},{3,2},{4,7},{5,4},{6,5},{7,6},{8,11},{9,8},{10,9... | collective-permute-start | bytes 393224 | tf_op jit(solution)/shard_map/ppermute | solution.py:89
  15.7 0.7 copy-start.17
  18.2 0.7 copy-start.15
  19.5 1.3 copy-start.9
  19.6 10.8 %copy-start.11 = (bf16[9,64,512]{2,1,0:T(8,128)(2,1)S(1)}, bf16[9,64,512]{2,1,0:T(8,128)(2,1)}, u32[]{:S(2)}) copy-start(bf16[9,64,512]{2,1,0:T(8,128)(2,1)} %param.12) | copy-start | bytes 1769476
  19.8 11.4 %copy-start.12 = (f32[32,1,512]{2,1,0:T(1,128)}, f32[32,1,512]{2,1,0:T(1,128)S(1)}, u32[]{:S(2)}) copy-start(f32[32,1,512]{2,1,0:T(1,128)S(1)} %copy.87) | copy-start | bytes 196612
  20.7 11.4 %copy-start.1 = (bf16[2,256,512]{2,1,0:T(8,128)(2,1)S(1)}, bf16[2,256,512]{2,1,0:T(8,128)(2,1)}, u32[]{:S(2)}) copy-start(bf16[2,256,512]{2,1,0:T(8,128)(2,1)} %param.9) | copy-start | bytes 1572868
  20.7 29.6 %all-to-all-start = ((f32[32,5,512]{2,1,0:T(8,128)}), f32[32,5,512]{2,1,0:T(8,128)S(1)}, u32[]{:S(2)}, u32[]{:S(2)}) async-start(f32[32,5,512]{2,1,0:T(8,128)} %pad_maximum_fusion.2), calls=%async_computation | async-start | bytes 1048576 | tf_op jit(solution)/shard_map/all_to_all | solution.py:129
  30.3 2.9 %copy-start.2 = (bf16[2,64,512]{2,1,0:T(8,128)(2,1)S(1)}, bf16[2,64,512]{2,1,0:T(8,128)(2,1)}, u32[]{:S(2)}) copy-start(bf16[2,64,512]{2,1,0:T(8,128)(2,1)} %param.13) | copy-start | bytes 393220
  31.2 11.9 %collective-permute-start.3 = (bf16[9,64,128]{2,1,0:T(8,128)(2,1)}, bf16[9,64,128]{2,1,0:T(8,128)(2,1)}, u32[]{:S(2)}, u32[]{:S(2)}) collective-permute-start(bf16[9,64,128]{2,1,0:T(8,128)(2,1)} %get-tuple-element.238), channel_id=1, source_target_pairs={{0,1},{1,2},{2,3},{3,0},{4,5},{5,6},{6,7},{7,4},{8,9},{9,10},{10,1... | collective-permute-start | bytes 442376 | tf_op jit(solution)/shard_map/ppermute | solution.py:90
  31.6 11.5 %collective-permute-start.4 = (bf16[9,64,128]{2,1,0:T(8,128)(2,1)}, bf16[9,64,128]{2,1,0:T(8,128)(2,1)}, u32[]{:S(2)}, u32[]{:S(2)}) collective-permute-start(bf16[9,64,128]{2,1,0:T(8,128)(2,1)} %get-tuple-element.240), channel_id=1, source_target_pairs={{0,2},{1,3},{2,0},{3,1},{4,6},{5,7},{6,4},{7,5},{8,10},{9,11},{10,... | collective-permute-start | bytes 442376 | tf_op jit(solution)/shard_map/ppermute | solution.py:90
  39.3 3.4 %copy-start.14 = (bf16[2,9,64,512]{3,2,0,1:T(8,128)(2,1)}, bf16[2,9,64,512]{3,2,0,1:T(8,128)(2,1)S(1)}, u32[]{:S(2)}) copy-start(bf16[2,9,64,512]{3,2,0,1:T(8,128)(2,1)S(1)} %fusion.62) | copy-start | bytes 3538948
  39.4 6.1 %collective-permute-start.5 = (bf16[9,64,128]{2,1,0:T(8,128)(2,1)}, bf16[9,64,128]{2,1,0:T(8,128)(2,1)S(1)}, u32[]{:S(2)}, u32[]{:S(2)}) collective-permute-start(bf16[9,64,128]{2,1,0:T(8,128)(2,1)} %get-tuple-element.239), channel_id=1, source_target_pairs={{0,3},{1,0},{2,1},{3,2},{4,7},{5,4},{6,5},{7,6},{8,11},{9,8},{10,9... | collective-permute-start | bytes 442376 | tf_op jit(solution)/shard_map/ppermute | solution.py:90
  45.4 1.9 %copy-start.18 = (pred[16,9]{0,1:T(8,128)(4,1)S(1)}, pred[16,9]{0,1:T(8,128)(4,1)}, u32[]{:S(2)}) copy-start(pred[16,9]{0,1:T(8,128)(4,1)} %constant.232) | copy-start | bytes 436
  52.1 0.8 copy-start.13
  52.9 44.2 %copy-start.3 = (f32[2,128,512]{2,1,0:T(8,128)}, f32[2,128,512]{2,1,0:T(8,128)S(1)}, u32[]{:S(2)}) copy-start(f32[2,128,512]{2,1,0:T(8,128)S(1)} %get-tuple-element.139) | copy-start | bytes 1572868
  54.1 25.3 %all-to-all-start.1 = ((f32[32,9,512]{2,1,0:T(8,128)}), f32[32,9,512]{2,1,0:T(8,128)S(1)}, u32[]{:S(2)}, u32[]{:S(2)}) async-start(f32[32,9,512]{2,1,0:T(8,128)} %pad_maximum_fusion), calls=%async_computation.1 | async-start | bytes 2097152 | tf_op jit(solution)/shard_map/all_to_all | solution.py:142
  62.5 40.2 %all-gather.2.cloned.1.call-start = ((), (), s32[]{:S(2)}) async-start(), calls=%async_computation.5 | async-start | bytes 1310720 | tf_op jit(solution)/shard_map/all_gather | solution.py:161
  80.2 2.2 %copy-start.5 = (f32[32,4,512]{2,1,0:T(4,128)}, f32[32,4,512]{2,1,0:T(4,128)S(1)}, u32[]{:S(2)}) copy-start(f32[32,4,512]{2,1,0:T(4,128)S(1)} %get-tuple-element.236) | copy-start | bytes 786436
  83.1 5.0 %copy-start.16 = (pred[2]{0:T(512)(128)(4,1)S(1)}, pred[2]{0:T(512)(128)(4,1)}, u32[]{:S(2)}) copy-start(pred[2]{0:T(512)(128)(4,1)} %constant.174.clone.1) | copy-start | bytes 10
  84.1 12.9 %all-to-all-start.2 = ((f32[32,4,512]{2,1,0:T(4,128)}), f32[32,4,512]{2,1,0:T(4,128)S(1)}, u32[]{:S(2)}, u32[]{:S(2)}) async-start(f32[32,4,512]{2,1,0:T(4,128)} %pad.129), calls=%async_computation.2 | async-start | bytes 524288 | tf_op jit(solution)/shard_map/all_to_all | solution.py:147
  97.1 0.7 copy-start.7
  105.5 4.2 %collective-permute-start.6 = (f32[294912]{0:T(1024)S(1)}, f32[294912]{0:T(1024)S(1)}, u32[]{:S(2)}, u32[]{:S(2)}) collective-permute-start(f32[294912]{0:T(1024)S(1)} %broadcast_select_fusion.2), channel_id=1, source_target_pairs={{0,4},{4,0},{1,5},{5,1},{2,6},{6,2},{3,7},{7,3},{8,12},{12,8},{9,1... | collective-permute-start | bytes 3538952 | tf_op jit(solution)/shard_map/ppermute | solution.py:103
  135.3 22.8 %copy-start.6 = (f32[32,4,512]{2,1,0:T(4,128)S(1)}, f32[32,4,512]{2,1,0:T(4,128)}, u32[]{:S(2)}) copy-start(f32[32,4,512]{2,1,0:T(4,128)} %copy-done.5) | copy-start | bytes 786436
  135.3 23.6 %copy-start.10 = (f32[2,128,512]{2,1,0:T(8,128)S(1)}, f32[2,128,512]{2,1,0:T(8,128)}, u32[]{:S(2)}) copy-start(f32[2,128,512]{2,1,0:T(8,128)} %get-tuple-element.232) | copy-start | bytes 1572868
  135.3 23.6 %copy-start.4 = (f32[2,128,512]{2,1,0:T(8,128)S(1)}, f32[2,128,512]{2,1,0:T(8,128)}, u32[]{:S(2)}) copy-start(f32[2,128,512]{2,1,0:T(8,128)} %copy-done.3) | copy-start | bytes 1572868
  135.3 23.6 %copy-start.8 = (f32[128,512]{1,0:T(8,128)S(1)}, f32[128,512]{1,0:T(8,128)}, u32[]{:S(2)}) copy-start(f32[128,512]{1,0:T(8,128)} %copy-done.7) | copy-start | bytes 786436
  155.1 5.6 %collective-permute-start.7 = (f32[294912]{0:T(1024)S(1)}, f32[294912]{0:T(1024)}, u32[]{:S(2)}, u32[]{:S(2)}) collective-permute-start(f32[294912]{0:T(1024)S(1)} %bitcast.177), channel_id=1, source_target_pairs={{0,4},{4,0},{1,5},{5,1},{2,6},{6,2},{3,7},{7,3},{8,12},{12,8},{9,1... | collective-permute-start | bytes 3538952 | tf_op jit(solution)/shard_map/ppermute | solution.py:107
Sparse Core Ops, SparseCore 0:
  82.5 19.0 all-gather.1

commit v13 on v12

--- a/solution.py
+++ b/solution.py
@@ -86,8 +86,9 @@
     for step in range(1, count):
         pairs = [(source, (source + step) % count) for source in range(count)]
         wanted = lax.dynamic_slice_in_dim(kernel_c, ((me + step) % count) * states_local, states_local, axis=2)
-        cot_blocks.append(lax.ppermute(cotangent, axis, pairs))
-        kernel_blocks.append(lax.ppermute(wanted, axis, pairs))
+        packed = lax.ppermute(jnp.concatenate([cotangent.reshape(-1), wanted.reshape(-1)]), axis, pairs)
+        cot_blocks.append(packed[: cotangent.size].reshape(cotangent.shape))
+        kernel_blocks.append(packed[cotangent.size :].reshape(wanted.shape))
     return jnp.concatenate(cot_blocks, axis=1), jnp.concatenate(kernel_blocks, axis=1)
 
 

time: 175 us -> 183 us (1.046)
  local copies, waits for them, and re-layouts: 17.4 us -> 27.3 us
  other arithmetic: 25.2 us -> 31.2 us
  starting transfers between devices: 35.3 us -> 30.1 us
  waiting for transfers between devices: 26.5 us -> 24.4 us
    slice x0 -> x6, local copies, waits for them, and re-layouts: none -> 5.5 us  [the longest x3 2.76 us: gather_readout(): kernel_blocks.append(packed[cotangent.size:].reshape(wanted.shape))]
    unnamed x18, other arithmetic: 9.22 us -> 14.5 us
    concatenate x0 -> x5, local copies, waits for them, and re-layouts: none -> 3.79 us  [gather_readout(): jnp.concatenate(cot_blocks, axis=1)]
    ppermute x6 -> x3, starting transfers between devices: 8.73 us -> 5.8 us  [gather_readout(): lax.ppermute(jnp.concatenate([cotangent.reshape(-1), wanted.reshape(-1)])...]
    ppermute x6 -> x3, waiting for transfers between devices: 2.26 us -> 0.01 us  [gather_readout(): lax.ppermute(jnp.concatenate([cotangent.reshape(-1), wanted.reshape(-1)])...]
    unnamed x46 -> x52, local copies, waits for them, and re-layouts: 5.87 us -> 6.16 us
  transfers between devices with their start and end apart: 12 -> 9, of which waited for: 4 -> 3; matrix products, arithmetic and copies ran while one was open for 19% -> 26% of each run, Pallas kernels for 0% -> 0%
where the time goes in v13:
time: 183 us; the launch traced here: 182 us
  blocking collectives  43.4 us (24%)
  other arithmetic  31.2 us (17%)
  starting transfers between devices  30.1 us (16%)
  local copies, waits for them, and re-layouts  27.3 us (15%)
  waiting for transfers between devices  24.4 us (13%)
  between operations  14.9 us (8%)
  matrix products  10.6 us (6%)
    all_to_all x1, blocking collectives, pair_then_chip_sum(): pieces = lax.all_to_all(pair_sum, 'chip', 0, 0, tiled=True)  23.6 us
    all_to_all x1, blocking collectives, pair_then_chip_sum(): lax.all_to_all(jnp.broadcast_to(reduced, pieces.shape), 'chip', 0, 0, til...  19.8 us
    unnamed x18, other arithmetic  14.5 us
    all_to_all x1, waiting for transfers between devices, body(): lax.all_to_all(jnp.concatenate([entering_owned, pack_chunks(decay_total,...  13.9 us
    all_to_all x1, starting transfers between devices, body(): lax.all_to_all(pack_chunks(decay_total, local_end, blocks), FRAME_AXES, 0...  9.58 us
    all_to_all x1, waiting for transfers between devices, body(): lax.all_to_all(arriving_owned, FRAME_AXES, 0, 0, tiled=True)  7.81 us
    all_to_all x1, starting transfers between devices, body(): lax.all_to_all(jnp.concatenate([entering_owned, pack_chunks(decay_total,...  7.51 us
    unnamed x52, local copies, waits for them, and re-layouts  6.16 us
  transfers between devices with their start and end apart: 9, of which 3 were waited for; matrix products, arithmetic and copies ran while one was open for 26% of the time, Pallas kernels for 0%

profile of v13, /device:TPU:1, one launch (start us, length us, event | category | flops | bytes accessed | tf_op | source)
XLA Modules:
  0.0 182.0 jit_solution(4595371708384895588)
XLA Ops:
  7.2 1.0 copy.142
  8.3 1.2 constant_dynamic-slice_fusion.4
  9.5 1.0 pad_maximum_fusion.5
  10.5 2.1 %collective-permute-start = (bf16[139264]{0:T(1024)(128)(2,1)}, bf16[139264]{0:T(1024)(128)(2,1)}, u32[]{:S(2)}, u32[]{:S(2)}) collective-permute-start(bf16[139264]{0:T(1024)(128)(2,1)} %get-tuple-element.251), channel_id=1, source_target_pairs={{0,1},{1,2},{2,3},{3,0},{4,5},{5,6},{6,7},{7,4},{8,9},{9,10},{10,1... | collective-permute-start | bytes 835592 | tf_op jit(solution)/shard_map/ppermute | solution.py:89
  12.6 2.6 %collective-permute-start.1 = (bf16[139264]{0:T(1024)(128)(2,1)}, bf16[139264]{0:T(1024)(128)(2,1)}, u32[]{:S(2)}, u32[]{:S(2)}) collective-permute-start(bf16[139264]{0:T(1024)(128)(2,1)} %get-tuple-element.252), channel_id=1, source_target_pairs={{0,2},{1,3},{2,0},{3,1},{4,6},{5,7},{6,4},{7,5},{8,10},{9,11},{10,... | collective-permute-start | bytes 835592 | tf_op jit(solution)/shard_map/ppermute | solution.py:89
  15.2 1.1 collective-permute-start.2
  17.5 1.5 convolution_select_fusion.1
  20.8 0.9 pad_maximum_fusion.2
  21.8 9.6 %all-to-all-start = ((f32[32,5,512]{2,1,0:T(8,128)}), f32[32,5,512]{2,1,0:T(8,128)S(1)}, u32[]{:S(2)}, u32[]{:S(2)}) async-start(f32[32,5,512]{2,1,0:T(8,128)} %pad_maximum_fusion.2), calls=%async_computation | async-start | bytes 1048576 | tf_op jit(solution)/shard_map/all_to_all | solution.py:130
  31.4 1.1 fusion.14
  33.2 1.1 fusion.17
  34.4 1.1 fusion.20
  35.5 1.1 fusion.23
  36.6 0.9 bitcast_dynamic-update-slice_fusion.2
  43.0 1.1 fusion.26
  44.0 0.9 slice.261
  45.8 0.9 slice.262
  46.7 0.9 concatenate.41
  47.5 0.9 slice.263
  48.4 0.8 concatenate.43
  49.3 1.4 maximum_bitcast_fusion
  50.7 1.6 copy.141
  52.3 1.1 pad.133.clone
  53.4 0.9 fusion.7
  54.3 0.9 slice.265
  55.2 0.9 slice.266
  56.1 0.9 slice.267
  57.1 0.9 rev.9
  58.0 2.8 %convolution_select_fusion = f32[8,16,9,128]{3,1,2,0:T(8,128)S(1)} fusion(bf16[3,3,128,256]{2,3,1,0:T(8,128)(2,1)} %bitcast.203, bf16[256,8,2,8,11]{0,1,4,3,2:T(8,128)(2,1)} %fusion.7, pred[16,9]{0,1:T(8,128)(4,1)S(1)} %copy-done.21), kind=kOutput, calls=%fused_computation.16 | convolution fusion | flops 623001600 | bytes 1900688 | tf_op jit(solution)/shard_map/conv_general_dilated | solution.py:74
  63.9 1.1 pad_maximum_fusion
  65.1 7.5 %all-to-all-start.1 = ((f32[32,9,512]{2,1,0:T(8,128)}), f32[32,9,512]{2,1,0:T(8,128)S(1)}, u32[]{:S(2)}, u32[]{:S(2)}) async-start(f32[32,9,512]{2,1,0:T(8,128)} %pad_maximum_fusion), calls=%async_computation.1 | async-start | bytes 2097152 | tf_op jit(solution)/shard_map/all_to_all | solution.py:143
  73.5 1.1 fusion.29
  74.6 1.0 fusion.32
  75.6 13.9 %all-to-all-done.1 = f32[32,9,512]{2,1,0:T(8,128)S(1)} async-done(((f32[32,9,512]{2,1,0:T(8,128)}), f32[32,9,512]{2,1,0:T(8,128)S(1)}, u32[]{:S(2)}, u32[]{:S(2)}) %all-to-all-start.1) | async-done | bytes 589856 | tf_op jit(solution)/shard_map/all_to_all | solution.py:143
  90.4 2.0 %fusion.74 = (bf16[2,128,512]{2,1,0:T(8,128)(2,1)}, f32[2,128,512]{2,1,0:T(8,128)}) fusion(f32[2,128,512]{2,1,0:T(8,128)} %copy-done.9, f32[128,512]{1,0:T(8,128)S(1)} %mul.257, f32[2,128]{1,0:T(2,128)S(1)} %reduce_window.16), kind=kLoop, calls=%fused_computation.151 | loop fusion | flops 393216 | bytes 1573888 | tf_op jit(solution)/shard_map/convert_element_type | solution.py:152
  94.2 3.9 %all-to-all-start.2 = ((f32[32,4,512]{2,1,0:T(4,128)}), f32[32,4,512]{2,1,0:T(4,128)S(1)}, u32[]{:S(2)}, u32[]{:S(2)}) async-start(f32[32,4,512]{2,1,0:T(4,128)} %pad.129), calls=%async_computation.2 | async-start | bytes 524288 | tf_op jit(solution)/shard_map/all_to_all | solution.py:148
  98.2 1.1 fusion.35
  99.3 7.8 %all-to-all-done.2 = f32[32,4,512]{2,1,0:T(4,128)S(1)} async-done(((f32[32,4,512]{2,1,0:T(4,128)}), f32[32,4,512]{2,1,0:T(4,128)S(1)}, u32[]{:S(2)}, u32[]{:S(2)}) %all-to-all-start.2) | async-done | bytes 262176 | tf_op jit(solution)/shard_map/all_to_all | solution.py:148
  107.9 3.8 %convolution_bitcast_fusion = f32[9,128,256]{1,2,0:T(8,128)S(1)} fusion(bf16[2,9,256,512]{3,2,0,1:T(8,128)(2,1)} %fusion.35, f32[2,128,512]{2,1,0:T(8,128)S(1)} %get-tuple-element.139, f32[128,512]{1,0:T(8,128)S(1)} %mul.253, f32[2,128]{1,0:T(2,128)S(1)} %broadcast_select_fusion.3), kind=kOutput, calls=%fused_computation.15 | convolution fusion | flops 604372992 | bytes 6685696 | tf_op jit(solution)/shard_map/fps,fkcs->kpc/dot_general | solution.py:159
  112.7 2.4 %fusion.4 = f32[9,64,512,1]{2,1,3,0:T(8,128)S(1)} fusion(bf16[2,9,64,512]{3,2,0,1:T(8,128)(2,1)} %fusion.65, bf16[2,512,512]{2,1,0:T(8,128)(2,1)} %all-gather.2.cloned.1.call-done), kind=kOutput, calls=%fused_computation.29 | convolution fusion | flops 603979776 | bytes 3407872 | tf_op jit(solution)/shard_map/fkus,fps->kup/dot_general | solution.py:163
  115.9 2.6 %collective-permute-done.3 = f32[294912]{0:T(1024)S(1)} collective-permute-done((f32[294912]{0:T(1024)S(1)}, f32[294912]{0:T(1024)S(1)}, u32[]{:S(2)}, u32[]{:S(2)}) %collective-permute-start.3) | collective-permute-done | bytes 1179680 | tf_op jit(solution)/shard_map/ppermute | solution.py:104
  118.7 23.6 %all_to_all.31 = f32[16,1,18432]{2,1,0:T(1,128)S(1)} all-to-all(f32[16,1,18432]{2,1,0:T(1,128)S(1)} %bitcast.187), channel_id=1, replica_groups=mesh['chip'=16,'core'=2,'chan'=4] {'chip'}, dimensions={0} | all-to-all | bytes 2359296 | tf_op jit(solution)/shard_map/all_to_all | solution.py:105
  143.6 19.8 %all_to_all.30 = f32[16,1,18432]{2,1,0:T(1,128)S(1)} all-to-all(f32[16,1,18432]{2,1,0:T(1,128)S(1)} %broadcast_in_dim.121), channel_id=1, replica_groups=mesh['chip'=16,'core'=2,'chan'=4] {'chip'}, dimensions={0} | all-to-all | bytes 2359296 | tf_op jit(solution)/shard_map/all_to_all | solution.py:107
  163.5 3.0 %collective-permute-start.4 = (f32[294912]{0:T(1024)S(1)}, f32[294912]{0:T(1024)}, u32[]{:S(2)}, u32[]{:S(2)}) collective-permute-start(f32[294912]{0:T(1024)S(1)} %bitcast.185), channel_id=1, source_target_pairs={{0,4},{4,0},{1,5},{5,1},{2,6},{6,2},{3,7},{7,3},{8,12},{12,8},{9,1... | collective-permute-start | bytes 3538952 | tf_op jit(solution)/shard_map/ppermute | solution.py:108
  167.3 1.7 fusion.36
  169.0 2.4 %broadcast_select_fusion = (f32[294912]{0:T(1024)S(1)}, f32[294912]{0:T(1024)}) fusion(f32[294912]{0:T(1024)} %collective-permute-done.4, f32[294912]{0:T(1024)S(1)} %bitcast.186, pred[]{:T(512)S(6)} %eq.29), kind=kLoop, calls=%fused_computation.38 | loop fusion | flops 589824 | bytes 4718593 | tf_op jit(solution)/shard_map/jit(_where)/select_n | solution.py:110
  171.5 2.5 %reshape.138 = f32[9,128,256]{2,1,0:T(8,128)} reshape(f32[294912]{0:T(1024)} %get-tuple-element.244) | data formatting | bytes 2359296 | tf_op jit(solution)/shard_map/reshape | solution.py:111
  174.0 1.2 reshape.139
  (175 shorter events, 22.5 us)
Async XLA Ops:
  7.2 9.8 %copy-start = (bf16[9,128,256]{2,1,0:T(8,128)(2,1)S(1)}, bf16[9,128,256]{2,1,0:T(8,128)(2,1)}, u32[]{:S(2)}) copy-start(bf16[9,128,256]{2,1,0:T(8,128)(2,1)} %param.11) | copy-start | bytes 1769476
  8.3 8.0 %copy-start.1 = (bf16[2,256,512]{2,1,0:T(8,128)(2,1)S(1)}, bf16[2,256,512]{2,1,0:T(8,128)(2,1)}, u32[]{:S(2)}) copy-start(bf16[2,256,512]{2,1,0:T(8,128)(2,1)} %param.9) | copy-start | bytes 1572868
  10.5 33.5 %collective-permute-start = (bf16[139264]{0:T(1024)(128)(2,1)}, bf16[139264]{0:T(1024)(128)(2,1)}, u32[]{:S(2)}, u32[]{:S(2)}) collective-permute-start(bf16[139264]{0:T(1024)(128)(2,1)} %get-tuple-element.251), channel_id=1, source_target_pairs={{0,1},{1,2},{2,3},{3,0},{4,5},{5,6},{6,7},{7,4},{8,9},{9,10},{10,1... | collective-permute-start | bytes 835592 | tf_op jit(solution)/shard_map/ppermute | solution.py:89
  12.6 33.2 %collective-permute-start.1 = (bf16[139264]{0:T(1024)(128)(2,1)}, bf16[139264]{0:T(1024)(128)(2,1)}, u32[]{:S(2)}, u32[]{:S(2)}) collective-permute-start(bf16[139264]{0:T(1024)(128)(2,1)} %get-tuple-element.252), channel_id=1, source_target_pairs={{0,2},{1,3},{2,0},{3,1},{4,6},{5,7},{6,4},{7,5},{8,10},{9,11},{10,... | collective-permute-start | bytes 835592 | tf_op jit(solution)/shard_map/ppermute | solution.py:89
  15.2 32.3 %collective-permute-start.2 = (bf16[139264]{0:T(1024)(128)(2,1)}, bf16[139264]{0:T(1024)(128)(2,1)}, u32[]{:S(2)}, u32[]{:S(2)}) collective-permute-start(bf16[139264]{0:T(1024)(128)(2,1)} %get-tuple-element.253), channel_id=1, source_target_pairs={{0,3},{1,0},{2,1},{3,2},{4,7},{5,4},{6,5},{7,6},{8,11},{9,8},{10,9... | collective-permute-start | bytes 835592 | tf_op jit(solution)/shard_map/ppermute | solution.py:89
  16.8 0.7 copy-start.20
  19.2 0.7 copy-start.17
  20.5 1.2 copy-start.9
  21.7 10.7 %copy-start.2 = (bf16[2,64,512]{2,1,0:T(8,128)(2,1)S(1)}, bf16[2,64,512]{2,1,0:T(8,128)(2,1)}, u32[]{:S(2)}) copy-start(bf16[2,64,512]{2,1,0:T(8,128)(2,1)} %param.13) | copy-start | bytes 393220
  21.8 39.4 %all-to-all-start = ((f32[32,5,512]{2,1,0:T(8,128)}), f32[32,5,512]{2,1,0:T(8,128)S(1)}, u32[]{:S(2)}, u32[]{:S(2)}) async-start(f32[32,5,512]{2,1,0:T(8,128)} %pad_maximum_fusion.2), calls=%async_computation | async-start | bytes 1048576 | tf_op jit(solution)/shard_map/all_to_all | solution.py:130
  31.3 9.1 %copy-start.15 = (pred[512]{0:T(512)(128)(4,1)}, pred[512]{0:T(512)(128)(4,1)S(1)}, u32[]{:S(2)}) copy-start(pred[512]{0:T(512)(128)(4,1)S(1)} %compare_and_fusion.1) | copy-start | bytes 1540
  31.4 10.6 %copy-start.13 = (pred[512]{0:T(512)(128)(4,1)}, pred[512]{0:T(512)(128)(4,1)S(1)}, u32[]{:S(2)}) copy-start(pred[512]{0:T(512)(128)(4,1)S(1)} %fusion.72) | copy-start | bytes 1540
  31.4 11.5 %copy-start.11 = (pred[512]{0:T(512)(128)(4,1)}, pred[512]{0:T(512)(128)(4,1)S(1)}, u32[]{:S(2)}) copy-start(pred[512]{0:T(512)(128)(4,1)S(1)} %compare_and_fusion) | copy-start | bytes 1540
  57.1 0.9 copy-start.21
  62.5 0.7 copy-start.18
  63.8 43.4 %copy-start.3 = (f32[2,128,512]{2,1,0:T(8,128)}, f32[2,128,512]{2,1,0:T(8,128)S(1)}, u32[]{:S(2)}) copy-start(f32[2,128,512]{2,1,0:T(8,128)S(1)} %get-tuple-element.139) | copy-start | bytes 1572868
  65.1 7.6 %copy-start.16 = (pred[512]{0:T(512)(128)(4,1)S(1)}, pred[512]{0:T(512)(128)(4,1)}, u32[]{:S(2)}) copy-start(pred[512]{0:T(512)(128)(4,1)} %copy-done.15) | copy-start | bytes 1540
  65.1 24.4 %all-to-all-start.1 = ((f32[32,9,512]{2,1,0:T(8,128)}), f32[32,9,512]{2,1,0:T(8,128)S(1)}, u32[]{:S(2)}, u32[]{:S(2)}) async-start(f32[32,9,512]{2,1,0:T(8,128)} %pad_maximum_fusion), calls=%async_computation.1 | async-start | bytes 2097152 | tf_op jit(solution)/shard_map/all_to_all | solution.py:143
  72.6 2.0 %copy-start.14 = (pred[512]{0:T(512)(128)(4,1)S(1)}, pred[512]{0:T(512)(128)(4,1)}, u32[]{:S(2)}) copy-start(pred[512]{0:T(512)(128)(4,1)} %copy-done.13) | copy-start | bytes 1540
  72.6 40.1 %all-gather.2.cloned.1.call-start = ((), (), s32[]{:S(2)}) async-start(), calls=%async_computation.5 | async-start | bytes 1310720 | tf_op jit(solution)/shard_map/all_gather | solution.py:162
  90.3 2.2 %copy-start.5 = (f32[32,4,512]{2,1,0:T(4,128)}, f32[32,4,512]{2,1,0:T(4,128)S(1)}, u32[]{:S(2)}) copy-start(f32[32,4,512]{2,1,0:T(4,128)S(1)} %get-tuple-element.246) | copy-start | bytes 786436
  93.1 5.0 %copy-start.19 = (pred[2]{0:T(512)(128)(4,1)S(1)}, pred[2]{0:T(512)(128)(4,1)}, u32[]{:S(2)}) copy-start(pred[2]{0:T(512)(128)(4,1)} %constant.174.clone.1) | copy-start | bytes 10
  93.2 5.0 %copy-start.12 = (pred[512]{0:T(512)(128)(4,1)S(1)}, pred[512]{0:T(512)(128)(4,1)}, u32[]{:S(2)}) copy-start(pred[512]{0:T(512)(128)(4,1)} %copy-done.11) | copy-start | bytes 1540
  94.2 12.9 %all-to-all-start.2 = ((f32[32,4,512]{2,1,0:T(4,128)}), f32[32,4,512]{2,1,0:T(4,128)S(1)}, u32[]{:S(2)}, u32[]{:S(2)}) async-start(f32[32,4,512]{2,1,0:T(4,128)} %pad.129), calls=%async_computation.2 | async-start | bytes 524288 | tf_op jit(solution)/shard_map/all_to_all | solution.py:148
  107.2 0.7 copy-start.7
  115.6 2.9 %collective-permute-start.3 = (f32[294912]{0:T(1024)S(1)}, f32[294912]{0:T(1024)S(1)}, u32[]{:S(2)}, u32[]{:S(2)}) collective-permute-start(f32[294912]{0:T(1024)S(1)} %broadcast_select_fusion.2), channel_id=1, source_target_pairs={{0,4},{4,0},{1,5},{5,1},{2,6},{6,2},{3,7},{7,3},{8,12},{12,8},{9,1... | collective-permute-start | bytes 3538952 | tf_op jit(solution)/shard_map/ppermute | solution.py:104
  143.6 22.8 %copy-start.6 = (f32[32,4,512]{2,1,0:T(4,128)S(1)}, f32[32,4,512]{2,1,0:T(4,128)}, u32[]{:S(2)}) copy-start(f32[32,4,512]{2,1,0:T(4,128)} %copy-done.5) | copy-start | bytes 786436
  143.6 23.6 %copy-start.10 = (f32[2,128,512]{2,1,0:T(8,128)S(1)}, f32[2,128,512]{2,1,0:T(8,128)}, u32[]{:S(2)}) copy-start(f32[2,128,512]{2,1,0:T(8,128)} %get-tuple-element.242) | copy-start | bytes 1572868
  143.6 23.6 %copy-start.4 = (f32[2,128,512]{2,1,0:T(8,128)S(1)}, f32[2,128,512]{2,1,0:T(8,128)}, u32[]{:S(2)}) copy-start(f32[2,128,512]{2,1,0:T(8,128)} %copy-done.3) | copy-start | bytes 1572868
  143.6 23.6 %copy-start.8 = (f32[128,512]{1,0:T(8,128)S(1)}, f32[128,512]{1,0:T(8,128)}, u32[]{:S(2)}) copy-start(f32[128,512]{1,0:T(8,128)} %copy-done.7) | copy-start | bytes 786436
  163.5 5.6 %collective-permute-start.4 = (f32[294912]{0:T(1024)S(1)}, f32[294912]{0:T(1024)}, u32[]{:S(2)}, u32[]{:S(2)}) collective-permute-start(f32[294912]{0:T(1024)S(1)} %bitcast.185), channel_id=1, source_target_pairs={{0,4},{4,0},{1,5},{5,1},{2,6},{6,2},{3,7},{7,3},{8,12},{12,8},{9,1... | collective-permute-start | bytes 3538952 | tf_op jit(solution)/shard_map/ppermute | solution.py:108
Sparse Core Ops, SparseCore 0:
  92.6 17.2 all-gather.1
